TPU v7x, 512 devices: a whole 4x8x8 slice. The times are simulated.
512 devices in a mesh: frame: 8 (over y), space: 32 (over z, x), dp: 2 (over core).
Axes of the slice: x: 4, y: 8, z: 8, core: 2. Of those that a mesh axis runs over, the one named last changes fastest.
Arguments:
- frames_in: bfloat16 [16, 4096, 768], P(('dp', 'frame'), 'space'), parts along dimension 0, may hold values from -6 to 6
- cotangent: bfloat16 [16, 4096, 768], P(('dp', 'frame'), 'space'), parts along dimension 0, may hold values from -6 to 6
- w_qkv_space: bfloat16 [768, 2304], P('space'), may hold values from -0.21875 to 0.21875
- w_out_space: bfloat16 [768, 768], P('space'), may hold values from -0.875 to 0.875
- w_qkv_time: bfloat16 [768, 2304], P('space'), may hold values from -0.21875 to 0.21875
- w_out_time: bfloat16 [768, 768], P('space'), may hold values from -0.21875 to 0.21875
- neighbours: int32 [32, 4], replicated, may hold values from 0 to 31, as said below
Outputs:
- frames_out: bfloat16 [16, 4096, 768], P(('dp', 'frame'), 'space'), parts along dimension 0
- grad_frames: bfloat16 [16, 4096, 768], P(('dp', 'frame'), 'space'), parts along dimension 0
There are 2 independent parts, one for each index of `dp`. A program takes and returns all parts, laid end to end along the dimension named above; an argument that names none is the same for every part. Nothing has to cross between parts.
Inputs may be any that keep to these rules, and one draw needn't show every extreme that they name: `neighbours`: row b lists block b first; every entry c satisfies |c - b| <= 1; entries may repeat, and a repeated entry counts once.
All inputs are finite; a program needn't handle non-finite values.
Results may differ from a plain program's by a relative error of at most 0.023.
Values may be sent and summed in bfloat16 or wider, within the bound.
No kernel may reach another device: no remote copies, remote signals or barrier semaphores. Data moves between devices by JAX's collectives and lax.ppermute only.
A program may use at most 64 MiB of HBM per device.

v0:
```python
import jax
import jax.numpy as jnp
from jax import lax
from jax.sharding import PartitionSpec as P

HEADS = 12
HD = 64
BLOCK = 128


EPS = 1e-06


def padded(cells, sides, width):
    for axis, dim in sides:
        count = lax.axis_size(axis)
        ends = count - 1
        head = lax.slice_in_dim(cells, 0, width, axis=dim)
        tail = lax.slice_in_dim(cells, cells.shape[dim] - width, cells.shape[dim], axis=dim)
        cells = jnp.concatenate(
            [
                lax.ppermute(tail, axis, [(i, (i + 1) % count) for i in range(ends)]),
                cells,
                lax.ppermute(head, axis, [((i + 1) % count, i) for i in range(ends)]),
            ],
            axis=dim,
        )
    return cells


def rms_norm(row_data):
    values = row_data.astype(jnp.float32)
    factor = lax.rsqrt(jnp.mean(values * values, axis=-1, keepdims=True) + EPS)
    return (values * factor).astype(jnp.bfloat16)


def rms_back(row_data, upstream):
    values = row_data.astype(jnp.float32)
    factor = lax.rsqrt(jnp.mean(values * values, axis=-1, keepdims=True) + EPS)
    inner_mean = jnp.mean(values * upstream, axis=-1, keepdims=True)
    return factor * upstream - values * factor**3 * inner_mean


def block_mask(neighbour_rows, first_id):
    block_count = neighbour_rows.shape[0]
    candidate = first_id + jnp.arange(3 * block_count, dtype=jnp.int32)
    matches = jnp.any(neighbour_rows[:, :, None] == candidate[None, None, :], axis=1)
    return jnp.repeat(jnp.repeat(matches, BLOCK, axis=0), BLOCK, axis=1)


def space_attend(queries, key_rows, value_rows, allowed):
    score_scale = HD ** (-0.5)
    query_count = queries.shape[0]
    key_count = key_rows.shape[0]
    output_list = []
    total_list = []
    for head_pair in range(HEADS // 2):
        start_col = head_pair * 2 * HD
        stop_col = start_col + 2 * HD
        query_part = queries[:, start_col:stop_col].reshape(query_count, 2, HD)
        key_part = key_rows[:, start_col:stop_col].reshape(key_count, 2, HD)
        value_part = value_rows[:, start_col:stop_col].reshape(key_count, 2, HD)
        scores = (
            jnp.einsum("sgh,tgh->gst", query_part, key_part, preferred_element_type=jnp.float32)
            * score_scale
        )
        exponent = jnp.where(allowed[None], jnp.exp(scores), 0.0)
        totals = jnp.sum(exponent, axis=-1)
        probability = (exponent / totals[:, :, None]).astype(jnp.bfloat16)
        combined = jnp.einsum(
            "gst,tgh->sgh", probability, value_part, preferred_element_type=jnp.float32
        )
        output_list.append(combined.astype(jnp.bfloat16).reshape(query_count, 2 * HD))
        total_list.append(totals)
    return (jnp.concatenate(output_list, axis=1), jnp.concatenate(total_list, axis=0))


def space_back(queries, key_rows, value_rows, allowed, totals, attended, grad_attended):
    score_scale = HD ** (-0.5)
    query_count = queries.shape[0]
    key_count = key_rows.shape[0]
    query_list = []
    key_list = []
    value_list = []
    for head_pair in range(HEADS // 2):
        start_col = head_pair * 2 * HD
        stop_col = start_col + 2 * HD
        query_part = queries[:, start_col:stop_col].reshape(query_count, 2, HD)
        key_part = key_rows[:, start_col:stop_col].reshape(key_count, 2, HD)
        value_part = value_rows[:, start_col:stop_col].reshape(key_count, 2, HD)
        out_part = attended[:, start_col:stop_col].reshape(query_count, 2, HD)
        grad_part = grad_attended[:, start_col:stop_col].reshape(query_count, 2, HD)
        scores = (
            jnp.einsum("sgh,tgh->gst", query_part, key_part, preferred_element_type=jnp.float32)
            * score_scale
        )
        exponent = jnp.where(allowed[None], jnp.exp(scores), 0.0)
        weight = exponent / totals[2 * head_pair : 2 * head_pair + 2, :, None]
        probability = weight.astype(jnp.bfloat16)
        prob_grad = jnp.einsum(
            "sgh,tgh->gst", grad_part, value_part, preferred_element_type=jnp.float32
        )
        row_delta = jnp.einsum(
            "sgh,sgh->gs", grad_part, out_part, preferred_element_type=jnp.float32
        )
        score_grad = (weight * (prob_grad - row_delta[:, :, None])).astype(jnp.bfloat16)
        query_grad = (
            jnp.einsum("gst,tgh->sgh", score_grad, key_part, preferred_element_type=jnp.float32)
            * score_scale
        )
        key_grad = (
            jnp.einsum("gst,sgh->tgh", score_grad, query_part, preferred_element_type=jnp.float32)
            * score_scale
        )
        value_grad = jnp.einsum(
            "gst,sgh->tgh", probability, grad_part, preferred_element_type=jnp.float32
        )
        query_list.append(query_grad.astype(jnp.bfloat16).reshape(query_count, 2 * HD))
        key_list.append(key_grad.reshape(key_count, 2 * HD))
        value_list.append(value_grad.reshape(key_count, 2 * HD))
    return (
        jnp.concatenate(query_list, axis=1),
        jnp.concatenate(key_list, axis=1),
        jnp.concatenate(value_list, axis=1),
    )


def time_attend(queries, key_rows, value_rows):
    frame_count, position_count, feature_count = queries.shape
    split_shape = (frame_count, position_count, HEADS, HD)
    score_scale = HD ** (-0.5)
    scores = (
        jnp.einsum(
            "fphd,gphd->phfg",
            queries.reshape(split_shape),
            key_rows.reshape(split_shape),
            preferred_element_type=jnp.float32,
        )
        * score_scale
    )
    causal = jnp.arange(frame_count)[:, None] >= jnp.arange(frame_count)[None, :]
    exponent = jnp.where(causal, jnp.exp(scores), 0.0)
    totals = jnp.sum(exponent, axis=-1)
    probability = (exponent / totals[..., None]).astype(jnp.bfloat16)
    combined = jnp.einsum(
        "phfg,gphd->fphd",
        probability,
        value_rows.reshape(split_shape),
        preferred_element_type=jnp.float32,
    )
    return (
        combined.astype(jnp.bfloat16).reshape(frame_count, position_count, feature_count),
        totals,
    )


def time_back(queries, key_rows, value_rows, attended, grad_attended, totals):
    frame_count, position_count, feature_count = queries.shape
    split_shape = (frame_count, position_count, HEADS, HD)
    score_scale = HD ** (-0.5)
    query_four = queries.reshape(split_shape)
    key_four = key_rows.reshape(split_shape)
    value_four = value_rows.reshape(split_shape)
    out_four = attended.reshape(split_shape)
    grad_four = grad_attended.reshape(split_shape)
    scores = (
        jnp.einsum("fphd,gphd->phfg", query_four, key_four, preferred_element_type=jnp.float32)
        * score_scale
    )
    causal = jnp.arange(frame_count)[:, None] >= jnp.arange(frame_count)[None, :]
    exponent = jnp.where(causal, jnp.exp(scores), 0.0)
    weight = exponent / totals[..., None]
    probability = weight.astype(jnp.bfloat16)
    prob_grad = jnp.einsum(
        "fphd,gphd->phfg", grad_four, value_four, preferred_element_type=jnp.float32
    )
    row_delta = jnp.einsum(
        "fphd,fphd->phf", grad_four, out_four, preferred_element_type=jnp.float32
    )
    score_grad = (weight * (prob_grad - row_delta[..., None])).astype(jnp.bfloat16)
    query_grad = (
        jnp.einsum("phfg,gphd->fphd", score_grad, key_four, preferred_element_type=jnp.float32)
        * score_scale
    )
    key_grad = (
        jnp.einsum("phfg,fphd->gphd", score_grad, query_four, preferred_element_type=jnp.float32)
        * score_scale
    )
    value_grad = jnp.einsum(
        "phfg,fphd->gphd", probability, grad_four, preferred_element_type=jnp.float32
    )
    pieces = [
        gradient.astype(jnp.bfloat16).reshape(frame_count, position_count, feature_count)
        for gradient in (query_grad, key_grad, value_grad)
    ]
    return jnp.concatenate(pieces, axis=-1)


def to_frames(local_rows):
    return lax.all_to_all(local_rows[None], "frame", split_axis=1, concat_axis=0, tiled=True)


def to_space(frame_rows):
    return lax.all_to_all(frame_rows, "frame", split_axis=0, concat_axis=1, tiled=True)[0]


def rim(first_part, second_part, width):
    return (padded(first_part, (("space", 0),), width), padded(second_part, (("space", 0),), width))


def local(frames_in, cotangent, w_qkv_space, w_out_space, w_qkv_time, w_out_time, neighbours):
    local_in = frames_in[0]
    grad_out = cotangent[0]
    shard, feature_count = local_in.shape
    full_qkv_space, full_out_space, full_qkv_time, full_out_time = (
        lax.all_gather(w_qkv_space, "space", axis=0, tiled=True),
        lax.all_gather(w_out_space, "space", axis=0, tiled=True),
        lax.all_gather(w_qkv_time, "space", axis=0, tiled=True),
        lax.all_gather(w_out_time, "space", axis=0, tiled=True),
    )
    block_count = shard // BLOCK
    space_index = lax.axis_index("space")
    lists_here = lax.dynamic_slice_in_dim(neighbours, space_index * block_count, block_count, 0)
    allowed = block_mask(lists_here, (space_index - 1) * block_count)
    normed_space = rms_norm(local_in)
    projected = jnp.dot(normed_space, full_qkv_space, preferred_element_type=jnp.float32).astype(
        jnp.bfloat16
    )
    queries = projected[:, :feature_count]
    key_window, value_window = rim(
        projected[:, feature_count : 2 * feature_count], projected[:, 2 * feature_count :], shard
    )
    attended, totals = space_attend(queries, key_window, value_window, allowed)
    update = jnp.dot(attended, full_out_space, preferred_element_type=jnp.float32)
    stream = (local_in.astype(jnp.float32) + update).astype(jnp.bfloat16)
    normed_time = rms_norm(stream)
    projected_time = jnp.dot(normed_time, full_qkv_time, preferred_element_type=jnp.float32).astype(
        jnp.bfloat16
    )
    time_rows = to_frames(projected_time)
    query_time = time_rows[..., :feature_count]
    key_time = time_rows[..., feature_count : 2 * feature_count]
    value_time = time_rows[..., 2 * feature_count :]
    attended_time, totals_time = time_attend(query_time, key_time, value_time)
    attended_back = to_space(attended_time)
    update_time = jnp.dot(attended_back, full_out_time, preferred_element_type=jnp.float32)
    frames_out = (stream.astype(jnp.float32) + update_time).astype(jnp.bfloat16)
    grad_att_time = jnp.dot(grad_out, full_out_time.T, preferred_element_type=jnp.float32).astype(
        jnp.bfloat16
    )
    grad_time_rows = to_frames(grad_att_time)
    gradients = time_back(
        query_time, key_time, value_time, attended_time, grad_time_rows, totals_time
    )
    grad_project_time = to_space(gradients)
    grad_normed_time = jnp.dot(
        grad_project_time, full_qkv_time.T, preferred_element_type=jnp.float32
    )
    grad_stream = (grad_out.astype(jnp.float32) + rms_back(stream, grad_normed_time)).astype(
        jnp.bfloat16
    )
    grad_attended = jnp.dot(
        grad_stream, full_out_space.T, preferred_element_type=jnp.float32
    ).astype(jnp.bfloat16)
    grad_query, key_partial, value_partial = space_back(
        queries, key_window, value_window, allowed, totals, attended, grad_attended
    )
    key_send = jnp.concatenate([key_partial[:shard], key_partial[2 * shard :]], axis=0).astype(
        jnp.bfloat16
    )
    value_send = jnp.concatenate(
        [value_partial[:shard], value_partial[2 * shard :]], axis=0
    ).astype(jnp.bfloat16)
    key_got, value_got = rim(key_send, value_send, shard)
    grad_key = (
        key_partial[shard : 2 * shard]
        + key_got[:shard].astype(jnp.float32)
        + key_got[3 * shard :].astype(jnp.float32)
    ).astype(jnp.bfloat16)
    grad_value = (
        value_partial[shard : 2 * shard]
        + value_got[:shard].astype(jnp.float32)
        + value_got[3 * shard :].astype(jnp.float32)
    ).astype(jnp.bfloat16)
    grad_project = jnp.concatenate([grad_query, grad_key, grad_value], axis=1)
    grad_normed = jnp.dot(grad_project, full_qkv_space.T, preferred_element_type=jnp.float32)
    grad_in = (grad_stream.astype(jnp.float32) + rms_back(local_in, grad_normed)).astype(
        jnp.bfloat16
    )
    return (frames_out[None], grad_in[None])


def solution(mesh):
    in_specs = (
        P(("dp", "frame"), "space", None),
        P(("dp", "frame"), "space", None),
        P("space", None),
        P("space", None),
        P("space", None),
        P("space", None),
        P(),
    )
    out_specs = (P(("dp", "frame"), "space", None), P(("dp", "frame"), "space", None))
    return jax.shard_map(local, mesh=mesh, in_specs=in_specs, out_specs=out_specs, check_vma=False)
```

profile of v0, /device:TPU:6, one launch (start us, length us, event | category | flops | bytes accessed | tf_op | source)
XLA Modules:
  0.0 480.3 jit_solution(3111090518492652607)
XLA Ops:
  7.2 0.7 all-gather.11.cloned.1.call-update
  8.0 0.7 all-gather.5.cloned.1.call-update
  8.7 0.7 all-gather.7.cloned.1.call-update
  10.3 1.0 fusion.45
  11.4 0.6 multiply_multiply_fusion
  12.0 85.6 %all-gather.11.cloned.1.call-done = bf16[768,768]{1,0:T(8,128)(2,1)} async-done(((bf16[24,768]{1,0:T(8,128)(2,1)}), bf16[768,768]{1,0:T(8,128)(2,1)}) %all-gather.11.cloned.1.call-update) | async-done | bytes 1179664 | tf_op jit(solution)/shard_map/all_gather | solution.py:219
  97.5 1.9 fusion.37
  100.3 1.8 reduce.19
  102.2 0.7 reshape.405
  102.9 6.7 %all-to-all-start.2 = ((bf16[8,2,6144]{2,1,0:T(2,128)(2,1)}), bf16[8,2,6144]{2,1,0:T(2,128)(2,1)S(1)}, u32[]{:S(2)}, u32[]{:S(2)}) async-start(bf16[8,2,6144]{2,1,0:T(2,128)(2,1)} %reshape.405), calls=%async_computation.2 | async-start | bytes 393216 | tf_op jit(solution)/shard_map/all_to_all | solution.py:200
  109.6 74.6 %all-gather.5.cloned.1.call-done = bf16[768,2304]{1,0:T(8,128)(2,1)} async-done(((bf16[24,2304]{1,0:T(8,128)(2,1)}), bf16[768,2304]{1,0:T(8,128)(2,1)}) %all-gather.5.cloned.1.call-update) | async-done | bytes 3538960 | tf_op jit(solution)/shard_map/all_gather | solution.py:216
  184.2 2.7 convolution_convert_fusion.1
  186.9 2.9 collective-permute-start.1
  189.8 5.1 %collective-permute-start = (bf16[128,768]{1,0:T(8,128)(2,1)S(1)}, bf16[128,768]{1,0:T(8,128)(2,1)S(1)}, u32[]{:S(2)}, u32[]{:S(2)}) collective-permute-start(bf16[128,768]{1,0:T(8,128)(2,1)S(1)} %get-tuple-element.28), channel_id=1, source_target_pairs={{0,2},{2,4},{4,6},{6,8},{8,10},{10,12},{12,14},{14,16},{16,18},{18... | collective-permute-start | bytes 589832 | tf_op jit(solution)/shard_map/ppermute | solution.py:22
  194.9 1.9 collective-permute-start.3
  196.8 6.2 %collective-permute-start.2 = (bf16[128,768]{1,0:T(8,128)(2,1)S(1)}, bf16[128,768]{1,0:T(8,128)(2,1)S(1)}, u32[]{:S(2)}, u32[]{:S(2)}) collective-permute-start(bf16[128,768]{1,0:T(8,128)(2,1)S(1)} %get-tuple-element.27), channel_id=1, source_target_pairs={{0,2},{2,4},{4,6},{6,8},{8,10},{10,12},{12,14},{14,16},{16,18},{18... | collective-permute-start | bytes 589832 | tf_op jit(solution)/shard_map/ppermute | solution.py:22
  204.2 0.6 collective-permute-done.3
  204.8 1.3 collective-permute-done.2
  211.6 55.6 %all-gather.7.cloned.1.call-done = bf16[768,768]{1,0:T(8,128)(2,1)} async-done(((bf16[24,768]{1,0:T(8,128)(2,1)}), bf16[768,768]{1,0:T(8,128)(2,1)}) %all-gather.7.cloned.1.call-update) | async-done | bytes 1179664 | tf_op jit(solution)/shard_map/all_gather | solution.py:217
  267.2 1.7 multiply_reduce_fusion.2
  269.5 84.2 %all-gather.9.cloned.1.call-done = bf16[768,2304]{1,0:T(8,128)(2,1)} async-done(((bf16[24,2304]{1,0:T(8,128)(2,1)}), bf16[768,2304]{1,0:T(8,128)(2,1)}) %all-gather.9.cloned.1.call-update) | async-done | bytes 3538960 | tf_op jit(solution)/shard_map/all_gather | solution.py:218
  353.7 2.7 fusion
  356.4 0.9 copy.309
  357.4 4.4 reduce.20
  361.7 1.0 reshape.403
  362.7 6.7 %all-to-all-start = ((bf16[8,2,18432]{2,1,0:T(2,128)(2,1)}), bf16[8,2,18432]{2,1,0:T(2,128)(2,1)S(1)}, u32[]{:S(2)}, u32[]{:S(2)}) async-start(bf16[8,2,18432]{2,1,0:T(2,128)(2,1)} %reshape.403), calls=%async_computation | async-start | bytes 1179648 | tf_op jit(solution)/shard_map/all_to_all | solution.py:200
  370.2 1.1 bitcast_reduce_fusion
  372.2 1.1 fusion.86
  373.3 1.1 fusion.84
  374.4 10.4 %all-to-all-done = bf16[8,2,18432]{2,1,0:T(2,128)(2,1)S(1)} async-done(((bf16[8,2,18432]{2,1,0:T(2,128)(2,1)}), bf16[8,2,18432]{2,1,0:T(2,128)(2,1)S(1)}, u32[]{:S(2)}, u32[]{:S(2)}) %all-to-all-start) | async-done | bytes 589856 | tf_op jit(solution)/shard_map/all_to_all | solution.py:200
  385.5 0.7 fusion.140
  386.9 1.5 fusion.2
  388.4 2.7 fusion.7
  391.1 2.5 fusion.57
  393.6 1.3 reshape.347
  394.8 3.1 multiply_reduce_fusion
  397.9 1.7 fusion.4
  400.7 1.0 reshape.350
  401.7 3.4 all-to-all-start.1
  406.4 0.9 pad_maximum_fusion.2
  407.3 7.5 %all-to-all-done.1 = bf16[8,16,768]{2,1,0:T(8,128)(2,1)S(1)} async-done(((bf16[8,16,768]{2,1,0:T(8,128)(2,1)}), bf16[8,16,768]{2,1,0:T(8,128)(2,1)S(1)}, u32[]{:S(2)}, u32[]{:S(2)}) %all-to-all-start.1) | async-done | bytes 196640 | tf_op jit(solution)/shard_map/all_to_all | solution.py:204
  414.8 4.5 all-to-all-start.3
  419.3 1.1 fusion.82
  420.4 1.1 fusion.80
  421.5 1.1 fusion.78
  422.6 2.2 fusion.76
  424.8 2.4 fusion.38
  427.2 5.8 %all-to-all-done.3 = bf16[8,16,2304]{2,1,0:T(8,128)(2,1)} async-done(((bf16[8,16,2304]{2,1,0:T(8,128)(2,1)}), bf16[8,16,2304]{2,1,0:T(8,128)(2,1)}, u32[]{:S(2)}, u32[]{:S(2)}) %all-to-all-start.3) | async-done | bytes 589856 | tf_op jit(solution)/shard_map/all_to_all | solution.py:204
  433.0 2.6 multiply_reduce_fusion.1
  435.8 1.1 copy-done.7
  443.1 1.4 fusion.103
  444.5 1.4 fusion.100
  445.8 1.4 fusion.97
  447.2 1.5 fusion.94
  448.7 1.4 fusion.91
  450.1 1.4 fusion.88
  451.7 2.7 collective-permute-start.5
  454.4 5.3 %collective-permute-start.4 = (bf16[128,768]{0,1:T(8,128)(2,1)S(1)}, bf16[128,768]{0,1:T(8,128)(2,1)S(1)}, u32[]{:S(2)}, u32[]{:S(2)}) collective-permute-start(bf16[128,768]{0,1:T(8,128)(2,1)S(1)} %get-tuple-element.4), channel_id=1, source_target_pairs={{0,2},{2,4},{4,6},{6,8},{8,10},{10,12},{12,14},{14,16},{16,18},{18... | collective-permute-start | bytes 589832 | tf_op jit(solution)/shard_map/ppermute | solution.py:22
  460.0 2.2 collective-permute-start.7
  462.1 6.0 %collective-permute-start.6 = (bf16[128,768]{0,1:T(8,128)(2,1)S(1)}, bf16[128,768]{0,1:T(8,128)(2,1)S(1)}, u32[]{:S(2)}, u32[]{:S(2)}) collective-permute-start(bf16[128,768]{0,1:T(8,128)(2,1)S(1)} %get-tuple-element.2), channel_id=1, source_target_pairs={{0,2},{2,4},{4,6},{6,8},{8,10},{10,12},{12,14},{14,16},{16,18},{18... | collective-permute-start | bytes 589832 | tf_op jit(solution)/shard_map/ppermute | solution.py:22
  468.4 1.5 collective-permute-done.7
  469.9 1.5 collective-permute-done.6
  471.5 1.4 fusion.51
  472.9 0.9 fusion.68
  (300 shorter events, 20.1 us)
Async XLA Ops:
  7.2 2.8 copy-start
  7.2 90.4 %all-gather.11.cloned.1.call-start = ((), (), s32[]{:S(2)}) async-start(), calls=%async_computation.7 | async-start | bytes 1216512 | tf_op jit(solution)/shard_map/all_gather | solution.py:219
  7.9 176.3 %all-gather.5.cloned.1.call-start = ((), (), s32[]{:S(2)}) async-start(), calls=%async_computation.4 | async-start | bytes 3649536 | tf_op jit(solution)/shard_map/all_gather | solution.py:216
  8.7 258.5 %all-gather.7.cloned.1.call-start = ((), (), s32[]{:S(2)}) async-start(), calls=%async_computation.5 | async-start | bytes 1216512 | tf_op jit(solution)/shard_map/all_gather | solution.py:217
  9.4 344.3 %all-gather.9.cloned.1.call-start = ((), (), s32[]{:S(2)}) async-start(), calls=%async_computation.6 | async-start | bytes 3649536 | tf_op jit(solution)/shard_map/all_gather | solution.py:218
  99.5 84.8 %copy-start.5 = (bf16[1,128,768]{2,1,0:T(8,128)(2,1)S(1)}, bf16[1,128,768]{2,1,0:T(8,128)(2,1)}, u32[]{:S(2)}) copy-start(bf16[1,128,768]{2,1,0:T(8,128)(2,1)} %param.7) | copy-start | bytes 589828
  102.9 259.8 %all-to-all-start.2 = ((bf16[8,2,6144]{2,1,0:T(2,128)(2,1)}), bf16[8,2,6144]{2,1,0:T(2,128)(2,1)S(1)}, u32[]{:S(2)}, u32[]{:S(2)}) async-start(bf16[8,2,6144]{2,1,0:T(2,128)(2,1)} %reshape.405), calls=%async_computation.2 | async-start | bytes 393216 | tf_op jit(solution)/shard_map/all_to_all | solution.py:200
  186.9 16.9 %collective-permute-start.1 = (bf16[128,768]{1,0:T(8,128)(2,1)S(1)}, bf16[128,768]{1,0:T(8,128)(2,1)S(1)}, u32[]{:S(2)}, u32[]{:S(2)}) collective-permute-start(bf16[128,768]{1,0:T(8,128)(2,1)S(1)} %get-tuple-element.28), channel_id=1, source_target_pairs={{2,0},{4,2},{6,4},{8,6},{10,8},{12,10},{14,12},{16,14},{18,16},{20... | collective-permute-start | bytes 589832 | tf_op jit(solution)/shard_map/ppermute | solution.py:24
  189.8 14.1 %collective-permute-start = (bf16[128,768]{1,0:T(8,128)(2,1)S(1)}, bf16[128,768]{1,0:T(8,128)(2,1)S(1)}, u32[]{:S(2)}, u32[]{:S(2)}) collective-permute-start(bf16[128,768]{1,0:T(8,128)(2,1)S(1)} %get-tuple-element.28), channel_id=1, source_target_pairs={{0,2},{2,4},{4,6},{6,8},{8,10},{10,12},{12,14},{14,16},{16,18},{18... | collective-permute-start | bytes 589832 | tf_op jit(solution)/shard_map/ppermute | solution.py:22
  194.9 9.9 %collective-permute-start.3 = (bf16[128,768]{1,0:T(8,128)(2,1)S(1)}, bf16[128,768]{1,0:T(8,128)(2,1)S(1)}, u32[]{:S(2)}, u32[]{:S(2)}) collective-permute-start(bf16[128,768]{1,0:T(8,128)(2,1)S(1)} %get-tuple-element.27), channel_id=1, source_target_pairs={{2,0},{4,2},{6,4},{8,6},{10,8},{12,10},{14,12},{16,14},{18,16},{20... | collective-permute-start | bytes 589832 | tf_op jit(solution)/shard_map/ppermute | solution.py:24
  196.8 9.2 %collective-permute-start.2 = (bf16[128,768]{1,0:T(8,128)(2,1)S(1)}, bf16[128,768]{1,0:T(8,128)(2,1)S(1)}, u32[]{:S(2)}, u32[]{:S(2)}) collective-permute-start(bf16[128,768]{1,0:T(8,128)(2,1)S(1)} %get-tuple-element.27), channel_id=1, source_target_pairs={{0,2},{2,4},{4,6},{6,8},{8,10},{10,12},{12,14},{14,16},{16,18},{18... | collective-permute-start | bytes 589832 | tf_op jit(solution)/shard_map/ppermute | solution.py:22
  203.2 4.5 copy-start.65
  203.4 5.0 %copy-start.62 = (bf16[128,128]{0,1:T(8,128)(2,1)}, bf16[128,128]{0,1:T(8,128)(2,1)S(1)}, u32[]{:S(2)}) copy-start(bf16[128,128]{0,1:T(8,128)(2,1)S(1)} %copy.187) | copy-start | bytes 98308
  203.5 5.5 %copy-start.59 = (bf16[128,128]{0,1:T(8,128)(2,1)}, bf16[128,128]{0,1:T(8,128)(2,1)S(1)}, u32[]{:S(2)}) copy-start(bf16[128,128]{0,1:T(8,128)(2,1)S(1)} %copy.190) | copy-start | bytes 98308
  203.6 6.1 %copy-start.56 = (bf16[128,128]{0,1:T(8,128)(2,1)}, bf16[128,128]{0,1:T(8,128)(2,1)S(1)}, u32[]{:S(2)}) copy-start(bf16[128,128]{0,1:T(8,128)(2,1)S(1)} %copy.193) | copy-start | bytes 98308
  203.7 6.6 %copy-start.53 = (bf16[128,128]{0,1:T(8,128)(2,1)}, bf16[128,128]{0,1:T(8,128)(2,1)S(1)}, u32[]{:S(2)}) copy-start(bf16[128,128]{0,1:T(8,128)(2,1)S(1)} %copy.196) | copy-start | bytes 98308
  203.9 7.1 %copy-start.51 = (bf16[128,128]{0,1:T(8,128)(2,1)}, bf16[128,128]{0,1:T(8,128)(2,1)S(1)}, u32[]{:S(2)}) copy-start(bf16[128,128]{0,1:T(8,128)(2,1)S(1)} %copy.199) | copy-start | bytes 98308
  204.2 3.8 copy-start.45
  206.3 1.7 copy-start.20
  206.5 2.2 copy-start.49
  206.6 1.8 copy-start.17
  206.7 2.6 copy-start.47
  206.9 2.1 copy-start.14
  207.0 2.9 copy-start.43
  207.2 213.2 %copy-start.12 = (bf16[384,128]{0,1:T(8,128)(2,1)}, bf16[384,128]{0,1:T(8,128)(2,1)S(1)}, u32[]{:S(2)}) copy-start(bf16[384,128]{0,1:T(8,128)(2,1)S(1)} %copy.194) | copy-start | bytes 294916
  207.3 3.3 copy-start.41
  207.4 214.1 %copy-start.10 = (bf16[384,128]{0,1:T(8,128)(2,1)}, bf16[384,128]{0,1:T(8,128)(2,1)S(1)}, u32[]{:S(2)}) copy-start(bf16[384,128]{0,1:T(8,128)(2,1)S(1)} %copy.197) | copy-start | bytes 294916
  207.6 3.7 copy-start.39
  207.7 3.3 copy-start.8
  210.9 58.0 %copy-start.70 = (bf16[2,64,128]{2,1,0:T(8,128)(2,1)}, bf16[2,64,128]{2,1,0:T(8,128)(2,1)S(1)}, u32[]{:S(2)}) copy-start(bf16[2,64,128]{2,1,0:T(8,128)(2,1)S(1)} %convolution_convert_fusion.7) | copy-start | bytes 98308
  211.3 57.7 %copy-start.32 = (f32[2,128,384]{2,1,0:T(8,128)}, f32[2,128,384]{2,1,0:T(8,128)S(1)}, u32[]{:S(2)}) copy-start(f32[2,128,384]{2,1,0:T(8,128)S(1)} %fusion.21) | copy-start | bytes 1179652
  211.6 144.8 %copy-start.68 = (bf16[2,64,128]{2,1,0:T(8,128)(2,1)}, bf16[2,64,128]{2,1,0:T(8,128)(2,1)S(1)}, u32[]{:S(2)}) copy-start(bf16[2,64,128]{2,1,0:T(8,128)(2,1)S(1)} %convolution_convert_fusion.6) | copy-start | bytes 98308
  268.9 87.5 %copy-start.3 = (f32[128,768]{1,0:T(8,128)}, f32[128,768]{1,0:T(8,128)S(1)}, u32[]{:S(2)}) copy-start(f32[128,768]{1,0:T(8,128)S(1)} %get-tuple-element.40) | copy-start | bytes 1179652
  362.7 22.1 %all-to-all-start = ((bf16[8,2,18432]{2,1,0:T(2,128)(2,1)}), bf16[8,2,18432]{2,1,0:T(2,128)(2,1)S(1)}, u32[]{:S(2)}, u32[]{:S(2)}) async-start(bf16[8,2,18432]{2,1,0:T(2,128)(2,1)} %reshape.403), calls=%async_computation | async-start | bytes 1179648 | tf_op jit(solution)/shard_map/all_to_all | solution.py:200
  400.5 4.6 copy-start.25
  401.7 13.1 %all-to-all-start.1 = ((bf16[8,16,768]{2,1,0:T(8,128)(2,1)}), bf16[8,16,768]{2,1,0:T(8,128)(2,1)S(1)}, u32[]{:S(2)}, u32[]{:S(2)}) async-start(bf16[8,16,768]{2,1,0:T(8,128)(2,1)} %reshape.350), calls=%async_computation.1 | async-start | bytes 393216 | tf_op jit(solution)/shard_map/all_to_all | solution.py:204
  406.4 12.9 %copy-start.15 = (bf16[384,128]{0,1:T(8,128)(2,1)S(1)}, bf16[384,128]{0,1:T(8,128)(2,1)}, u32[]{:S(2)}) copy-start(bf16[384,128]{0,1:T(8,128)(2,1)} %copy-done.14) | copy-start | bytes 294916
  406.4 12.9 %copy-start.60 = (bf16[128,128]{0,1:T(8,128)(2,1)S(1)}, bf16[128,128]{0,1:T(8,128)(2,1)}, u32[]{:S(2)}) copy-start(bf16[128,128]{0,1:T(8,128)(2,1)} %copy-done.59) | copy-start | bytes 98308
  414.8 5.6 %copy-start.24 = (bf16[8,16,768]{2,1,0:T(8,128)(2,1)}, bf16[8,16,768]{2,1,0:T(8,128)(2,1)S(1)}, u32[]{:S(2)}) copy-start(bf16[8,16,768]{2,1,0:T(8,128)(2,1)S(1)} %all-to-all-done.1) | copy-start | bytes 589828
  414.8 18.2 %all-to-all-start.3 = ((bf16[8,16,2304]{2,1,0:T(8,128)(2,1)}), bf16[8,16,2304]{2,1,0:T(8,128)(2,1)}, u32[]{:S(2)}, u32[]{:S(2)}) async-start(bf16[8,16,2304]{2,1,0:T(8,128)(2,1)} %pad_maximum_fusion.2), calls=%async_computation.3 | async-start | bytes 1179648 | tf_op jit(solution)/shard_map/all_to_all | solution.py:204
  422.6 10.4 %copy-start.2 = (bf16[768,2304]{1,0:T(8,128)(2,1)S(1)}, bf16[768,2304]{1,0:T(8,128)(2,1)}, u32[]{:S(2)}) copy-start(bf16[768,2304]{1,0:T(8,128)(2,1)} %all-gather.9.cloned.1.call-done) | copy-start | bytes 10616836
  433.0 2.7 copy-start.4
  433.0 2.7 copy-start.23
  433.0 2.7 copy-start.80
  437.9 1.4 copy-start.64
  438.2 1.5 copy-start.75
  438.2 1.5 copy-start.38
  438.2 1.5 copy-start.48
  438.8 1.4 copy-start.61
  439.1 1.5 copy-start.73
  439.1 1.5 copy-start.37
  439.1 1.5 copy-start.44
  439.7 1.4 copy-start.58
  440.0 1.5 copy-start.71
  440.0 1.5 copy-start.36
  440.0 1.5 copy-start.42
  440.9 1.5 copy-start.35
  440.9 1.4 copy-start.40
  451.7 16.6 %collective-permute-start.5 = (bf16[128,768]{0,1:T(8,128)(2,1)S(1)}, bf16[128,768]{0,1:T(8,128)(2,1)S(1)}, u32[]{:S(2)}, u32[]{:S(2)}) collective-permute-start(bf16[128,768]{0,1:T(8,128)(2,1)S(1)} %get-tuple-element.5), channel_id=1, source_target_pairs={{2,0},{4,2},{6,4},{8,6},{10,8},{12,10},{14,12},{16,14},{18,16},{20... | collective-permute-start | bytes 589832 | tf_op jit(solution)/shard_map/ppermute | solution.py:24
  454.4 13.9 %collective-permute-start.4 = (bf16[128,768]{0,1:T(8,128)(2,1)S(1)}, bf16[128,768]{0,1:T(8,128)(2,1)S(1)}, u32[]{:S(2)}, u32[]{:S(2)}) collective-permute-start(bf16[128,768]{0,1:T(8,128)(2,1)S(1)} %get-tuple-element.4), channel_id=1, source_target_pairs={{0,2},{2,4},{4,6},{6,8},{8,10},{10,12},{12,14},{14,16},{16,18},{18... | collective-permute-start | bytes 589832 | tf_op jit(solution)/shard_map/ppermute | solution.py:22
  459.8 11.6 %copy-start.1 = (bf16[768,2304]{1,0:T(8,128)(2,1)S(1)}, bf16[768,2304]{1,0:T(8,128)(2,1)}, u32[]{:S(2)}) copy-start(bf16[768,2304]{1,0:T(8,128)(2,1)} %all-gather.5.cloned.1.call-done) | copy-start | bytes 10616836
  459.9 11.5 %copy-start.6 = (bf16[1,128,768]{2,1,0:T(8,128)(2,1)S(1)}, bf16[1,128,768]{2,1,0:T(8,128)(2,1)}, u32[]{:S(2)}) copy-start(bf16[1,128,768]{2,1,0:T(8,128)(2,1)} %param.7) | copy-start | bytes 589828
  460.0 9.9 %collective-permute-start.7 = (bf16[128,768]{0,1:T(8,128)(2,1)S(1)}, bf16[128,768]{0,1:T(8,128)(2,1)S(1)}, u32[]{:S(2)}, u32[]{:S(2)}) collective-permute-start(bf16[128,768]{0,1:T(8,128)(2,1)S(1)} %get-tuple-element.3), channel_id=1, source_target_pairs={{2,0},{4,2},{6,4},{8,6},{10,8},{12,10},{14,12},{16,14},{18,16},{20... | collective-permute-start | bytes 589832 | tf_op jit(solution)/shard_map/ppermute | solution.py:24
  462.1 9.2 %collective-permute-start.6 = (bf16[128,768]{0,1:T(8,128)(2,1)S(1)}, bf16[128,768]{0,1:T(8,128)(2,1)S(1)}, u32[]{:S(2)}, u32[]{:S(2)}) collective-permute-start(bf16[128,768]{0,1:T(8,128)(2,1)S(1)} %get-tuple-element.2), channel_id=1, source_target_pairs={{0,2},{2,4},{4,6},{6,8},{8,10},{10,12},{12,14},{14,16},{16,18},{18... | collective-permute-start | bytes 589832 | tf_op jit(solution)/shard_map/ppermute | solution.py:22
  (35 other events, 39.5 us)
Sparse Core Ops, SparseCore 0:
  11.2 86.2 all-gather.10
  100.7 83.4 all-gather.4
  187.4 79.7 all-gather.6
  270.2 83.4 all-gather.8
where the time goes:
time: 484 us; the launch traced here: 480 us
  waiting for transfers between devices  331 us (68%)
  starting transfers between devices  53.7 us (11%)
  matrix products  48.9 us (10%)
  local copies, waits for them, and re-layouts  16.5 us (3%)
  between operations  15.8 us (3%)
  other arithmetic  14.1 us (3%)
    all_gather x1, waiting for transfers between devices, local(): lax.all_gather(w_out_time, 'space', axis=0, tiled=True)  85.6 us
    all_gather x1, waiting for transfers between devices, local(): lax.all_gather(w_qkv_time, 'space', axis=0, tiled=True)  84.2 us
    all_gather x1, waiting for transfers between devices, local(): lax.all_gather(w_qkv_space, 'space', axis=0, tiled=True)  74.6 us
    all_gather x1, waiting for transfers between devices, local(): lax.all_gather(w_out_space, 'space', axis=0, tiled=True)  55.6 us
    ppermute x4, starting transfers between devices, padded(): lax.ppermute(tail, axis, [(i, (i + 1) % count) for i in range(ends)])  22.6 us
    all_to_all x2, starting transfers between devices, to_frames(): lax.all_to_all(local_rows[None], 'frame', split_axis=1, concat_axis=0, ti...  13.5 us
    all_to_all x2, waiting for transfers between devices, to_space(): lax.all_to_all(frame_rows, 'frame', split_axis=0, concat_axis=1, tiled=True)  13.3 us
    all_to_all x2, waiting for transfers between devices, to_frames(): lax.all_to_all(local_rows[None], 'frame', split_axis=1, concat_axis=0, ti...  10.4 us
  transfers between devices with their start and end apart: 16, of which 11 were waited for; matrix products, arithmetic and copies ran while one was open for 9% of the time, Pallas kernels for 0%

commit v1 on v0

--- a/solution.py
+++ b/solution.py
@@ -212,11 +212,14 @@
     local_in = frames_in[0]
     grad_out = cotangent[0]
     shard, feature_count = local_in.shape
+    weight_rows = jnp.concatenate([w_qkv_space, w_out_space, w_qkv_time, w_out_time], axis=1)
+    all_weights = lax.all_gather(weight_rows, "space", axis=0, tiled=True)
+    widths = [w_qkv_space.shape[1], w_out_space.shape[1], w_qkv_time.shape[1], w_out_time.shape[1]]
+    bounds = [0]
+    for width in widths:
+        bounds.append(bounds[-1] + width)
     full_qkv_space, full_out_space, full_qkv_time, full_out_time = (
-        lax.all_gather(w_qkv_space, "space", axis=0, tiled=True),
-        lax.all_gather(w_out_space, "space", axis=0, tiled=True),
-        lax.all_gather(w_qkv_time, "space", axis=0, tiled=True),
-        lax.all_gather(w_out_time, "space", axis=0, tiled=True),
+        all_weights[:, bounds[index] : bounds[index + 1]] for index in range(4)
     )
     block_count = shard // BLOCK
     space_index = lax.axis_index("space")

time: 484 us -> 303 us (0.63)
  waiting for transfers between devices: 331 us -> 149 us
    all_gather x4 -> x1, waiting for transfers between devices: 300 us -> 113 us  [local(): all_weights = lax.all_gather(weight_rows, 'space', axis=0, tiled=True)]
  transfers between devices with their start and end apart: 16 -> 13, of which waited for: 11 -> 6; matrix products, arithmetic and copies ran while one was open for 9% -> 12% of each run, Pallas kernels for 0% -> 0%
where the time goes in v1:
time: 303 us; the launch traced here: 298 us
  waiting for transfers between devices  149 us (49%)
  matrix products  52 us (17%)
  starting transfers between devices  49.6 us (16%)
  local copies, waits for them, and re-layouts  17.4 us (6%)
  between operations  15.7 us (5%)
  other arithmetic  14.7 us (5%)
    all_gather x1, waiting for transfers between devices, local(): all_weights = lax.all_gather(weight_rows, 'space', axis=0, tiled=True)  113 us
    ppermute x4, starting transfers between devices, padded(): lax.ppermute(tail, axis, [(i, (i + 1) % count) for i in range(ends)])  19.9 us
    all_to_all x2, waiting for transfers between devices, to_space(): lax.all_to_all(frame_rows, 'frame', split_axis=0, concat_axis=1, tiled=True)  17 us
    all_to_all x2, starting transfers between devices, to_frames(): lax.all_to_all(local_rows[None], 'frame', split_axis=1, concat_axis=0, ti...  13.9 us
    all_to_all x2, waiting for transfers between devices, to_frames(): lax.all_to_all(local_rows[None], 'frame', split_axis=1, concat_axis=0, ti...  11.6 us
    dot_general x6, matrix products, space_back(): jnp.einsum('gst,sgh->tgh', probability, grad_part, preferred_element_type...  9.81 us
    ppermute x4, starting transfers between devices, padded(): lax.ppermute(head, axis, [((i + 1) % count, i) for i in range(ends)])  8.53 us
    unnamed x4, other arithmetic  7.2 us
  transfers between devices with their start and end apart: 13, of which 6 were waited for; matrix products, arithmetic and copies ran while one was open for 12% of the time, Pallas kernels for 0%

profile of v1, /device:TPU:6, one launch (start us, length us, event | category | flops | bytes accessed | tf_op | source)
XLA Modules:
  0.0 298.4 jit_solution(5994388892875304705)
XLA Ops:
  7.2 1.7 pad_maximum_fusion.3
  9.3 1.0 fusion.55
  10.4 0.6 multiply_multiply_fusion
  11.0 112.7 %all-gather.2.cloned.1.call-done = bf16[768,6144]{1,0:T(8,128)(2,1)} async-done(((bf16[24,6144]{1,0:T(8,128)(2,1)}), bf16[768,6144]{1,0:T(8,128)(2,1)}) %all-gather.2.cloned.1.call-update) | async-done | bytes 9437200 | tf_op jit(solution)/shard_map/all_gather | solution.py:216
  123.7 2.8 convolution_convert_fusion.1
  126.5 3.2 %collective-permute-start.2 = (bf16[128,768]{1,0:T(8,128)(2,1)S(1)}, bf16[128,768]{1,0:T(8,128)(2,1)S(1)}, u32[]{:S(2)}, u32[]{:S(2)}) collective-permute-start(bf16[128,768]{1,0:T(8,128)(2,1)S(1)} %get-tuple-element.27), channel_id=1, source_target_pairs={{0,2},{2,4},{4,6},{6,8},{8,10},{10,12},{12,14},{14,16},{16,18},{18... | collective-permute-start | bytes 589832 | tf_op jit(solution)/shard_map/ppermute | solution.py:22
  129.8 2.8 collective-permute-start.3
  132.6 5.2 %collective-permute-start = (bf16[128,768]{1,0:T(8,128)(2,1)S(1)}, bf16[128,768]{1,0:T(8,128)(2,1)S(1)}, u32[]{:S(2)}, u32[]{:S(2)}) collective-permute-start(bf16[128,768]{1,0:T(8,128)(2,1)S(1)} %get-tuple-element.28), channel_id=1, source_target_pairs={{0,2},{2,4},{4,6},{6,8},{8,10},{10,12},{12,14},{14,16},{16,18},{18... | collective-permute-start | bytes 589832 | tf_op jit(solution)/shard_map/ppermute | solution.py:22
  137.8 1.9 collective-permute-start.1
  140.5 1.8 fusion.43
  142.2 0.4 copy.208
  142.7 0.5 broadcast.211
  143.2 1.8 reduce.19
  144.9 0.7 reshape.405
  145.7 6.7 %all-to-all-start.2 = ((bf16[8,2,6144]{2,1,0:T(2,128)(2,1)}), bf16[8,2,6144]{2,1,0:T(2,128)(2,1)S(1)}, u32[]{:S(2)}, u32[]{:S(2)}) async-start(bf16[8,2,6144]{2,1,0:T(2,128)(2,1)} %reshape.405), calls=%async_computation.2 | async-start | bytes 393216 | tf_op jit(solution)/shard_map/all_to_all | solution.py:200
  154.0 0.5 copy-done.39
  158.9 0.4 copy-done.9
  159.3 1.7 multiply_reduce_fusion.2
  161.1 2.7 fusion
  163.8 0.9 copy.309
  164.7 4.3 %reduce.20 = bf16[128,2304]{1,0:T(8,128)(2,1)S(1)} reduce(bf16[128,1,2304]{2,1,0:T(2,128)(2,1)S(1)} %bitcast.286, bf16[]{:T(256)} %broadcast.211), dimensions={1}, to_apply=%bitcast.285.reduce_sub_computation | reduce | bytes 1179650
  169.0 1.0 reshape.403
  170.0 7.2 %all-to-all-start = ((bf16[8,2,18432]{2,1,0:T(2,128)(2,1)}), bf16[8,2,18432]{2,1,0:T(2,128)(2,1)S(1)}, u32[]{:S(2)}, u32[]{:S(2)}) async-start(bf16[8,2,18432]{2,1,0:T(2,128)(2,1)} %reshape.403), calls=%async_computation | async-start | bytes 1179648 | tf_op jit(solution)/shard_map/all_to_all | solution.py:200
  177.2 0.6 iota_compare_fusion
  177.7 1.1 fusion.94
  178.8 1.1 fusion.96
  180.1 1.1 bitcast_reduce_fusion
  181.6 1.1 bitcast_convert_fusion
  182.7 11.6 %all-to-all-done = bf16[8,2,18432]{2,1,0:T(2,128)(2,1)S(1)} async-done(((bf16[8,2,18432]{2,1,0:T(2,128)(2,1)}), bf16[8,2,18432]{2,1,0:T(2,128)(2,1)S(1)}, u32[]{:S(2)}, u32[]{:S(2)}) %all-to-all-start) | async-done | bytes 589856 | tf_op jit(solution)/shard_map/all_to_all | solution.py:200
  194.3 0.6 reshape.404
  196.0 1.3 fusion.8
  197.3 0.9 copy-done.54
  198.2 1.1 fusion.67
  199.3 3.4 %multiply_reduce_fusion = (f32[16,12,8]{2,1,0:T(8,128)S(1)}, bf16[16,12,64,8]{2,3,1,0:T(8,128)(2,1)}) fusion(f32[16,12,8,64]{3,1,0,2:T(8,128)} %bitcast_convert_fusion, f32[16,12,8,8]{2,3,1,0:T(8,128)} %copy-done.54, bf16[8,16,12,64]{3,2,1,0:T(8,128)(2,1)S(1)} %reshape.347), kind=kOutput, calls=%fused_computation.101 | convolution fusion | flops 1990663 | bytes 841728 | tf_op jit(solution)/shard_map/phfg,gphd->fphd/dot_general | solution.py:145
  202.7 1.7 fusion.10
  204.4 1.2 fusion.15
  206.0 2.0 fusion.13
  209.6 1.0 reshape.350
  210.6 3.4 %all-to-all-start.1 = ((bf16[8,16,768]{2,1,0:T(8,128)(2,1)}), bf16[8,16,768]{2,1,0:T(8,128)(2,1)S(1)}, u32[]{:S(2)}, u32[]{:S(2)}) async-start(bf16[8,16,768]{2,1,0:T(8,128)(2,1)} %reshape.350), calls=%async_computation.1 | async-start | bytes 393216 | tf_op jit(solution)/shard_map/all_to_all | solution.py:204
  214.0 0.8 pad_maximum_fusion.2
  214.9 8.8 %all-to-all-done.1 = bf16[8,16,768]{2,1,0:T(8,128)(2,1)S(1)} async-done(((bf16[8,16,768]{2,1,0:T(8,128)(2,1)}), bf16[8,16,768]{2,1,0:T(8,128)(2,1)S(1)}, u32[]{:S(2)}, u32[]{:S(2)}) %all-to-all-start.1) | async-done | bytes 196640 | tf_op jit(solution)/shard_map/all_to_all | solution.py:204
  223.7 3.8 %all-to-all-start.3 = ((bf16[8,16,2304]{2,1,0:T(8,128)(2,1)}), bf16[8,16,2304]{2,1,0:T(8,128)(2,1)S(1)}, u32[]{:S(2)}, u32[]{:S(2)}) async-start(bf16[8,16,2304]{2,1,0:T(8,128)(2,1)} %pad_maximum_fusion.2), calls=%async_computation.3 | async-start | bytes 1179648 | tf_op jit(solution)/shard_map/all_to_all | solution.py:204
  229.0 1.1 fusion.88
  230.1 1.1 fusion.86
  231.2 2.3 fusion.44
  233.5 8.2 %all-to-all-done.3 = bf16[8,16,2304]{2,1,0:T(8,128)(2,1)S(1)} async-done(((bf16[8,16,2304]{2,1,0:T(8,128)(2,1)}), bf16[8,16,2304]{2,1,0:T(8,128)(2,1)S(1)}, u32[]{:S(2)}, u32[]{:S(2)}) %all-to-all-start.3) | async-done | bytes 589856 | tf_op jit(solution)/shard_map/all_to_all | solution.py:204
  241.7 3.4 %multiply_reduce_fusion.1 = (f32[128]{0:T(128)S(1)}, f32[128,768]{1,0:T(8,128)S(1)}) fusion(f32[128,768]{1,0:T(8,128)S(1)} %get-tuple-element.40, bf16[128,2304]{1,0:T(8,128)(2,1)S(1)} %bitcast.315, bf16[768,6144]{1,0:T(8,128)(2,1)} %all-gather.2.cloned.1.call-done), kind=kOutput, calls=%fused_computation.120 | convolution fusion | flops 453181312 | bytes 4915712 | tf_op jit(solution)/shard_map/dot_general | solution.py:259
  245.4 1.8 convolution_convert_fusion.4
  247.2 0.6 fusion.155
  248.0 2.1 fusion.98
  250.9 2.1 fusion.101
  253.8 1.4 fusion.104
  256.1 1.4 fusion.107
  258.4 1.5 fusion.110
  260.7 1.4 fusion.113
  262.9 0.4 copy-done.37
  263.6 5.5 %collective-permute-start.6 = (bf16[128,768]{0,1:T(8,128)(2,1)S(1)}, bf16[128,768]{0,1:T(8,128)(2,1)S(1)}, u32[]{:S(2)}, u32[]{:S(2)}) collective-permute-start(bf16[128,768]{0,1:T(8,128)(2,1)S(1)} %get-tuple-element.2), channel_id=1, source_target_pairs={{0,2},{2,4},{4,6},{6,8},{8,10},{10,12},{12,14},{14,16},{16,18},{18... | collective-permute-start | bytes 589832 | tf_op jit(solution)/shard_map/ppermute | solution.py:22
  269.1 1.9 collective-permute-start.7
  271.3 6.0 %collective-permute-start.4 = (bf16[128,768]{0,1:T(8,128)(2,1)S(1)}, bf16[128,768]{0,1:T(8,128)(2,1)S(1)}, u32[]{:S(2)}, u32[]{:S(2)}) collective-permute-start(bf16[128,768]{0,1:T(8,128)(2,1)S(1)} %get-tuple-element.4), channel_id=1, source_target_pairs={{0,2},{2,4},{4,6},{6,8},{8,10},{10,12},{12,14},{14,16},{16,18},{18... | collective-permute-start | bytes 589832 | tf_op jit(solution)/shard_map/ppermute | solution.py:22
  277.3 1.9 collective-permute-start.5
  279.4 1.1 collective-permute-done.4
  280.5 6.5 %collective-permute-done.5 = bf16[128,768]{0,1:T(8,128)(2,1)S(1)} collective-permute-done((bf16[128,768]{0,1:T(8,128)(2,1)S(1)}, bf16[128,768]{0,1:T(8,128)(2,1)S(1)}, u32[]{:S(2)}, u32[]{:S(2)}) %collective-permute-start.5) | collective-permute-done | bytes 196640 | tf_op jit(solution)/shard_map/ppermute | solution.py:24
  287.2 3.4 %fusion.61 = (f32[128]{0:T(128)S(1)}, f32[128,768]{1,0:T(8,128)S(1)}) fusion(bf16[1,128,768]{2,1,0:T(8,128)(2,1)S(1)} %copy-done.1, bf16[128,2304]{0,1:T(8,128)(2,1)S(1)} %fusion.77, bf16[768,6144]{1,0:T(8,128)(2,1)} %all-gather.2.cloned.1.call-done), kind=kOutput, calls=%fused_computation.112 | convolution fusion | flops 453279616 | bytes 4719104 | tf_op jit(solution)/shard_map/dot_general | solution.py:289
  290.7 0.9 fusion.78
  (236 shorter events, 17.5 us)
Async XLA Ops:
  7.2 1.8 copy-start
  7.2 116.5 %all-gather.2.cloned.1.call-start = ((), (), s32[]{:S(2)}) async-start(), calls=%async_computation.4 | async-start | bytes 9732096 | tf_op jit(solution)/shard_map/all_gather | solution.py:216
  11.0 112.7 %copy-start.52 = (f32[128]{0:T(128)}, f32[128]{0:T(128)S(1)}, u32[]{:S(2)}) copy-start(f32[128]{0:T(128)S(1)} %get-tuple-element.36) | copy-start | bytes 1540
  126.5 14.0 %copy-start.34 = (bf16[1,128,768]{2,1,0:T(8,128)(2,1)S(1)}, bf16[1,128,768]{2,1,0:T(8,128)(2,1)}, u32[]{:S(2)}) copy-start(bf16[1,128,768]{2,1,0:T(8,128)(2,1)} %param.8) | copy-start | bytes 589828
  126.5 25.9 %collective-permute-start.2 = (bf16[128,768]{1,0:T(8,128)(2,1)S(1)}, bf16[128,768]{1,0:T(8,128)(2,1)S(1)}, u32[]{:S(2)}, u32[]{:S(2)}) collective-permute-start(bf16[128,768]{1,0:T(8,128)(2,1)S(1)} %get-tuple-element.27), channel_id=1, source_target_pairs={{0,2},{2,4},{4,6},{6,8},{8,10},{10,12},{12,14},{14,16},{16,18},{18... | collective-permute-start | bytes 589832 | tf_op jit(solution)/shard_map/ppermute | solution.py:22
  129.8 22.7 %collective-permute-start.3 = (bf16[128,768]{1,0:T(8,128)(2,1)S(1)}, bf16[128,768]{1,0:T(8,128)(2,1)S(1)}, u32[]{:S(2)}, u32[]{:S(2)}) collective-permute-start(bf16[128,768]{1,0:T(8,128)(2,1)S(1)} %get-tuple-element.27), channel_id=1, source_target_pairs={{2,0},{4,2},{6,4},{8,6},{10,8},{12,10},{14,12},{16,14},{18,16},{20... | collective-permute-start | bytes 589832 | tf_op jit(solution)/shard_map/ppermute | solution.py:24
  132.6 20.1 %collective-permute-start = (bf16[128,768]{1,0:T(8,128)(2,1)S(1)}, bf16[128,768]{1,0:T(8,128)(2,1)S(1)}, u32[]{:S(2)}, u32[]{:S(2)}) collective-permute-start(bf16[128,768]{1,0:T(8,128)(2,1)S(1)} %get-tuple-element.28), channel_id=1, source_target_pairs={{0,2},{2,4},{4,6},{6,8},{8,10},{10,12},{12,14},{14,16},{16,18},{18... | collective-permute-start | bytes 589832 | tf_op jit(solution)/shard_map/ppermute | solution.py:22
  137.8 15.0 %collective-permute-start.1 = (bf16[128,768]{1,0:T(8,128)(2,1)S(1)}, bf16[128,768]{1,0:T(8,128)(2,1)S(1)}, u32[]{:S(2)}, u32[]{:S(2)}) collective-permute-start(bf16[128,768]{1,0:T(8,128)(2,1)S(1)} %get-tuple-element.28), channel_id=1, source_target_pairs={{2,0},{4,2},{6,4},{8,6},{10,8},{12,10},{14,12},{16,14},{18,16},{20... | collective-permute-start | bytes 589832 | tf_op jit(solution)/shard_map/ppermute | solution.py:24
  140.1 16.0 %copy-start.26 = (bf16[128,128]{0,1:T(8,128)(2,1)}, bf16[128,128]{0,1:T(8,128)(2,1)S(1)}, u32[]{:S(2)}) copy-start(bf16[128,128]{0,1:T(8,128)(2,1)S(1)} %copy.191) | copy-start | bytes 98308
  140.2 16.5 %copy-start.28 = (bf16[128,128]{0,1:T(8,128)(2,1)}, bf16[128,128]{0,1:T(8,128)(2,1)S(1)}, u32[]{:S(2)}) copy-start(bf16[128,128]{0,1:T(8,128)(2,1)S(1)} %copy.194) | copy-start | bytes 98308
  140.3 17.0 %copy-start.30 = (bf16[128,128]{0,1:T(8,128)(2,1)}, bf16[128,128]{0,1:T(8,128)(2,1)S(1)}, u32[]{:S(2)}) copy-start(bf16[128,128]{0,1:T(8,128)(2,1)S(1)} %copy.197) | copy-start | bytes 98308
  140.5 17.8 %copy-start.32 = (bf16[128,128]{0,1:T(8,128)(2,1)}, bf16[128,128]{0,1:T(8,128)(2,1)S(1)}, u32[]{:S(2)}) copy-start(bf16[128,128]{0,1:T(8,128)(2,1)S(1)} %copy.200) | copy-start | bytes 98308
  145.7 24.3 %all-to-all-start.2 = ((bf16[8,2,6144]{2,1,0:T(2,128)(2,1)}), bf16[8,2,6144]{2,1,0:T(2,128)(2,1)S(1)}, u32[]{:S(2)}, u32[]{:S(2)}) async-start(bf16[8,2,6144]{2,1,0:T(2,128)(2,1)} %reshape.405), calls=%async_computation.2 | async-start | bytes 393216 | tf_op jit(solution)/shard_map/all_to_all | solution.py:200
  153.0 2.7 copy-start.16
  153.3 1.3 copy-start.14
  153.6 1.3 copy-start.4
  154.6 1.7 copy-start.18
  154.9 2.1 copy-start.20
  155.2 2.5 copy-start.22
  155.4 3.1 %copy-start.24 = (bf16[384,128]{0,1:T(8,128)(2,1)}, bf16[384,128]{0,1:T(8,128)(2,1)S(1)}, u32[]{:S(2)}) copy-start(bf16[384,128]{0,1:T(8,128)(2,1)S(1)} %copy.199) | copy-start | bytes 294916
  155.7 0.9 copy-start.5
  156.0 0.9 copy-start.41
  156.4 1.0 copy-start.6
  156.7 1.0 copy-start.43
  157.0 1.2 copy-start.7
  157.6 1.2 copy-start.8
  158.2 2.8 copy-start.47
  158.2 1.1 copy-start.1
  158.6 0.8 copy-start.9
  158.9 4.9 %copy-start.49 = (bf16[2,64,128]{2,1,0:T(8,128)(2,1)}, bf16[2,64,128]{2,1,0:T(8,128)(2,1)S(1)}, u32[]{:S(2)}) copy-start(bf16[2,64,128]{2,1,0:T(8,128)(2,1)S(1)} %convolution_convert_fusion.6) | copy-start | bytes 98308
  170.0 24.3 %all-to-all-start = ((bf16[8,2,18432]{2,1,0:T(2,128)(2,1)}), bf16[8,2,18432]{2,1,0:T(2,128)(2,1)S(1)}, u32[]{:S(2)}, u32[]{:S(2)}) async-start(bf16[8,2,18432]{2,1,0:T(2,128)(2,1)} %reshape.403), calls=%async_computation | async-start | bytes 1179648 | tf_op jit(solution)/shard_map/all_to_all | solution.py:200
  197.3 0.9 copy-start.54
  206.0 2.0 copy-start.2
  208.5 1.0 copy-start.3
  210.6 13.1 %all-to-all-start.1 = ((bf16[8,16,768]{2,1,0:T(8,128)(2,1)}), bf16[8,16,768]{2,1,0:T(8,128)(2,1)S(1)}, u32[]{:S(2)}, u32[]{:S(2)}) async-start(bf16[8,16,768]{2,1,0:T(8,128)(2,1)} %reshape.350), calls=%async_computation.1 | async-start | bytes 393216 | tf_op jit(solution)/shard_map/all_to_all | solution.py:204
  214.0 13.5 %copy-start.27 = (bf16[128,128]{0,1:T(8,128)(2,1)S(1)}, bf16[128,128]{0,1:T(8,128)(2,1)}, u32[]{:S(2)}) copy-start(bf16[128,128]{0,1:T(8,128)(2,1)} %copy-done.26) | copy-start | bytes 98308
  223.7 18.1 %all-to-all-start.3 = ((bf16[8,16,2304]{2,1,0:T(8,128)(2,1)}), bf16[8,16,2304]{2,1,0:T(8,128)(2,1)S(1)}, u32[]{:S(2)}, u32[]{:S(2)}) async-start(bf16[8,16,2304]{2,1,0:T(8,128)(2,1)} %pad_maximum_fusion.2), calls=%async_computation.3 | async-start | bytes 1179648 | tf_op jit(solution)/shard_map/all_to_all | solution.py:204
  229.0 1.1 copy-start.33
  241.7 3.4 %copy-start.35 = (bf16[1,128,768]{2,1,0:T(8,128)(2,1)S(1)}, bf16[1,128,768]{2,1,0:T(8,128)(2,1)}, u32[]{:S(2)}) copy-start(bf16[1,128,768]{2,1,0:T(8,128)(2,1)} %param.8) | copy-start | bytes 589828
  245.3 2.6 copy-start.50
  247.2 2.9 copy-start.13
  247.2 2.9 copy-start.25
  248.0 2.9 copy-start.48
  250.4 2.6 copy-start.12
  250.4 2.6 copy-start.23
  250.9 2.9 copy-start.46
  253.3 2.0 copy-start.21
  253.8 2.2 copy-start.44
  255.5 2.0 copy-start.19
  256.1 2.2 copy-start.42
  257.8 2.1 copy-start.11
  257.8 2.1 copy-start.17
  258.3 2.2 copy-start.38
  258.3 2.3 copy-start.40
  260.1 2.0 copy-start.10
  260.1 2.0 copy-start.15
  262.4 0.9 copy-start.37
  262.6 1.0 copy-start.36
  263.6 23.5 %collective-permute-start.6 = (bf16[128,768]{0,1:T(8,128)(2,1)S(1)}, bf16[128,768]{0,1:T(8,128)(2,1)S(1)}, u32[]{:S(2)}, u32[]{:S(2)}) collective-permute-start(bf16[128,768]{0,1:T(8,128)(2,1)S(1)} %get-tuple-element.2), channel_id=1, source_target_pairs={{0,2},{2,4},{4,6},{6,8},{8,10},{10,12},{12,14},{14,16},{16,18},{18... | collective-permute-start | bytes 589832 | tf_op jit(solution)/shard_map/ppermute | solution.py:22
  269.1 18.0 %collective-permute-start.7 = (bf16[128,768]{0,1:T(8,128)(2,1)S(1)}, bf16[128,768]{0,1:T(8,128)(2,1)S(1)}, u32[]{:S(2)}, u32[]{:S(2)}) collective-permute-start(bf16[128,768]{0,1:T(8,128)(2,1)S(1)} %get-tuple-element.3), channel_id=1, source_target_pairs={{2,0},{4,2},{6,4},{8,6},{10,8},{12,10},{14,12},{16,14},{18,16},{20... | collective-permute-start | bytes 589832 | tf_op jit(solution)/shard_map/ppermute | solution.py:24
  271.3 9.2 %collective-permute-start.4 = (bf16[128,768]{0,1:T(8,128)(2,1)S(1)}, bf16[128,768]{0,1:T(8,128)(2,1)S(1)}, u32[]{:S(2)}, u32[]{:S(2)}) collective-permute-start(bf16[128,768]{0,1:T(8,128)(2,1)S(1)} %get-tuple-element.4), channel_id=1, source_target_pairs={{0,2},{2,4},{4,6},{6,8},{8,10},{10,12},{12,14},{14,16},{16,18},{18... | collective-permute-start | bytes 589832 | tf_op jit(solution)/shard_map/ppermute | solution.py:22
  277.3 9.7 %collective-permute-start.5 = (bf16[128,768]{0,1:T(8,128)(2,1)S(1)}, bf16[128,768]{0,1:T(8,128)(2,1)S(1)}, u32[]{:S(2)}, u32[]{:S(2)}) collective-permute-start(bf16[128,768]{0,1:T(8,128)(2,1)S(1)} %get-tuple-element.5), channel_id=1, source_target_pairs={{2,0},{4,2},{6,4},{8,6},{10,8},{12,10},{14,12},{16,14},{18,16},{20... | collective-permute-start | bytes 589832 | tf_op jit(solution)/shard_map/ppermute | solution.py:24
  287.2 3.4 %copy-start.51 = (f32[128]{0:T(128)S(1)}, f32[128]{0:T(128)}, u32[]{:S(2)}) copy-start(f32[128]{0:T(128)} %get-tuple-element.35) | copy-start | bytes 1540
  287.2 3.4 %copy-start.53 = (f32[128]{0:T(128)S(1)}, f32[128]{0:T(128)}, u32[]{:S(2)}) copy-start(f32[128]{0:T(128)} %copy-done.52) | copy-start | bytes 1540
  (4 other events, 2.7 us)
Sparse Core Ops, SparseCore 0:
  11.2 112.4 all-gather.1

commit v2 on v1

--- a/solution.py
+++ b/solution.py
@@ -52,76 +52,60 @@
     score_scale = HD ** (-0.5)
     query_count = queries.shape[0]
     key_count = key_rows.shape[0]
-    output_list = []
-    total_list = []
-    for head_pair in range(HEADS // 2):
-        start_col = head_pair * 2 * HD
-        stop_col = start_col + 2 * HD
-        query_part = queries[:, start_col:stop_col].reshape(query_count, 2, HD)
-        key_part = key_rows[:, start_col:stop_col].reshape(key_count, 2, HD)
-        value_part = value_rows[:, start_col:stop_col].reshape(key_count, 2, HD)
-        scores = (
-            jnp.einsum("sgh,tgh->gst", query_part, key_part, preferred_element_type=jnp.float32)
-            * score_scale
-        )
-        exponent = jnp.where(allowed[None], jnp.exp(scores), 0.0)
-        totals = jnp.sum(exponent, axis=-1)
-        probability = (exponent / totals[:, :, None]).astype(jnp.bfloat16)
-        combined = jnp.einsum(
-            "gst,tgh->sgh", probability, value_part, preferred_element_type=jnp.float32
-        )
-        output_list.append(combined.astype(jnp.bfloat16).reshape(query_count, 2 * HD))
-        total_list.append(totals)
-    return (jnp.concatenate(output_list, axis=1), jnp.concatenate(total_list, axis=0))
+    query_heads = queries.reshape(query_count, HEADS, HD)
+    key_heads = key_rows.reshape(key_count, HEADS, HD)
+    value_heads = value_rows.reshape(key_count, HEADS, HD)
+    scores = (
+        jnp.einsum("sgh,tgh->gst", query_heads, key_heads, preferred_element_type=jnp.float32)
+        * score_scale
+    )
+    exponent = jnp.where(allowed[None], jnp.exp(scores), 0.0)
+    totals = jnp.sum(exponent, axis=-1)
+    probability = (exponent / totals[:, :, None]).astype(jnp.bfloat16)
+    combined = jnp.einsum(
+        "gst,tgh->sgh", probability, value_heads, preferred_element_type=jnp.float32
+    )
+    return combined.astype(jnp.bfloat16).reshape(query_count, HEADS * HD), totals
 
 
 def space_back(queries, key_rows, value_rows, allowed, totals, attended, grad_attended):
     score_scale = HD ** (-0.5)
     query_count = queries.shape[0]
     key_count = key_rows.shape[0]
-    query_list = []
-    key_list = []
-    value_list = []
-    for head_pair in range(HEADS // 2):
-        start_col = head_pair * 2 * HD
-        stop_col = start_col + 2 * HD
-        query_part = queries[:, start_col:stop_col].reshape(query_count, 2, HD)
-        key_part = key_rows[:, start_col:stop_col].reshape(key_count, 2, HD)
-        value_part = value_rows[:, start_col:stop_col].reshape(key_count, 2, HD)
-        out_part = attended[:, start_col:stop_col].reshape(query_count, 2, HD)
-        grad_part = grad_attended[:, start_col:stop_col].reshape(query_count, 2, HD)
-        scores = (
-            jnp.einsum("sgh,tgh->gst", query_part, key_part, preferred_element_type=jnp.float32)
-            * score_scale
-        )
-        exponent = jnp.where(allowed[None], jnp.exp(scores), 0.0)
-        weight = exponent / totals[2 * head_pair : 2 * head_pair + 2, :, None]
-        probability = weight.astype(jnp.bfloat16)
-        prob_grad = jnp.einsum(
-            "sgh,tgh->gst", grad_part, value_part, preferred_element_type=jnp.float32
-        )
-        row_delta = jnp.einsum(
-            "sgh,sgh->gs", grad_part, out_part, preferred_element_type=jnp.float32
-        )
-        score_grad = (weight * (prob_grad - row_delta[:, :, None])).astype(jnp.bfloat16)
-        query_grad = (
-            jnp.einsum("gst,tgh->sgh", score_grad, key_part, preferred_element_type=jnp.float32)
-            * score_scale
-        )
-        key_grad = (
-            jnp.einsum("gst,sgh->tgh", score_grad, query_part, preferred_element_type=jnp.float32)
-            * score_scale
-        )
-        value_grad = jnp.einsum(
-            "gst,sgh->tgh", probability, grad_part, preferred_element_type=jnp.float32
-        )
-        query_list.append(query_grad.astype(jnp.bfloat16).reshape(query_count, 2 * HD))
-        key_list.append(key_grad.reshape(key_count, 2 * HD))
-        value_list.append(value_grad.reshape(key_count, 2 * HD))
+    query_heads = queries.reshape(query_count, HEADS, HD)
+    key_heads = key_rows.reshape(key_count, HEADS, HD)
+    value_heads = value_rows.reshape(key_count, HEADS, HD)
+    out_heads = attended.reshape(query_count, HEADS, HD)
+    grad_heads = grad_attended.reshape(query_count, HEADS, HD)
+    scores = (
+        jnp.einsum("sgh,tgh->gst", query_heads, key_heads, preferred_element_type=jnp.float32)
+        * score_scale
+    )
+    exponent = jnp.where(allowed[None], jnp.exp(scores), 0.0)
+    weight = exponent / totals[:, :, None]
+    probability = weight.astype(jnp.bfloat16)
+    prob_grad = jnp.einsum(
+        "sgh,tgh->gst", grad_heads, value_heads, preferred_element_type=jnp.float32
+    )
+    row_delta = jnp.einsum(
+        "sgh,sgh->gs", grad_heads, out_heads, preferred_element_type=jnp.float32
+    )
+    score_grad = (weight * (prob_grad - row_delta[:, :, None])).astype(jnp.bfloat16)
+    query_grad = (
+        jnp.einsum("gst,tgh->sgh", score_grad, key_heads, preferred_element_type=jnp.float32)
+        * score_scale
+    )
+    key_grad = (
+        jnp.einsum("gst,sgh->tgh", score_grad, query_heads, preferred_element_type=jnp.float32)
+        * score_scale
+    )
+    value_grad = jnp.einsum(
+        "gst,sgh->tgh", probability, grad_heads, preferred_element_type=jnp.float32
+    )
     return (
-        jnp.concatenate(query_list, axis=1),
-        jnp.concatenate(key_list, axis=1),
-        jnp.concatenate(value_list, axis=1),
+        query_grad.astype(jnp.bfloat16).reshape(query_count, HEADS * HD),
+        key_grad.reshape(key_count, HEADS * HD),
+        value_grad.reshape(key_count, HEADS * HD),
     )
 
 
@@ -202,10 +186,6 @@
 
 def to_space(frame_rows):
     return lax.all_to_all(frame_rows, "frame", split_axis=0, concat_axis=1, tiled=True)[0]
-
-
-def rim(first_part, second_part, width):
-    return (padded(first_part, (("space", 0),), width), padded(second_part, (("space", 0),), width))
 
 
 def local(frames_in, cotangent, w_qkv_space, w_out_space, w_qkv_time, w_out_time, neighbours):
@@ -230,9 +210,9 @@
         jnp.bfloat16
     )
     queries = projected[:, :feature_count]
-    key_window, value_window = rim(
-        projected[:, feature_count : 2 * feature_count], projected[:, 2 * feature_count :], shard
-    )
+    kv_window = padded(projected[:, feature_count:], (("space", 0),), shard)
+    key_window = kv_window[:, :feature_count]
+    value_window = kv_window[:, feature_count:]
     attended, totals = space_attend(queries, key_window, value_window, allowed)
     update = jnp.dot(attended, full_out_space, preferred_element_type=jnp.float32)
     stream = (local_in.astype(jnp.float32) + update).astype(jnp.bfloat16)
@@ -240,22 +220,23 @@
     projected_time = jnp.dot(normed_time, full_qkv_time, preferred_element_type=jnp.float32).astype(
         jnp.bfloat16
     )
-    time_rows = to_frames(projected_time)
+    grad_att_time = jnp.dot(grad_out, full_out_time.T, preferred_element_type=jnp.float32).astype(
+        jnp.bfloat16
+    )
+    time_rows = to_frames(jnp.concatenate([projected_time, grad_att_time], axis=1))
     query_time = time_rows[..., :feature_count]
     key_time = time_rows[..., feature_count : 2 * feature_count]
-    value_time = time_rows[..., 2 * feature_count :]
+    value_time = time_rows[..., 2 * feature_count : 3 * feature_count]
+    grad_time_rows = time_rows[..., 3 * feature_count :]
     attended_time, totals_time = time_attend(query_time, key_time, value_time)
-    attended_back = to_space(attended_time)
+    gradients = time_back(
+        query_time, key_time, value_time, attended_time, grad_time_rows, totals_time
+    )
+    back_rows = to_space(jnp.concatenate([attended_time, gradients], axis=-1))
+    attended_back = back_rows[:, :feature_count]
+    grad_project_time = back_rows[:, feature_count:]
     update_time = jnp.dot(attended_back, full_out_time, preferred_element_type=jnp.float32)
     frames_out = (stream.astype(jnp.float32) + update_time).astype(jnp.bfloat16)
-    grad_att_time = jnp.dot(grad_out, full_out_time.T, preferred_element_type=jnp.float32).astype(
-        jnp.bfloat16
-    )
-    grad_time_rows = to_frames(grad_att_time)
-    gradients = time_back(
-        query_time, key_time, value_time, attended_time, grad_time_rows, totals_time
-    )
-    grad_project_time = to_space(gradients)
     grad_normed_time = jnp.dot(
         grad_project_time, full_qkv_time.T, preferred_element_type=jnp.float32
     )
@@ -268,24 +249,17 @@
     grad_query, key_partial, value_partial = space_back(
         queries, key_window, value_window, allowed, totals, attended, grad_attended
     )
-    key_send = jnp.concatenate([key_partial[:shard], key_partial[2 * shard :]], axis=0).astype(
-        jnp.bfloat16
-    )
-    value_send = jnp.concatenate(
-        [value_partial[:shard], value_partial[2 * shard :]], axis=0
+    kv_partial = jnp.concatenate([key_partial, value_partial], axis=1)
+    kv_send = jnp.concatenate([kv_partial[:shard], kv_partial[2 * shard :]], axis=0).astype(
+        jnp.bfloat16
+    )
+    kv_got = padded(kv_send, (("space", 0),), shard)
+    grad_kv = (
+        kv_partial[shard : 2 * shard]
+        + kv_got[:shard].astype(jnp.float32)
+        + kv_got[3 * shard :].astype(jnp.float32)
     ).astype(jnp.bfloat16)
-    key_got, value_got = rim(key_send, value_send, shard)
-    grad_key = (
-        key_partial[shard : 2 * shard]
-        + key_got[:shard].astype(jnp.float32)
-        + key_got[3 * shard :].astype(jnp.float32)
-    ).astype(jnp.bfloat16)
-    grad_value = (
-        value_partial[shard : 2 * shard]
-        + value_got[:shard].astype(jnp.float32)
-        + value_got[3 * shard :].astype(jnp.float32)
-    ).astype(jnp.bfloat16)
-    grad_project = jnp.concatenate([grad_query, grad_key, grad_value], axis=1)
+    grad_project = jnp.concatenate([grad_query, grad_kv], axis=1)
     grad_normed = jnp.dot(grad_project, full_qkv_space.T, preferred_element_type=jnp.float32)
     grad_in = (grad_stream.astype(jnp.float32) + rms_back(local_in, grad_normed)).astype(
         jnp.bfloat16

time: 303 us -> 263 us (0.87); the launches traced: 298 us -> 262 us
  starting transfers between devices: 49.6 us -> 18.7 us
  blocking collectives: 0 us -> 23.6 us
  matrix products: 52 us -> 31.5 us
  local copies, waits for them, and re-layouts: 17.4 us -> 11.1 us
    all_to_all x0 -> x1, blocking collectives: none -> 23.6 us  [to_space(): lax.all_to_all(frame_rows, 'frame', split_axis=0, concat_axis=1, tiled=True)]
    all_to_all x2 -> x0, waiting for transfers between devices: 17 us -> none  [to_space(): lax.all_to_all(frame_rows, 'frame', split_axis=0, concat_axis=1, tiled=True)]
    ppermute x4 -> x2, starting transfers between devices: 19.9 us -> 5.25 us  [padded(): lax.ppermute(tail, axis, [(i, (i + 1) % count) for i in range(ends)])]
    dot_general x36 -> x6, matrix products: 17 us -> 5.93 us  [the longest x1 2.5 us: space_back(): jnp.einsum('gst,sgh->tgh', probability, grad_heads, preferred_element_typ...]
    all_to_all x2 -> x1, waiting for transfers between devices: 11.6 us -> 21 us  [to_frames(): lax.all_to_all(local_rows[None], 'frame', split_axis=1, concat_axis=0, ti...]
    all_to_all x2 -> x1, starting transfers between devices: 13.9 us -> 6.74 us  [to_frames(): lax.all_to_all(local_rows[None], 'frame', split_axis=1, concat_axis=0, ti...]
    all_to_all x2 -> x0, starting transfers between devices: 7.19 us -> none  [to_space(): lax.all_to_all(frame_rows, 'frame', split_axis=0, concat_axis=1, tiled=True)]
    ppermute x4 -> x2, waiting for transfers between devices: 1.16 us -> 6.44 us  [padded(): lax.ppermute(tail, axis, [(i, (i + 1) % count) for i in range(ends)])]
  transfers between devices with their start and end apart: 13 -> 6, of which waited for: 6 -> 6; matrix products, arithmetic and copies ran while one was open for 12% -> 2% of each run, Pallas kernels for 0% -> 0%
where the time goes in v2:
time: 263 us; the launch traced here: 262 us
  waiting for transfers between devices  150 us (57%)
  matrix products  31.5 us (12%)
  blocking collectives  23.6 us (9%)
  starting transfers between devices  18.7 us (7%)
  between operations  14.7 us (6%)
  other arithmetic  12.7 us (5%)
  local copies, waits for them, and re-layouts  11.1 us (4%)
    all_gather x1, waiting for transfers between devices, local(): all_weights = lax.all_gather(weight_rows, 'space', axis=0, tiled=True)  113 us
    all_to_all x1, blocking collectives, to_space(): lax.all_to_all(frame_rows, 'frame', split_axis=0, concat_axis=1, tiled=True)  23.6 us
    all_to_all x1, waiting for transfers between devices, to_frames(): lax.all_to_all(local_rows[None], 'frame', split_axis=1, concat_axis=0, ti...  21 us
    ppermute x2, waiting for transfers between devices, padded(): lax.ppermute(head, axis, [((i + 1) % count, i) for i in range(ends)])  8.98 us
    all_to_all x1, starting transfers between devices, to_frames(): lax.all_to_all(local_rows[None], 'frame', split_axis=1, concat_axis=0, ti...  6.74 us
    ppermute x2, starting transfers between devices, padded(): lax.ppermute(head, axis, [((i + 1) % count, i) for i in range(ends)])  6.69 us
    ppermute x2, waiting for transfers between devices, padded(): lax.ppermute(tail, axis, [(i, (i + 1) % count) for i in range(ends)])  6.44 us
    unnamed x3, other arithmetic  6.4 us
  transfers between devices with their start and end apart: 6, of which 6 were waited for; matrix products, arithmetic and copies ran while one was open for 2% of the time, Pallas kernels for 0%

profile of v2, /device:TPU:6, one launch (start us, length us, event | category | flops | bytes accessed | tf_op | source)
XLA Modules:
  0.0 262.0 jit_solution(16806980639411938792)
XLA Ops:
  7.2 1.7 pad_maximum_fusion.3
  9.0 0.2 dynamic-slice_reduce_fusion
  9.3 1.0 fusion.39
  10.3 113.3 %all-gather.2.cloned.1.call-done = bf16[768,6144]{1,0:T(8,128)(2,1)} async-done(((bf16[24,6144]{1,0:T(8,128)(2,1)}), bf16[768,6144]{1,0:T(8,128)(2,1)}) %all-gather.2.cloned.1.call-update) | async-done | bytes 9437200 | tf_op jit(solution)/shard_map/all_gather | solution.py:196
  123.7 2.8 %convolution_convert_fusion.1 = bf16[128,2304]{1,0:T(8,128)(2,1)S(1)} fusion(bf16[768,6144]{1,0:T(8,128)(2,1)} %all-gather.2.cloned.1.call-done, bf16[1,128,768]{2,1,0:T(8,128)(2,1)} %param.7, f32[128]{0:T(128)S(1)} %get-tuple-element.11), kind=kOutput, calls=%fused_computation.1 | convolution fusion | flops 453574656 | bytes 4325888 | tf_op jit(solution)/shard_map/dot_general | solution.py:209
  126.6 3.1 %collective-permute-start = (bf16[128,1536]{1,0:T(8,128)(2,1)S(1)}, bf16[128,1536]{1,0:T(8,128)(2,1)S(1)}, u32[]{:S(2)}, u32[]{:S(2)}) collective-permute-start(bf16[128,1536]{1,0:T(8,128)(2,1)S(1)} %slice.73), channel_id=1, source_target_pairs={{0,2},{2,4},{4,6},{6,8},{8,10},{10,12},{12,14},{14,16},{16,18},{18... | collective-permute-start | bytes 1179656 | tf_op jit(solution)/shard_map/ppermute | solution.py:22
  129.7 2.8 %collective-permute-start.1 = (bf16[128,1536]{1,0:T(8,128)(2,1)S(1)}, bf16[128,1536]{1,0:T(8,128)(2,1)S(1)}, u32[]{:S(2)}, u32[]{:S(2)}) collective-permute-start(bf16[128,1536]{1,0:T(8,128)(2,1)S(1)} %slice.73), channel_id=1, source_target_pairs={{2,0},{4,2},{6,4},{8,6},{10,8},{12,10},{14,12},{16,14},{18,16},{20... | collective-permute-start | bytes 1179656 | tf_op jit(solution)/shard_map/ppermute | solution.py:24
  132.5 0.2 copy.84
  132.7 1.9 fusion.22
  134.6 4.3 %collective-permute-done = bf16[128,1536]{1,0:T(8,128)(2,1)S(1)} collective-permute-done((bf16[128,1536]{1,0:T(8,128)(2,1)S(1)}, bf16[128,1536]{1,0:T(8,128)(2,1)S(1)}, u32[]{:S(2)}, u32[]{:S(2)}) %collective-permute-start) | collective-permute-done | bytes 393248 | tf_op jit(solution)/shard_map/ppermute | solution.py:22
  138.9 4.9 %collective-permute-done.1 = bf16[128,1536]{1,0:T(8,128)(2,1)S(1)} collective-permute-done((bf16[128,1536]{1,0:T(8,128)(2,1)S(1)}, bf16[128,1536]{1,0:T(8,128)(2,1)S(1)}, u32[]{:S(2)}, u32[]{:S(2)}) %collective-permute-start.1) | collective-permute-done | bytes 393248 | tf_op jit(solution)/shard_map/ppermute | solution.py:24
  144.0 0.3 copy.85
  144.3 0.3 copy.83
  144.7 0.7 fusion.8
  145.4 0.7 convolution_convert_fusion.6
  146.2 0.6 copy-done.18
  146.8 0.7 copy-done.5
  147.5 1.7 multiply_reduce_fusion.2
  149.2 2.7 %convolution_convert_fusion = bf16[128,2304]{1,0:T(8,128)(2,1)S(1)} fusion(bf16[768,6144]{1,0:T(8,128)(2,1)} %all-gather.2.cloned.1.call-done, f32[128,768]{1,0:T(8,128)S(1)} %get-tuple-element.17, f32[128]{0:T(128)S(1)} %get-tuple-element.13), kind=kOutput, calls=%fused_computation | convolution fusion | flops 453476352 | bytes 4522496 | tf_op jit(solution)/shard_map/dot_general | solution.py:220
  152.0 1.2 copy.144
  153.2 0.5 broadcast.162
  153.8 5.3 %reduce.7 = bf16[128,3072]{1,0:T(8,128)(2,1)S(1)} reduce(bf16[128,1,3072]{2,1,0:T(2,128)(2,1)S(1)} %bitcast.84, bf16[]{:T(256)} %broadcast.162), dimensions={1}, to_apply=%bitcast.81.reduce_sub_computation | reduce | bytes 1572866
  159.1 1.5 reshape.194
  160.5 6.7 %all-to-all-start = ((bf16[8,2,24576]{2,1,0:T(2,128)(2,1)}), bf16[8,2,24576]{2,1,0:T(2,128)(2,1)S(1)}, u32[]{:S(2)}, u32[]{:S(2)}) async-start(bf16[8,2,24576]{2,1,0:T(2,128)(2,1)} %reshape.194), calls=%async_computation | async-start | bytes 1572864 | tf_op jit(solution)/shard_map/all_to_all | solution.py:184
  167.3 0.6 iota_compare_fusion
  167.9 21.0 %all-to-all-done = bf16[8,2,24576]{2,1,0:T(2,128)(2,1)S(1)} async-done(((bf16[8,2,24576]{2,1,0:T(2,128)(2,1)}), bf16[8,2,24576]{2,1,0:T(2,128)(2,1)S(1)}, u32[]{:S(2)}, u32[]{:S(2)}) %all-to-all-start) | async-done | bytes 786464 | tf_op jit(solution)/shard_map/all_to_all | solution.py:184
  188.9 0.8 reshape.195
  189.7 0.2 copy.123
  190.0 0.3 reshape.175
  190.3 0.3 reshape.176
  190.7 0.3 reshape.178
  191.0 1.1 bitcast_convert_fusion
  192.1 0.3 reshape.174
  192.4 0.6 fusion.10
  193.0 1.0 copy-done.20
  194.0 1.1 fusion.48
  195.1 3.6 %multiply_reduce_fusion = (f32[16,12,8]{2,1,0:T(8,128)S(1)}, bf16[16,12,64,8]{2,3,1,0:T(8,128)(2,1)}) fusion(f32[16,12,8,64]{3,1,0,2:T(8,128)} %bitcast_convert_fusion, f32[16,12,8,8]{2,3,1,0:T(8,128)} %copy-done.20, bf16[8,16,12,64]{3,2,1,0:T(8,128)(2,1)S(1)} %reshape.174), kind=kOutput, calls=%fused_computation.59 | convolution fusion | flops 1990663 | bytes 841728 | tf_op jit(solution)/shard_map/phfg,gphd->fphd/dot_general | solution.py:129
  198.7 1.7 fusion.12
  200.4 1.2 fusion.17
  201.6 0.4 fusion.16
  202.1 1.3 fusion.15
  203.4 0.3 reshape.179
  203.8 0.3 reshape.180
  204.1 0.2 copy-done.9
  204.4 0.3 reshape.177
  204.8 0.3 reshape.181
  205.2 23.6 %all_to_all.21 = bf16[8,16,3072]{2,1,0:T(8,128)(2,1)S(1)} all-to-all(bf16[8,16,3072]{2,1,0:T(8,128)(2,1)S(1)} %pad_maximum_fusion.2), channel_id=1, replica_groups=mesh['frame'=8,'space'=32,'dp'=2] {'frame'}, dimensions={0} | all-to-all | bytes 1572864 | tf_op jit(solution)/shard_map/all_to_all | solution.py:188
  228.8 3.4 %multiply_reduce_fusion.1 = (f32[128]{0:T(128)S(1)}, f32[128,768]{1,0:T(8,128)S(1)}) fusion(f32[128,768]{1,0:T(8,128)S(1)} %get-tuple-element.17, bf16[768,6144]{1,0:T(8,128)(2,1)} %all-gather.2.cloned.1.call-done, bf16[128,3072]{1,0:T(8,128)(2,1)S(1)} %bitcast.91), kind=kOutput, calls=%fused_computation.78 | convolution fusion | flops 453181312 | bytes 4915712 | tf_op jit(solution)/shard_map/dot_general | solution.py:240
  232.2 0.2 add_convert_fusion
  232.4 1.8 convolution_convert_fusion.4
  234.2 0.2 copy.103
  234.4 2.5 fusion.36
  237.1 1.0 multiply_convert_fusion
  238.1 0.4 convolution_multiply_fusion
  238.5 0.1 fusion.6
  238.7 2.2 collective-permute-start.2
  240.8 3.9 %collective-permute-start.3 = (bf16[128,1536]{0,1:T(8,128)(2,1)S(1)}, bf16[128,1536]{0,1:T(8,128)(2,1)S(1)}, u32[]{:S(2)}, u32[]{:S(2)}) collective-permute-start(bf16[128,1536]{0,1:T(8,128)(2,1)S(1)} %get-tuple-element.3), channel_id=1, source_target_pairs={{2,0},{4,2},{6,4},{8,6},{10,8},{12,10},{14,12},{16,14},{18,16},{20... | collective-permute-start | bytes 1179656 | tf_op jit(solution)/shard_map/ppermute | solution.py:24
  244.8 1.0 fusion.23
  245.8 0.6 fusion.18
  246.5 2.1 collective-permute-done.2
  248.6 4.0 %collective-permute-done.3 = bf16[128,1536]{0,1:T(8,128)(2,1)S(1)} collective-permute-done((bf16[128,1536]{0,1:T(8,128)(2,1)S(1)}, bf16[128,1536]{0,1:T(8,128)(2,1)S(1)}, u32[]{:S(2)}, u32[]{:S(2)}) %collective-permute-start.3) | collective-permute-done | bytes 393248 | tf_op jit(solution)/shard_map/ppermute | solution.py:24
  252.6 0.2 fusion.31
  252.8 1.4 fusion.45
  254.3 0.9 fusion.57
  (73 shorter events, 1.3 us)
Async XLA Ops:
  7.2 1.8 copy-start
  7.2 116.5 %all-gather.2.cloned.1.call-start = ((), (), s32[]{:S(2)}) async-start(), calls=%async_computation.2 | async-start | bytes 9732096 | tf_op jit(solution)/shard_map/all_gather | solution.py:196
  10.3 116.2 %copy-start.13 = (f32[128]{0:T(128)}, f32[128]{0:T(128)S(1)}, u32[]{:S(2)}) copy-start(f32[128]{0:T(128)S(1)} %get-tuple-element.11) | copy-start | bytes 1540
  123.7 9.0 %copy-start.11 = (bf16[1,128,768]{2,1,0:T(8,128)(2,1)S(1)}, bf16[1,128,768]{2,1,0:T(8,128)(2,1)}, u32[]{:S(2)}) copy-start(bf16[1,128,768]{2,1,0:T(8,128)(2,1)} %param.8) | copy-start | bytes 589828
  126.6 12.3 %collective-permute-start = (bf16[128,1536]{1,0:T(8,128)(2,1)S(1)}, bf16[128,1536]{1,0:T(8,128)(2,1)S(1)}, u32[]{:S(2)}, u32[]{:S(2)}) collective-permute-start(bf16[128,1536]{1,0:T(8,128)(2,1)S(1)} %slice.73), channel_id=1, source_target_pairs={{0,2},{2,4},{4,6},{6,8},{8,10},{10,12},{12,14},{14,16},{16,18},{18... | collective-permute-start | bytes 1179656 | tf_op jit(solution)/shard_map/ppermute | solution.py:22
  129.7 14.2 %collective-permute-start.1 = (bf16[128,1536]{1,0:T(8,128)(2,1)S(1)}, bf16[128,1536]{1,0:T(8,128)(2,1)S(1)}, u32[]{:S(2)}, u32[]{:S(2)}) collective-permute-start(bf16[128,1536]{1,0:T(8,128)(2,1)S(1)} %slice.73), channel_id=1, source_target_pairs={{2,0},{4,2},{6,4},{8,6},{10,8},{12,10},{14,12},{16,14},{18,16},{20... | collective-permute-start | bytes 1179656 | tf_op jit(solution)/shard_map/ppermute | solution.py:24
  132.5 12.9 %copy-start.16 = (pred[384]{0:T(512)(128)(4,1)}, pred[384]{0:T(512)(128)(4,1)S(1)}, u32[]{:S(2)}) copy-start(pred[384]{0:T(512)(128)(4,1)S(1)} %broadcast_bitcast_fusion) | copy-start | bytes 1156
  132.7 12.0 %copy-start.3 = (bf16[128,768]{0,1:T(8,128)(2,1)}, bf16[128,768]{0,1:T(8,128)(2,1)S(1)}, u32[]{:S(2)}) copy-start(bf16[128,768]{0,1:T(8,128)(2,1)S(1)} %copy.84) | copy-start | bytes 589828
  144.6 1.5 copy-start.7
  145.4 1.4 copy-start.18
  145.4 1.4 copy-start.22
  145.4 2.1 copy-start.1
  146.8 0.7 copy-start.5
  160.5 28.3 %all-to-all-start = ((bf16[8,2,24576]{2,1,0:T(2,128)(2,1)}), bf16[8,2,24576]{2,1,0:T(2,128)(2,1)S(1)}, u32[]{:S(2)}, u32[]{:S(2)}) async-start(bf16[8,2,24576]{2,1,0:T(2,128)(2,1)} %reshape.194), calls=%async_computation | async-start | bytes 1572864 | tf_op jit(solution)/shard_map/all_to_all | solution.py:184
  190.0 2.4 copy-start.15
  193.0 1.0 copy-start.20
  200.4 1.6 copy-start.21
  202.0 1.3 copy-start.2
  203.3 1.0 copy-start.9
  203.4 1.3 copy-start.10
  228.7 3.5 %copy-start.12 = (bf16[1,128,768]{2,1,0:T(8,128)(2,1)S(1)}, bf16[1,128,768]{2,1,0:T(8,128)(2,1)}, u32[]{:S(2)}) copy-start(bf16[1,128,768]{2,1,0:T(8,128)(2,1)} %param.8) | copy-start | bytes 589828
  232.2 2.2 copy-start.17
  232.2 2.2 copy-start.23
  234.4 2.5 copy-start.6
  234.4 2.6 copy-start.8
  234.4 2.6 %copy-start.19 = (f32[12,128,384]{2,1,0:T(8,128)S(1)}, f32[12,128,384]{2,1,0:T(8,128)}, u32[]{:S(2)}) copy-start(f32[12,128,384]{2,1,0:T(8,128)} %copy-done.18) | copy-start | bytes 7077892
  237.1 1.0 copy-start.4
  237.1 7.7 %slice-start = ((s8[9437184]{0:T(1024)(128)(4,1)}), s8[4194304]{0:T(1024)(128)(4,1)S(1)}, s32[]{:S(2)}) async-start(s8[9437184]{0:T(1024)(128)(4,1)} %bitcast.99), calls=%async_computation.3 | async-start | bytes 8388608
  237.1 7.7 %slice-start.1 = ((s8[9437184]{0:T(1024)(128)(4,1)}), s8[4194304]{0:T(1024)(128)(4,1)S(1)}, s32[]{:S(2)}) async-start(s8[9437184]{0:T(1024)(128)(4,1)} %bitcast.99), calls=%async_computation.4 | async-start | bytes 8388608
  238.1 6.7 %slice-start.2 = ((s8[9437184]{0:T(1024)(128)(4,1)}), s8[1048576]{0:T(1024)(128)(4,1)S(1)}, s32[]{:S(2)}) async-start(s8[9437184]{0:T(1024)(128)(4,1)} %bitcast.99), calls=%async_computation.5 | async-start | bytes 2097152
  238.7 9.9 %collective-permute-start.2 = (bf16[128,1536]{0,1:T(8,128)(2,1)S(1)}, bf16[128,1536]{0,1:T(8,128)(2,1)S(1)}, u32[]{:S(2)}, u32[]{:S(2)}) collective-permute-start(bf16[128,1536]{0,1:T(8,128)(2,1)S(1)} %get-tuple-element.2), channel_id=1, source_target_pairs={{0,2},{2,4},{4,6},{6,8},{8,10},{10,12},{12,14},{14,16},{16,18},{18... | collective-permute-start | bytes 1179656 | tf_op jit(solution)/shard_map/ppermute | solution.py:22
  240.8 11.8 %collective-permute-start.3 = (bf16[128,1536]{0,1:T(8,128)(2,1)S(1)}, bf16[128,1536]{0,1:T(8,128)(2,1)S(1)}, u32[]{:S(2)}, u32[]{:S(2)}) collective-permute-start(bf16[128,1536]{0,1:T(8,128)(2,1)S(1)} %get-tuple-element.3), channel_id=1, source_target_pairs={{2,0},{4,2},{6,4},{8,6},{10,8},{12,10},{14,12},{16,14},{18,16},{20... | collective-permute-start | bytes 1179656 | tf_op jit(solution)/shard_map/ppermute | solution.py:24
  252.8 1.4 copy-start.14
Sparse Core Ops, SparseCore 0:
  11.2 112.4 all-gather.1

commit v3 on v2

--- a/solution.py
+++ b/solution.py
@@ -205,44 +205,45 @@
     space_index = lax.axis_index("space")
     lists_here = lax.dynamic_slice_in_dim(neighbours, space_index * block_count, block_count, 0)
     allowed = block_mask(lists_here, (space_index - 1) * block_count)
-    normed_space = rms_norm(local_in)
-    projected = jnp.dot(normed_space, full_qkv_space, preferred_element_type=jnp.float32).astype(
-        jnp.bfloat16
-    )
-    queries = projected[:, :feature_count]
-    kv_window = padded(projected[:, feature_count:], (("space", 0),), shard)
+    input_window = padded(local_in, (("space", 0),), shard)
+    cot_rows = to_frames(grad_out)
+    normed_window = rms_norm(input_window)
+    normed_space = normed_window[shard : 2 * shard]
+    queries = jnp.dot(
+        normed_space, full_qkv_space[:, :feature_count], preferred_element_type=jnp.float32
+    ).astype(jnp.bfloat16)
+    kv_window = jnp.dot(
+        normed_window, full_qkv_space[:, feature_count:], preferred_element_type=jnp.float32
+    ).astype(jnp.bfloat16)
     key_window = kv_window[:, :feature_count]
     value_window = kv_window[:, feature_count:]
     attended, totals = space_attend(queries, key_window, value_window, allowed)
     update = jnp.dot(attended, full_out_space, preferred_element_type=jnp.float32)
     stream = (local_in.astype(jnp.float32) + update).astype(jnp.bfloat16)
-    normed_time = rms_norm(stream)
+    stream_rows = to_frames(stream)
+    normed_time = rms_norm(stream_rows)
     projected_time = jnp.dot(normed_time, full_qkv_time, preferred_element_type=jnp.float32).astype(
         jnp.bfloat16
     )
-    grad_att_time = jnp.dot(grad_out, full_out_time.T, preferred_element_type=jnp.float32).astype(
-        jnp.bfloat16
-    )
-    time_rows = to_frames(jnp.concatenate([projected_time, grad_att_time], axis=1))
-    query_time = time_rows[..., :feature_count]
-    key_time = time_rows[..., feature_count : 2 * feature_count]
-    value_time = time_rows[..., 2 * feature_count : 3 * feature_count]
-    grad_time_rows = time_rows[..., 3 * feature_count :]
+    query_time = projected_time[..., :feature_count]
+    key_time = projected_time[..., feature_count : 2 * feature_count]
+    value_time = projected_time[..., 2 * feature_count :]
     attended_time, totals_time = time_attend(query_time, key_time, value_time)
+    update_time = jnp.dot(attended_time, full_out_time, preferred_element_type=jnp.float32)
+    frames_out_rows = (stream_rows.astype(jnp.float32) + update_time).astype(jnp.bfloat16)
+    grad_att_time = jnp.dot(cot_rows, full_out_time.T, preferred_element_type=jnp.float32).astype(
+        jnp.bfloat16
+    )
     gradients = time_back(
-        query_time, key_time, value_time, attended_time, grad_time_rows, totals_time
-    )
-    back_rows = to_space(jnp.concatenate([attended_time, gradients], axis=-1))
-    attended_back = back_rows[:, :feature_count]
-    grad_project_time = back_rows[:, feature_count:]
-    update_time = jnp.dot(attended_back, full_out_time, preferred_element_type=jnp.float32)
-    frames_out = (stream.astype(jnp.float32) + update_time).astype(jnp.bfloat16)
-    grad_normed_time = jnp.dot(
-        grad_project_time, full_qkv_time.T, preferred_element_type=jnp.float32
-    )
-    grad_stream = (grad_out.astype(jnp.float32) + rms_back(stream, grad_normed_time)).astype(
-        jnp.bfloat16
-    )
+        query_time, key_time, value_time, attended_time, grad_att_time, totals_time
+    )
+    grad_normed_time = jnp.dot(gradients, full_qkv_time.T, preferred_element_type=jnp.float32)
+    grad_stream_rows = (
+        cot_rows.astype(jnp.float32) + rms_back(stream_rows, grad_normed_time)
+    ).astype(jnp.bfloat16)
+    back_rows = to_space(jnp.concatenate([frames_out_rows, grad_stream_rows], axis=-1))
+    frames_out = back_rows[:, :feature_count]
+    grad_stream = back_rows[:, feature_count:]
     grad_attended = jnp.dot(
         grad_stream, full_out_space.T, preferred_element_type=jnp.float32
     ).astype(jnp.bfloat16)

time: 263 us -> 229 us (0.87)
  waiting for transfers between devices: 150 us -> 109 us
  starting transfers between devices: 18.7 us -> 27.7 us
  blocking collectives: 23.6 us -> 15.4 us
  matrix products: 31.5 us -> 37.6 us
    all_gather x1, waiting for transfers between devices: 113 us -> 85.1 us  [local(): all_weights = lax.all_gather(weight_rows, 'space', axis=0, tiled=True)]
    all_to_all x1, blocking collectives: 23.6 us -> 15.4 us  [to_space(): lax.all_to_all(frame_rows, 'frame', split_axis=0, concat_axis=1, tiled=True)]
    all_to_all x1 -> x2, starting transfers between devices: 6.74 us -> 13.8 us  [to_frames(): lax.all_to_all(local_rows[None], 'frame', split_axis=1, concat_axis=0, ti...]
    all_to_all x1 -> x2, waiting for transfers between devices: 21 us -> 16 us  [to_frames(): lax.all_to_all(local_rows[None], 'frame', split_axis=1, concat_axis=0, ti...]
    ppermute x2, waiting for transfers between devices: 6.44 us -> 2.48 us  [padded(): lax.ppermute(tail, axis, [(i, (i + 1) % count) for i in range(ends)])]
    ppermute x2, waiting for transfers between devices: 8.98 us -> 5.23 us  [padded(): lax.ppermute(head, axis, [((i + 1) % count, i) for i in range(ends)])]
    ppermute x2, starting transfers between devices: 5.25 us -> 8.33 us  [padded(): lax.ppermute(tail, axis, [(i, (i + 1) % count) for i in range(ends)])]
    dot_general x4 -> x5, matrix products: 9.15 us -> 11.2 us  [the longest x1 3.42 us: local(): jnp.dot(gradients, full_qkv_time.T, preferred_element_type=jnp.float32)]
  transfers between devices with their start and end apart: 6 -> 7, of which waited for: 6 -> 5; matrix products, arithmetic and copies ran while one was open for 2% -> 4% of each run, Pallas kernels for 0% -> 0%
where the time goes in v3:
time: 229 us; the launch traced here: 228 us
  waiting for transfers between devices  109 us (48%)
  matrix products  37.6 us (16%)
  starting transfers between devices  27.7 us (12%)
  blocking collectives  15.4 us (7%)
  between operations  14.5 us (6%)
  local copies, waits for them, and re-layouts  12 us (5%)
  other arithmetic  12 us (5%)
    all_gather x1, waiting for transfers between devices, local(): all_weights = lax.all_gather(weight_rows, 'space', axis=0, tiled=True)  85.1 us
    all_to_all x2, waiting for transfers between devices, to_frames(): lax.all_to_all(local_rows[None], 'frame', split_axis=1, concat_axis=0, ti...  16 us
    all_to_all x1, blocking collectives, to_space(): lax.all_to_all(frame_rows, 'frame', split_axis=0, concat_axis=1, tiled=True)  15.4 us
    all_to_all x2, starting transfers between devices, to_frames(): lax.all_to_all(local_rows[None], 'frame', split_axis=1, concat_axis=0, ti...  13.8 us
    ppermute x2, starting transfers between devices, padded(): lax.ppermute(tail, axis, [(i, (i + 1) % count) for i in range(ends)])  8.33 us
    ppermute x2, starting transfers between devices, padded(): lax.ppermute(head, axis, [((i + 1) % count, i) for i in range(ends)])  5.47 us
    ppermute x2, waiting for transfers between devices, padded(): lax.ppermute(head, axis, [((i + 1) % count, i) for i in range(ends)])  5.23 us
    unnamed x32, local copies, waits for them, and re-layouts  5.1 us
  transfers between devices with their start and end apart: 7, of which 5 were waited for; matrix products, arithmetic and copies ran while one was open for 4% of the time, Pallas kernels for 0%

profile of v3, /device:TPU:6, one launch (start us, length us, event | category | flops | bytes accessed | tf_op | source)
XLA Modules:
  0.0 228.1 jit_solution(8160856804556990980)
XLA Ops:
  7.2 1.8 pad_maximum_fusion.3
  9.0 2.7 %collective-permute-start.1 = (bf16[128,768]{1,0:T(8,128)(2,1)}, bf16[128,768]{1,0:T(8,128)(2,1)S(1)}, u32[]{:S(2)}, u32[]{:S(2)}) collective-permute-start(bf16[128,768]{1,0:T(8,128)(2,1)} %bitcast.100), channel_id=1, source_target_pairs={{2,0},{4,2},{6,4},{8,6},{10,8},{12,10},{14,12},{16,14},{18,16},{20... | collective-permute-start | bytes 589832 | tf_op jit(solution)/shard_map/ppermute | solution.py:24
  11.8 5.2 %collective-permute-start = (bf16[128,768]{1,0:T(8,128)(2,1)}, bf16[128,768]{1,0:T(8,128)(2,1)S(1)}, u32[]{:S(2)}, u32[]{:S(2)}) collective-permute-start(bf16[128,768]{1,0:T(8,128)(2,1)} %bitcast.101), channel_id=1, source_target_pairs={{0,2},{2,4},{4,6},{6,8},{8,10},{10,12},{12,14},{14,16},{16,18},{18... | collective-permute-start | bytes 589832 | tf_op jit(solution)/shard_map/ppermute | solution.py:22
  17.0 1.2 copy.151
  18.2 0.6 broadcast.177
  18.8 1.8 reduce.9
  20.6 0.7 reshape.215
  21.4 7.1 %all-to-all-start.1 = ((bf16[8,2,6144]{2,1,0:T(2,128)(2,1)}), bf16[8,2,6144]{2,1,0:T(2,128)(2,1)S(1)}, u32[]{:S(2)}, u32[]{:S(2)}) async-start(bf16[8,2,6144]{2,1,0:T(2,128)(2,1)} %reshape.215), calls=%async_computation.1 | async-start | bytes 393216 | tf_op jit(solution)/shard_map/all_to_all | solution.py:184
  28.5 0.2 dynamic-slice_reduce_fusion
  28.8 0.2 fusion.16
  29.2 9.1 %all-to-all-done.1 = bf16[8,2,6144]{2,1,0:T(2,128)(2,1)S(1)} async-done(((bf16[8,2,6144]{2,1,0:T(2,128)(2,1)}), bf16[8,2,6144]{2,1,0:T(2,128)(2,1)S(1)}, u32[]{:S(2)}, u32[]{:S(2)}) %all-to-all-start.1) | async-done | bytes 196640 | tf_op jit(solution)/shard_map/all_to_all | solution.py:184
  38.4 0.2 reshape.216
  38.6 85.1 %all-gather.2.cloned.1.call-done = bf16[768,6144]{1,0:T(8,128)(2,1)} async-done(((bf16[24,6144]{1,0:T(8,128)(2,1)}), bf16[768,6144]{1,0:T(8,128)(2,1)}) %all-gather.2.cloned.1.call-update) | async-done | bytes 9437200 | tf_op jit(solution)/shard_map/all_gather | solution.py:196
  123.7 1.6 fusion.21
  125.5 2.7 %convolution_convert_fusion.1 = bf16[384,1536]{1,0:T(8,128)(2,1)S(1)} fusion(bf16[384,768]{1,0:T(8,128)(2,1)S(1)} %fusion.17, bf16[768,6144]{1,0:T(8,128)(2,1)} %all-gather.2.cloned.1.call-done), kind=kOutput, calls=%fused_computation.7 | convolution fusion | flops 906559488 | bytes 4128768 | tf_op jit(solution)/shard_map/dot_general | solution.py:215
  128.3 0.3 copy.91
  128.6 0.3 copy.89
  128.9 0.7 fusion.6
  129.7 0.7 convolution_convert_fusion.6
  130.4 0.6 copy-done.10
  131.1 0.7 copy-done.2
  131.7 1.6 fusion.27
  133.4 0.3 copy.152
  133.7 1.8 reduce.8
  135.5 0.7 reshape.213
  136.2 6.7 %all-to-all-start = ((bf16[8,2,6144]{2,1,0:T(2,128)(2,1)}), bf16[8,2,6144]{2,1,0:T(2,128)(2,1)S(1)}, u32[]{:S(2)}, u32[]{:S(2)}) async-start(bf16[8,2,6144]{2,1,0:T(2,128)(2,1)} %reshape.213), calls=%async_computation | async-start | bytes 393216 | tf_op jit(solution)/shard_map/all_to_all | solution.py:184
  143.0 1.8 fusion.26
  144.8 0.3 reshape.195
  145.1 1.1 bitcast_convert_fusion
  146.2 6.8 %all-to-all-done = bf16[8,2,6144]{2,1,0:T(2,128)(2,1)S(1)} async-done(((bf16[8,2,6144]{2,1,0:T(2,128)(2,1)}), bf16[8,2,6144]{2,1,0:T(2,128)(2,1)S(1)}, u32[]{:S(2)}, u32[]{:S(2)}) %all-to-all-start) | async-done | bytes 196640 | tf_op jit(solution)/shard_map/all_to_all | solution.py:184
  153.0 0.2 reshape.214
  153.2 1.0 multiply_reduce_fusion.2
  154.4 2.7 %convolution_convert_fusion = bf16[8,16,2304]{2,1,0:T(8,128)(2,1)S(1)} fusion(bf16[768,6144]{1,0:T(8,128)(2,1)} %all-gather.2.cloned.1.call-done, f32[8,16,768]{2,1,0:T(8,128)S(1)} %bitcast.96, f32[8,16]{1,0:T(8,128)S(1)} %rsqrt.36), kind=kOutput, calls=%fused_computation | convolution fusion | flops 453476352 | bytes 4522496 | tf_op jit(solution)/shard_map/dot_general | solution.py:225
  157.1 0.7 fusion.76
  157.8 0.3 reshape.193
  158.1 0.3 reshape.192
  158.5 1.5 fusion.8
  160.0 2.7 %fusion.13 = bf16[8,16,12,64]{3,0,2,1:T(8,128)(2,1)} fusion(bf16[8,16,12,64]{3,2,1,0:T(8,128)(2,1)S(1)} %reshape.195, f32[16,12,8,8]{2,3,1,0:T(8,128)} %fusion.8), kind=kOutput, calls=%fused_computation.30 | convolution fusion | flops 1697287 | bytes 442368 | tf_op jit(solution)/shard_map/phfg,fphd->gphd/dot_general | solution.py:173
  162.7 2.5 %fusion.53 = f32[16,12,8,8]{2,3,1,0:T(8,128)} fusion(f32[16,12,8,8]{2,3,1,0:T(8,128)} %fusion.8), kind=kOutput, calls=%fused_computation.85 | output fusion | flops 13831 | bytes 98304 | tf_op jit(solution)/shard_map/div | solution.py:128
  165.3 1.3 reshape.191
  166.5 4.2 %multiply_reduce_fusion = (f32[16,12,8]{2,1,0:T(8,128)}, bf16[16,12,64,8]{2,3,1,0:T(8,128)(2,1)}) fusion(f32[16,12,8,64]{3,1,0,2:T(8,128)} %bitcast_convert_fusion, f32[16,12,8,8]{2,3,1,0:T(8,128)} %fusion.8, bf16[8,16,12,64]{3,2,1,0:T(8,128)(2,1)S(1)} %reshape.191), kind=kOutput, calls=%fused_computation.56 | convolution fusion | flops 1990663 | bytes 841728 | tf_op jit(solution)/shard_map/phfg,gphd->fphd/dot_general | solution.py:129
  170.7 1.8 fusion.10
  172.5 0.4 fusion.14
  172.9 0.4 fusion.15
  173.5 0.3 reshape.194
  173.9 0.3 reshape.196
  174.3 0.3 reshape.197
  174.7 0.3 reshape.198
  175.0 3.4 %multiply_reduce_fusion.1 = (f32[8,16]{1,0:T(8,128)S(1)}, f32[8,16,768]{2,1,0:T(8,128)S(1)}) fusion(f32[8,16,768]{2,1,0:T(8,128)S(1)} %bitcast.97, bf16[768,6144]{1,0:T(8,128)(2,1)} %all-gather.2.cloned.1.call-done, bf16[8,16,768]{2,1,0:T(8,128)(2,1)S(1)} %reshape.198, bf16[8,16,768]{2,1,0:T(8,128)(2,1)S(1)} %reshape.197, bf16[8,16,768]{2,1,0:T(8,128)(2,1)S(1)} %reshape.196), kind=kOutput, calls=%fused_computation.83 | convolution fusion | flops 454950784 | bytes 4915712 | tf_op jit(solution)/shard_map/dot_general | solution.py:240
  178.7 1.6 fusion.25
  180.3 15.4 %all_to_all.30 = bf16[8,16,1536]{2,1,0:T(8,128)(2,1)S(1)} all-to-all(bf16[8,16,1536]{2,1,0:T(8,128)(2,1)S(1)} %pad_maximum_fusion.2), channel_id=1, replica_groups=mesh['frame'=8,'space'=32,'dp'=2] {'frame'}, dimensions={0} | all-to-all | bytes 786432 | tf_op jit(solution)/shard_map/all_to_all | solution.py:188
  195.7 1.8 convolution_convert_fusion.4
  197.8 2.5 %fusion.42 = f32[12,64,384]{2,1,0:T(8,128)S(1)} fusion(bf16[128,12,64]{0,2,1:T(8,128)(2,1)S(1)} %bitcast.118, f32[12,128,384]{2,1,0:T(8,128)} %copy-done.10, f32[12,128]{1,0:T(8,128)S(1)} %get-tuple-element.13, pred[384]{0:T(512)(128)(4,1)S(1)} %broadcast_bitcast_fusion), kind=kOutput, calls=%fused_computation.69 | convolution fusion | flops 77856768 | bytes 3742080 | tf_op jit(solution)/shard_map/gst,sgh->tgh/dot_general | solution.py:102
  200.3 1.0 multiply_convert_fusion
  201.3 0.4 convolution_multiply_fusion
  201.8 3.1 %collective-permute-start.2 = (bf16[128,1536]{0,1:T(8,128)(2,1)S(1)}, bf16[128,1536]{0,1:T(8,128)(2,1)S(1)}, u32[]{:S(2)}, u32[]{:S(2)}) collective-permute-start(bf16[128,1536]{0,1:T(8,128)(2,1)S(1)} %get-tuple-element.4), channel_id=1, source_target_pairs={{0,2},{2,4},{4,6},{6,8},{8,10},{10,12},{12,14},{14,16},{16,18},{18... | collective-permute-start | bytes 1179656 | tf_op jit(solution)/shard_map/ppermute | solution.py:22
  205.0 2.7 %collective-permute-start.3 = (bf16[128,1536]{0,1:T(8,128)(2,1)S(1)}, bf16[128,1536]{0,1:T(8,128)(2,1)S(1)}, u32[]{:S(2)}, u32[]{:S(2)}) collective-permute-start(bf16[128,1536]{0,1:T(8,128)(2,1)S(1)} %get-tuple-element.5), channel_id=1, source_target_pairs={{2,0},{4,2},{6,4},{8,6},{10,8},{12,10},{14,12},{16,14},{18,16},{20... | collective-permute-start | bytes 1179656 | tf_op jit(solution)/shard_map/ppermute | solution.py:24
  207.7 0.7 slice_bitcast_fusion.6
  208.4 0.6 fusion.20
  209.0 2.5 %collective-permute-done.2 = bf16[128,1536]{0,1:T(8,128)(2,1)S(1)} collective-permute-done((bf16[128,1536]{0,1:T(8,128)(2,1)S(1)}, bf16[128,1536]{0,1:T(8,128)(2,1)S(1)}, u32[]{:S(2)}, u32[]{:S(2)}) %collective-permute-start.2) | collective-permute-done | bytes 393248 | tf_op jit(solution)/shard_map/ppermute | solution.py:22
  211.5 5.2 %collective-permute-done.3 = bf16[128,1536]{0,1:T(8,128)(2,1)S(1)} collective-permute-done((bf16[128,1536]{0,1:T(8,128)(2,1)S(1)}, bf16[128,1536]{0,1:T(8,128)(2,1)S(1)}, u32[]{:S(2)}, u32[]{:S(2)}) %collective-permute-start.3) | collective-permute-done | bytes 393248 | tf_op jit(solution)/shard_map/ppermute | solution.py:24
  216.7 0.2 fusion.33
  216.9 3.4 %fusion.45 = (f32[128]{0:T(128)S(1)}, f32[128]{0:T(128)S(1)}, f32[128,768]{1,0:T(8,128)S(1)}) fusion(bf16[1,128,768]{2,1,0:T(8,128)(2,1)S(1)} %copy-done.1, bf16[768,6144]{1,0:T(8,128)(2,1)} %all-gather.2.cloned.1.call-done, bf16[128,1536]{0,1:T(8,128)(2,1)S(1)} %fusion.33, bf16[128,768]{0,1:T(8,128)(2,1)S(1)} %bitcast.123), kind=kOutput, calls=%fused_computation.73 | convolution fusion | flops 454655744 | bytes 4719616 | tf_op jit(solution)/shard_map/dot_general | solution.py:264
  220.4 0.9 fusion.62
  (51 shorter events, 1.9 us)
Async XLA Ops:
  7.2 21.3 %copy-start = (s32[32,4]{0,1:T(4,128)S(1)}, s32[32,4]{0,1:T(4,128)}, u32[]{:S(2)}) copy-start(s32[32,4]{0,1:T(4,128)} %param.13) | copy-start | bytes 1540
  7.2 21.7 %copy-start.1 = (bf16[1,128,768]{2,1,0:T(8,128)(2,1)S(1)}, bf16[1,128,768]{2,1,0:T(8,128)(2,1)}, u32[]{:S(2)}) copy-start(bf16[1,128,768]{2,1,0:T(8,128)(2,1)} %param.7) | copy-start | bytes 589828
  7.2 116.5 %all-gather.2.cloned.1.call-start = ((), (), s32[]{:S(2)}) async-start(), calls=%async_computation.3 | async-start | bytes 9732096 | tf_op jit(solution)/shard_map/all_gather | solution.py:196
  9.0 19.8 %collective-permute-start.1 = (bf16[128,768]{1,0:T(8,128)(2,1)}, bf16[128,768]{1,0:T(8,128)(2,1)S(1)}, u32[]{:S(2)}, u32[]{:S(2)}) collective-permute-start(bf16[128,768]{1,0:T(8,128)(2,1)} %bitcast.100), channel_id=1, source_target_pairs={{2,0},{4,2},{6,4},{8,6},{10,8},{12,10},{14,12},{16,14},{18,16},{20... | collective-permute-start | bytes 589832 | tf_op jit(solution)/shard_map/ppermute | solution.py:24
  11.8 17.1 %collective-permute-start = (bf16[128,768]{1,0:T(8,128)(2,1)}, bf16[128,768]{1,0:T(8,128)(2,1)S(1)}, u32[]{:S(2)}, u32[]{:S(2)}) collective-permute-start(bf16[128,768]{1,0:T(8,128)(2,1)} %bitcast.101), channel_id=1, source_target_pairs={{0,2},{2,4},{4,6},{6,8},{8,10},{10,12},{12,14},{14,16},{16,18},{18... | collective-permute-start | bytes 589832 | tf_op jit(solution)/shard_map/ppermute | solution.py:22
  21.4 17.0 %all-to-all-start.1 = ((bf16[8,2,6144]{2,1,0:T(2,128)(2,1)}), bf16[8,2,6144]{2,1,0:T(2,128)(2,1)S(1)}, u32[]{:S(2)}, u32[]{:S(2)}) async-start(bf16[8,2,6144]{2,1,0:T(2,128)(2,1)} %reshape.215), calls=%async_computation.1 | async-start | bytes 393216 | tf_op jit(solution)/shard_map/all_to_all | solution.py:184
  38.6 104.4 %copy-start.4 = (bf16[1,128,768]{2,1,0:T(8,128)(2,1)}, bf16[1,128,768]{2,1,0:T(8,128)(2,1)S(1)}, u32[]{:S(2)}) copy-start(bf16[1,128,768]{2,1,0:T(8,128)(2,1)S(1)} %copy.129) | copy-start | bytes 589828
  128.9 1.5 copy-start.6
  129.7 1.4 copy-start.10
  131.1 0.7 copy-start.2
  136.2 16.8 %all-to-all-start = ((bf16[8,2,6144]{2,1,0:T(2,128)(2,1)}), bf16[8,2,6144]{2,1,0:T(2,128)(2,1)S(1)}, u32[]{:S(2)}, u32[]{:S(2)}) async-start(bf16[8,2,6144]{2,1,0:T(2,128)(2,1)} %reshape.213), calls=%async_computation | async-start | bytes 393216 | tf_op jit(solution)/shard_map/all_to_all | solution.py:184
  170.7 2.6 %copy-start.9 = (bf16[16,12,64,8]{2,3,1,0:T(8,128)(2,1)S(1)}, bf16[16,12,64,8]{2,3,1,0:T(8,128)(2,1)}, u32[]{:S(2)}) copy-start(bf16[16,12,64,8]{2,3,1,0:T(8,128)(2,1)} %get-tuple-element.16) | copy-start | bytes 589828
  173.4 1.2 copy-start.8
  175.0 3.5 %copy-start.5 = (bf16[1,128,768]{2,1,0:T(8,128)(2,1)S(1)}, bf16[1,128,768]{2,1,0:T(8,128)(2,1)}, u32[]{:S(2)}) copy-start(bf16[1,128,768]{2,1,0:T(8,128)(2,1)} %copy-done.4) | copy-start | bytes 589828
  180.3 17.4 %copy-start.3 = (bf16[12,64,128]{2,1,0:T(8,128)(2,1)S(1)}, bf16[12,64,128]{2,1,0:T(8,128)(2,1)}, u32[]{:S(2)}) copy-start(bf16[12,64,128]{2,1,0:T(8,128)(2,1)} %copy-done.2) | copy-start | bytes 589828
  197.7 2.5 %copy-start.7 = (bf16[384,768]{0,1:T(8,128)(2,1)S(1)}, bf16[384,768]{0,1:T(8,128)(2,1)}, u32[]{:S(2)}) copy-start(bf16[384,768]{0,1:T(8,128)(2,1)} %copy-done.6) | copy-start | bytes 1769476
  197.7 2.6 %copy-start.11 = (f32[12,128,384]{2,1,0:T(8,128)S(1)}, f32[12,128,384]{2,1,0:T(8,128)}, u32[]{:S(2)}) copy-start(f32[12,128,384]{2,1,0:T(8,128)} %copy-done.10) | copy-start | bytes 7077892
  201.8 9.7 %collective-permute-start.2 = (bf16[128,1536]{0,1:T(8,128)(2,1)S(1)}, bf16[128,1536]{0,1:T(8,128)(2,1)S(1)}, u32[]{:S(2)}, u32[]{:S(2)}) collective-permute-start(bf16[128,1536]{0,1:T(8,128)(2,1)S(1)} %get-tuple-element.4), channel_id=1, source_target_pairs={{0,2},{2,4},{4,6},{6,8},{8,10},{10,12},{12,14},{14,16},{16,18},{18... | collective-permute-start | bytes 1179656 | tf_op jit(solution)/shard_map/ppermute | solution.py:22
  205.0 11.8 %collective-permute-start.3 = (bf16[128,1536]{0,1:T(8,128)(2,1)S(1)}, bf16[128,1536]{0,1:T(8,128)(2,1)S(1)}, u32[]{:S(2)}, u32[]{:S(2)}) collective-permute-start(bf16[128,1536]{0,1:T(8,128)(2,1)S(1)} %get-tuple-element.5), channel_id=1, source_target_pairs={{2,0},{4,2},{6,4},{8,6},{10,8},{12,10},{14,12},{16,14},{18,16},{20... | collective-permute-start | bytes 1179656 | tf_op jit(solution)/shard_map/ppermute | solution.py:24
Sparse Core Ops, SparseCore 0:
  11.2 112.4 all-gather.1

commit v4 on v3

--- a/solution.py
+++ b/solution.py
@@ -192,15 +192,19 @@
     local_in = frames_in[0]
     grad_out = cotangent[0]
     shard, feature_count = local_in.shape
-    weight_rows = jnp.concatenate([w_qkv_space, w_out_space, w_qkv_time, w_out_time], axis=1)
-    all_weights = lax.all_gather(weight_rows, "space", axis=0, tiled=True)
-    widths = [w_qkv_space.shape[1], w_out_space.shape[1], w_qkv_time.shape[1], w_out_time.shape[1]]
-    bounds = [0]
-    for width in widths:
-        bounds.append(bounds[-1] + width)
-    full_qkv_space, full_out_space, full_qkv_time, full_out_time = (
-        all_weights[:, bounds[index] : bounds[index + 1]] for index in range(4)
-    )
+    space_rows = jnp.concatenate([w_qkv_space, w_out_space], axis=1)
+    time_rows = jnp.concatenate([w_qkv_time, w_out_time], axis=1)
+    mine = lax.dynamic_index_in_dim(
+        jnp.stack([space_rows, time_rows]), lax.axis_index("dp"), 0, keepdims=False
+    )
+    all_weights = lax.all_gather(mine, ("dp", "space"), axis=0, tiled=True).reshape(
+        2, -1, space_rows.shape[1]
+    )
+    qkv_width = w_qkv_space.shape[1]
+    full_qkv_space = all_weights[0, :, :qkv_width]
+    full_out_space = all_weights[0, :, qkv_width:]
+    full_qkv_time = all_weights[1, :, :qkv_width]
+    full_out_time = all_weights[1, :, qkv_width:]
     block_count = shard // BLOCK
     space_index = lax.axis_index("space")
     lists_here = lax.dynamic_slice_in_dim(neighbours, space_index * block_count, block_count, 0)

time: 229 us -> 212 us (0.926)
  waiting for transfers between devices: 109 us -> 94 us
  local copies, waits for them, and re-layouts: 12 us -> 16.2 us
  matrix products: 37.6 us -> 33.6 us
    all_gather x1, waiting for transfers between devices: 85.1 us -> 68.2 us  [local(): lax.all_gather(mine, ('dp', 'space'), axis=0, tiled=True)]
    unnamed x32 -> x31, local copies, waits for them, and re-layouts: 5.1 us -> 6 us
  transfers between devices with their start and end apart: 7 -> 7, of which waited for: 5 -> 5; matrix products, arithmetic and copies ran while one was open for 4% -> 5% of each run, Pallas kernels for 0% -> 0%
where the time goes in v4:
time: 212 us; the launch traced here: 211 us
  waiting for transfers between devices  94 us (44%)
  matrix products  33.6 us (16%)
  starting transfers between devices  26.7 us (13%)
  local copies, waits for them, and re-layouts  16.2 us (8%)
  blocking collectives  16.2 us (8%)
  between operations  14.6 us (7%)
  other arithmetic  9.83 us (5%)
    all_gather x1, waiting for transfers between devices, local(): lax.all_gather(mine, ('dp', 'space'), axis=0, tiled=True)  68.2 us
    all_to_all x2, waiting for transfers between devices, to_frames(): lax.all_to_all(local_rows[None], 'frame', split_axis=1, concat_axis=0, ti...  17.1 us
    all_to_all x1, blocking collectives, to_space(): lax.all_to_all(frame_rows, 'frame', split_axis=0, concat_axis=1, tiled=True)  16.2 us
    all_to_all x2, starting transfers between devices, to_frames(): lax.all_to_all(local_rows[None], 'frame', split_axis=1, concat_axis=0, ti...  13.8 us
    ppermute x2, starting transfers between devices, padded(): lax.ppermute(tail, axis, [(i, (i + 1) % count) for i in range(ends)])  8.96 us
    ppermute x2, waiting for transfers between devices, padded(): lax.ppermute(head, axis, [((i + 1) % count, i) for i in range(ends)])  6.23 us
    unnamed x31, local copies, waits for them, and re-layouts  6 us
    unnamed x3, other arithmetic  4.74 us
  transfers between devices with their start and end apart: 7, of which 5 were waited for; matrix products, arithmetic and copies ran while one was open for 5% of the time, Pallas kernels for 0%

profile of v4, /device:TPU:6, one launch (start us, length us, event | category | flops | bytes accessed | tf_op | source)
XLA Modules:
  0.0 211.1 jit_solution(3548123915584443304)
XLA Ops:
  7.2 1.0 maximum_bitcast_fusion
  8.3 0.7 fusion.64
  9.1 4.2 %collective-permute-start = (bf16[128,768]{1,0:T(8,128)(2,1)}, bf16[128,768]{1,0:T(8,128)(2,1)S(1)}, u32[]{:S(2)}, u32[]{:S(2)}) collective-permute-start(bf16[128,768]{1,0:T(8,128)(2,1)} %bitcast.126), channel_id=1, source_target_pairs={{0,2},{2,4},{4,6},{6,8},{8,10},{10,12},{12,14},{14,16},{16,18},{18... | collective-permute-start | bytes 589832 | tf_op jit(solution)/shard_map/ppermute | solution.py:22
  13.3 1.9 collective-permute-start.1
  15.2 1.2 copy.157
  16.4 0.6 broadcast.184
  17.0 1.8 reduce.9
  18.8 0.7 reshape.230
  19.6 7.1 %all-to-all-start.1 = ((bf16[8,2,6144]{2,1,0:T(2,128)(2,1)}), bf16[8,2,6144]{2,1,0:T(2,128)(2,1)S(1)}, u32[]{:S(2)}, u32[]{:S(2)}) async-start(bf16[8,2,6144]{2,1,0:T(2,128)(2,1)} %reshape.230), calls=%async_computation.1 | async-start | bytes 393216 | tf_op jit(solution)/shard_map/all_to_all | solution.py:184
  26.7 0.2 dynamic-slice_reduce_fusion
  27.0 0.2 fusion.14
  27.4 9.4 %all-to-all-done.1 = bf16[8,2,6144]{2,1,0:T(2,128)(2,1)S(1)} async-done(((bf16[8,2,6144]{2,1,0:T(2,128)(2,1)}), bf16[8,2,6144]{2,1,0:T(2,128)(2,1)S(1)}, u32[]{:S(2)}, u32[]{:S(2)}) %all-to-all-start.1) | async-done | bytes 196640 | tf_op jit(solution)/shard_map/all_to_all | solution.py:184
  37.1 68.2 %all-gather.3.cloned.1.call-done = bf16[1,1536,3072]{2,1,0:T(8,128)(2,1)} async-done(((bf16[1,24,3072]{2,1,0:T(8,128)(2,1)}), bf16[1,1536,3072]{2,1,0:T(8,128)(2,1)}) %all-gather.3.cloned.1.call-update) | async-done | bytes 9437200 | tf_op jit(solution)/shard_map/all_gather | solution.py:200
  105.3 2.2 %slice_bitcast_fusion.1 = bf16[768,2304]{1,0:T(8,128)(2,1)S(1)} fusion(bf16[2,768,3072]{2,1,0:T(8,128)(2,1)} %bitcast.115), kind=kLoop, calls=%fused_computation.2 | loop fusion | bytes 7077888 | tf_op jit(solution)/shard_map/squeeze | solution.py:204
  107.5 1.1 convolution_convert_fusion.1
  108.6 0.3 fusion.19
  109.1 0.3 copy.92
  109.5 0.3 copy.90
  109.9 0.7 fusion.4
  110.6 0.7 convolution_convert_fusion.6
  111.3 0.6 copy-done.9
  112.0 0.7 copy-done.3
  112.6 1.6 fusion.25
  114.3 0.3 copy.158
  114.6 1.8 reduce.8
  116.4 0.7 reshape.228
  117.1 6.7 %all-to-all-start = ((bf16[8,2,6144]{2,1,0:T(2,128)(2,1)}), bf16[8,2,6144]{2,1,0:T(2,128)(2,1)S(1)}, u32[]{:S(2)}, u32[]{:S(2)}) async-start(bf16[8,2,6144]{2,1,0:T(2,128)(2,1)} %reshape.228), calls=%async_computation | async-start | bytes 393216 | tf_op jit(solution)/shard_map/all_to_all | solution.py:184
  123.9 1.8 fusion.24
  125.7 0.3 reshape.208
  126.0 1.1 bitcast_convert_fusion
  127.1 7.7 %all-to-all-done = bf16[8,2,6144]{2,1,0:T(2,128)(2,1)S(1)} async-done(((bf16[8,2,6144]{2,1,0:T(2,128)(2,1)}), bf16[8,2,6144]{2,1,0:T(2,128)(2,1)S(1)}, u32[]{:S(2)}, u32[]{:S(2)}) %all-to-all-start) | async-done | bytes 196640 | tf_op jit(solution)/shard_map/all_to_all | solution.py:184
  135.2 2.6 %convolution_convert_fusion = bf16[8,16,2304]{2,1,0:T(8,128)(2,1)S(1)} fusion(bf16[8,16,768]{2,1,0:T(8,128)(2,1)S(1)} %bitcast.149, bf16[2,768,3072]{2,1,0:T(8,128)(2,1)} %bitcast.118), kind=kOutput, calls=%fused_computation | convolution fusion | flops 453279744 | bytes 4325376 | tf_op jit(solution)/shard_map/dot_general | solution.py:229
  137.9 0.7 fusion.73
  138.6 0.3 reshape.205
  138.9 0.3 reshape.206
  139.3 1.3 reshape.204
  140.5 0.6 fusion.6
  141.1 1.0 copy-done.11
  142.1 1.1 fusion.50
  143.2 4.2 %multiply_reduce_fusion = (f32[16,12,8]{2,1,0:T(8,128)}, bf16[16,12,64,8]{2,3,1,0:T(8,128)(2,1)}) fusion(f32[16,12,8,64]{3,1,0,2:T(8,128)} %bitcast_convert_fusion, f32[16,12,8,8]{2,3,1,0:T(8,128)} %copy-done.11, bf16[8,16,12,64]{3,2,1,0:T(8,128)(2,1)S(1)} %reshape.204), kind=kOutput, calls=%fused_computation.54 | convolution fusion | flops 1990663 | bytes 841728 | tf_op jit(solution)/shard_map/phfg,gphd->fphd/dot_general | solution.py:129
  147.4 1.7 fusion.8
  149.1 1.2 fusion.13
  150.3 0.4 fusion.12
  150.7 2.0 fusion.11
  152.8 1.1 copy.99
  153.9 0.3 reshape.207
  154.3 0.3 reshape.209
  154.7 0.3 reshape.210
  155.1 0.3 reshape.211
  155.4 1.6 fusion.23
  157.0 3.4 %multiply_reduce_fusion.1 = (f32[8,16]{1,0:T(8,128)S(1)}, f32[8,16,768]{2,1,0:T(8,128)S(1)}) fusion(f32[8,16,768]{2,1,0:T(8,128)S(1)} %bitcast.124, bf16[2,768,3072]{2,1,0:T(8,128)(2,1)} %bitcast.120, bf16[8,16,768]{2,1,0:T(8,128)(2,1)S(1)} %reshape.211, bf16[8,16,768]{2,1,0:T(8,128)(2,1)S(1)} %reshape.210, bf16[8,16,768]{2,1,0:T(8,128)(2,1)S(1)} %reshape.209), kind=kOutput, calls=%fused_computation.82 | convolution fusion | flops 454950784 | bytes 4915712 | tf_op jit(solution)/shard_map/dot_general | solution.py:244
  160.7 16.2 %all_to_all.30 = bf16[8,16,1536]{2,1,0:T(8,128)(2,1)S(1)} all-to-all(bf16[8,16,1536]{2,1,0:T(8,128)(2,1)S(1)} %pad_maximum_fusion.2), channel_id=1, replica_groups=mesh['frame'=8,'space'=32,'dp'=2] {'frame'}, dimensions={0} | all-to-all | bytes 786432 | tf_op jit(solution)/shard_map/all_to_all | solution.py:188
  176.9 1.8 convolution_convert_fusion.4
  179.0 2.5 %fusion.39 = f32[12,64,384]{2,1,0:T(8,128)S(1)} fusion(bf16[128,12,64]{0,2,1:T(8,128)(2,1)S(1)} %bitcast.144, f32[12,128,384]{2,1,0:T(8,128)} %copy-done.9, f32[12,128]{1,0:T(8,128)S(1)} %get-tuple-element.13, pred[384]{0:T(512)(128)(4,1)S(1)} %broadcast_bitcast_fusion), kind=kOutput, calls=%fused_computation.68 | convolution fusion | flops 77856768 | bytes 3742080 | tf_op jit(solution)/shard_map/gst,sgh->tgh/dot_general | solution.py:102
  181.6 0.9 multiply_convert_fusion
  182.5 0.4 convolution_multiply_fusion
  183.1 4.8 %collective-permute-start.2 = (bf16[128,1536]{0,1:T(8,128)(2,1)S(1)}, bf16[128,1536]{0,1:T(8,128)(2,1)S(1)}, u32[]{:S(2)}, u32[]{:S(2)}) collective-permute-start(bf16[128,1536]{0,1:T(8,128)(2,1)S(1)} %get-tuple-element.4), channel_id=1, source_target_pairs={{0,2},{2,4},{4,6},{6,8},{8,10},{10,12},{12,14},{14,16},{16,18},{18... | collective-permute-start | bytes 1179656 | tf_op jit(solution)/shard_map/ppermute | solution.py:22
  187.8 1.9 collective-permute-start.3
  189.8 0.7 slice_bitcast_fusion.10
  190.5 0.6 fusion.18
  191.1 2.4 %collective-permute-done.2 = bf16[128,1536]{0,1:T(8,128)(2,1)S(1)} collective-permute-done((bf16[128,1536]{0,1:T(8,128)(2,1)S(1)}, bf16[128,1536]{0,1:T(8,128)(2,1)S(1)}, u32[]{:S(2)}, u32[]{:S(2)}) %collective-permute-start.2) | collective-permute-done | bytes 393248 | tf_op jit(solution)/shard_map/ppermute | solution.py:22
  193.5 6.2 %collective-permute-done.3 = bf16[128,1536]{0,1:T(8,128)(2,1)S(1)} collective-permute-done((bf16[128,1536]{0,1:T(8,128)(2,1)S(1)}, bf16[128,1536]{0,1:T(8,128)(2,1)S(1)}, u32[]{:S(2)}, u32[]{:S(2)}) %collective-permute-start.3) | collective-permute-done | bytes 393248 | tf_op jit(solution)/shard_map/ppermute | solution.py:24
  199.9 3.4 %fusion.42 = (f32[128]{0:T(128)S(1)}, f32[128]{0:T(128)S(1)}, f32[128,768]{1,0:T(8,128)S(1)}) fusion(bf16[1,128,768]{2,1,0:T(8,128)(2,1)S(1)} %copy-done.1, bf16[2,768,3072]{2,1,0:T(8,128)(2,1)} %bitcast.122, bf16[128,1536]{0,1:T(8,128)(2,1)S(1)} %fusion.29, bf16[128,768]{0,1:T(8,128)(2,1)S(1)} %bitcast.150), kind=kOutput, calls=%fused_computation.72 | convolution fusion | flops 454655744 | bytes 4719616 | tf_op jit(solution)/shard_map/dot_general | solution.py:268
  203.4 0.9 fusion.59
  (55 shorter events, 2.5 us)
Async XLA Ops:
  7.2 19.5 %copy-start = (s32[32,4]{0,1:T(4,128)S(1)}, s32[32,4]{0,1:T(4,128)}, u32[]{:S(2)}) copy-start(s32[32,4]{0,1:T(4,128)} %param.13) | copy-start | bytes 1540
  7.2 19.9 %copy-start.1 = (bf16[1,128,768]{2,1,0:T(8,128)(2,1)S(1)}, bf16[1,128,768]{2,1,0:T(8,128)(2,1)}, u32[]{:S(2)}) copy-start(bf16[1,128,768]{2,1,0:T(8,128)(2,1)} %param.7) | copy-start | bytes 589828
  7.2 98.1 %all-gather.3.cloned.1.call-start = ((), (), s32[]{:S(2)}) async-start(), calls=%async_computation.3 | async-start | bytes 9584640 | tf_op jit(solution)/shard_map/all_gather | solution.py:200
  9.1 18.0 %collective-permute-start = (bf16[128,768]{1,0:T(8,128)(2,1)}, bf16[128,768]{1,0:T(8,128)(2,1)S(1)}, u32[]{:S(2)}, u32[]{:S(2)}) collective-permute-start(bf16[128,768]{1,0:T(8,128)(2,1)} %bitcast.126), channel_id=1, source_target_pairs={{0,2},{2,4},{4,6},{6,8},{8,10},{10,12},{12,14},{14,16},{16,18},{18... | collective-permute-start | bytes 589832 | tf_op jit(solution)/shard_map/ppermute | solution.py:22
  13.3 13.8 %collective-permute-start.1 = (bf16[128,768]{1,0:T(8,128)(2,1)}, bf16[128,768]{1,0:T(8,128)(2,1)S(1)}, u32[]{:S(2)}, u32[]{:S(2)}) collective-permute-start(bf16[128,768]{1,0:T(8,128)(2,1)} %bitcast.127), channel_id=1, source_target_pairs={{2,0},{4,2},{6,4},{8,6},{10,8},{12,10},{14,12},{16,14},{18,16},{20... | collective-permute-start | bytes 589832 | tf_op jit(solution)/shard_map/ppermute | solution.py:24
  19.6 17.3 %all-to-all-start.1 = ((bf16[8,2,6144]{2,1,0:T(2,128)(2,1)}), bf16[8,2,6144]{2,1,0:T(2,128)(2,1)S(1)}, u32[]{:S(2)}, u32[]{:S(2)}) async-start(bf16[8,2,6144]{2,1,0:T(2,128)(2,1)} %reshape.230), calls=%async_computation.1 | async-start | bytes 393216 | tf_op jit(solution)/shard_map/all_to_all | solution.py:184
  37.1 86.8 %copy-start.5 = (bf16[1,128,768]{2,1,0:T(8,128)(2,1)}, bf16[1,128,768]{2,1,0:T(8,128)(2,1)S(1)}, u32[]{:S(2)}) copy-start(bf16[1,128,768]{2,1,0:T(8,128)(2,1)S(1)} %copy.130) | copy-start | bytes 589828
  109.9 1.5 copy-start.7
  110.6 1.4 copy-start.9
  112.0 0.7 copy-start.3
  117.1 17.6 %all-to-all-start = ((bf16[8,2,6144]{2,1,0:T(2,128)(2,1)}), bf16[8,2,6144]{2,1,0:T(2,128)(2,1)S(1)}, u32[]{:S(2)}, u32[]{:S(2)}) async-start(bf16[8,2,6144]{2,1,0:T(2,128)(2,1)} %reshape.228), calls=%async_computation | async-start | bytes 393216 | tf_op jit(solution)/shard_map/all_to_all | solution.py:184
  141.1 1.0 copy-start.11
  150.7 3.5 %copy-start.2 = (bf16[8,16,12,64]{3,0,2,1:T(8,128)(2,1)S(1)}, bf16[8,16,12,64]{3,0,2,1:T(8,128)(2,1)}, u32[]{:S(2)}) copy-start(bf16[8,16,12,64]{3,0,2,1:T(8,128)(2,1)} %fusion.13) | copy-start | bytes 589828
  157.0 3.5 %copy-start.6 = (bf16[1,128,768]{2,1,0:T(8,128)(2,1)S(1)}, bf16[1,128,768]{2,1,0:T(8,128)(2,1)}, u32[]{:S(2)}) copy-start(bf16[1,128,768]{2,1,0:T(8,128)(2,1)} %copy-done.5) | copy-start | bytes 589828
  160.5 18.4 %copy-start.4 = (bf16[12,64,128]{2,1,0:T(8,128)(2,1)S(1)}, bf16[12,64,128]{2,1,0:T(8,128)(2,1)}, u32[]{:S(2)}) copy-start(bf16[12,64,128]{2,1,0:T(8,128)(2,1)} %copy-done.3) | copy-start | bytes 589828
  179.0 2.5 %copy-start.8 = (bf16[384,768]{0,1:T(8,128)(2,1)S(1)}, bf16[384,768]{0,1:T(8,128)(2,1)}, u32[]{:S(2)}) copy-start(bf16[384,768]{0,1:T(8,128)(2,1)} %copy-done.7) | copy-start | bytes 1769476
  179.0 2.6 %copy-start.10 = (f32[12,128,384]{2,1,0:T(8,128)S(1)}, f32[12,128,384]{2,1,0:T(8,128)}, u32[]{:S(2)}) copy-start(f32[12,128,384]{2,1,0:T(8,128)} %copy-done.9) | copy-start | bytes 7077892
  183.1 10.5 %collective-permute-start.2 = (bf16[128,1536]{0,1:T(8,128)(2,1)S(1)}, bf16[128,1536]{0,1:T(8,128)(2,1)S(1)}, u32[]{:S(2)}, u32[]{:S(2)}) collective-permute-start(bf16[128,1536]{0,1:T(8,128)(2,1)S(1)} %get-tuple-element.4), channel_id=1, source_target_pairs={{0,2},{2,4},{4,6},{6,8},{8,10},{10,12},{12,14},{14,16},{16,18},{18... | collective-permute-start | bytes 1179656 | tf_op jit(solution)/shard_map/ppermute | solution.py:22
  187.8 11.9 %collective-permute-start.3 = (bf16[128,1536]{0,1:T(8,128)(2,1)S(1)}, bf16[128,1536]{0,1:T(8,128)(2,1)S(1)}, u32[]{:S(2)}, u32[]{:S(2)}) collective-permute-start(bf16[128,1536]{0,1:T(8,128)(2,1)S(1)} %get-tuple-element.5), channel_id=1, source_target_pairs={{2,0},{4,2},{6,4},{8,6},{10,8},{12,10},{14,12},{16,14},{18,16},{20... | collective-permute-start | bytes 1179656 | tf_op jit(solution)/shard_map/ppermute | solution.py:24
Sparse Core Ops, SparseCore 0:
  11.4 93.9 all-gather.2

commit v5 on v4

--- a/solution.py
+++ b/solution.py
@@ -109,77 +109,6 @@
     )
 
 
-def time_attend(queries, key_rows, value_rows):
-    frame_count, position_count, feature_count = queries.shape
-    split_shape = (frame_count, position_count, HEADS, HD)
-    score_scale = HD ** (-0.5)
-    scores = (
-        jnp.einsum(
-            "fphd,gphd->phfg",
-            queries.reshape(split_shape),
-            key_rows.reshape(split_shape),
-            preferred_element_type=jnp.float32,
-        )
-        * score_scale
-    )
-    causal = jnp.arange(frame_count)[:, None] >= jnp.arange(frame_count)[None, :]
-    exponent = jnp.where(causal, jnp.exp(scores), 0.0)
-    totals = jnp.sum(exponent, axis=-1)
-    probability = (exponent / totals[..., None]).astype(jnp.bfloat16)
-    combined = jnp.einsum(
-        "phfg,gphd->fphd",
-        probability,
-        value_rows.reshape(split_shape),
-        preferred_element_type=jnp.float32,
-    )
-    return (
-        combined.astype(jnp.bfloat16).reshape(frame_count, position_count, feature_count),
-        totals,
-    )
-
-
-def time_back(queries, key_rows, value_rows, attended, grad_attended, totals):
-    frame_count, position_count, feature_count = queries.shape
-    split_shape = (frame_count, position_count, HEADS, HD)
-    score_scale = HD ** (-0.5)
-    query_four = queries.reshape(split_shape)
-    key_four = key_rows.reshape(split_shape)
-    value_four = value_rows.reshape(split_shape)
-    out_four = attended.reshape(split_shape)
-    grad_four = grad_attended.reshape(split_shape)
-    scores = (
-        jnp.einsum("fphd,gphd->phfg", query_four, key_four, preferred_element_type=jnp.float32)
-        * score_scale
-    )
-    causal = jnp.arange(frame_count)[:, None] >= jnp.arange(frame_count)[None, :]
-    exponent = jnp.where(causal, jnp.exp(scores), 0.0)
-    weight = exponent / totals[..., None]
-    probability = weight.astype(jnp.bfloat16)
-    prob_grad = jnp.einsum(
-        "fphd,gphd->phfg", grad_four, value_four, preferred_element_type=jnp.float32
-    )
-    row_delta = jnp.einsum(
-        "fphd,fphd->phf", grad_four, out_four, preferred_element_type=jnp.float32
-    )
-    score_grad = (weight * (prob_grad - row_delta[..., None])).astype(jnp.bfloat16)
-    query_grad = (
-        jnp.einsum("phfg,gphd->fphd", score_grad, key_four, preferred_element_type=jnp.float32)
-        * score_scale
-    )
-    key_grad = (
-        jnp.einsum("phfg,fphd->gphd", score_grad, query_four, preferred_element_type=jnp.float32)
-        * score_scale
-    )
-    value_grad = jnp.einsum(
-        "phfg,fphd->gphd", probability, grad_four, preferred_element_type=jnp.float32
-    )
-    pieces = [
-        gradient.astype(jnp.bfloat16).reshape(frame_count, position_count, feature_count)
-        for gradient in (query_grad, key_grad, value_grad)
-    ]
-    return jnp.concatenate(pieces, axis=-1)
-
-
 def to_frames(local_rows):
     return lax.all_to_all(local_rows[None], "frame", split_axis=1, concat_axis=0, tiled=True)
 
@@ -229,18 +158,36 @@
     projected_time = jnp.dot(normed_time, full_qkv_time, preferred_element_type=jnp.float32).astype(
         jnp.bfloat16
     )
-    query_time = projected_time[..., :feature_count]
-    key_time = projected_time[..., feature_count : 2 * feature_count]
-    value_time = projected_time[..., 2 * feature_count :]
-    attended_time, totals_time = time_attend(query_time, key_time, value_time)
+    frame_count, position_count = stream_rows.shape[:2]
+    row_count = frame_count * position_count
+    time_flat = projected_time.reshape(row_count, 3 * feature_count)
+    query_time = time_flat[:, :feature_count]
+    key_time = time_flat[:, feature_count : 2 * feature_count]
+    value_time = time_flat[:, 2 * feature_count :]
+    row_ids = jnp.arange(row_count, dtype=jnp.int32)
+    same_position = (row_ids[:, None] % position_count) == (row_ids[None, :] % position_count)
+    causal = (row_ids[None, :] // position_count) <= (row_ids[:, None] // position_count)
+    allowed_time = same_position & causal
+    attended_flat, totals_time = space_attend(query_time, key_time, value_time, allowed_time)
+    attended_time = attended_flat.reshape(frame_count, position_count, feature_count)
     update_time = jnp.dot(attended_time, full_out_time, preferred_element_type=jnp.float32)
     frames_out_rows = (stream_rows.astype(jnp.float32) + update_time).astype(jnp.bfloat16)
     grad_att_time = jnp.dot(cot_rows, full_out_time.T, preferred_element_type=jnp.float32).astype(
         jnp.bfloat16
     )
-    gradients = time_back(
-        query_time, key_time, value_time, attended_time, grad_att_time, totals_time
-    )
+    grad_query_time, grad_key_time, grad_value_time = space_back(
+        query_time,
+        key_time,
+        value_time,
+        allowed_time,
+        totals_time,
+        attended_flat,
+        grad_att_time.reshape(row_count, feature_count),
+    )
+    gradients = jnp.concatenate(
+        [grad_query_time, grad_key_time.astype(jnp.bfloat16), grad_value_time.astype(jnp.bfloat16)],
+        axis=1,
+    ).reshape(frame_count, position_count, 3 * feature_count)
     grad_normed_time = jnp.dot(gradients, full_qkv_time.T, preferred_element_type=jnp.float32)
     grad_stream_rows = (
         cot_rows.astype(jnp.float32) + rms_back(stream_rows, grad_normed_time)

time: 212 us -> 208 us (0.981)
  waiting for transfers between devices: 94 us -> 91.5 us
    dot_general x6 -> x0, matrix products: 10 us -> none  [the longest x1 4.15 us: time_attend(): jnp.einsum('phfg,gphd->fphd', probability, value_rows.reshape(split_shape...]
    reshape x8 -> x0, local copies, waits for them, and re-layouts: 3.46 us -> none  [the longest x1 1.26 us: time_attend(): value_rows.reshape(split_shape)]
    convert_element_type x4 -> x6, local copies, waits for them, and re-layouts: 1.35 us -> 4.19 us  [the longest x2 1.66 us: local(): grad_value_time.astype(jnp.bfloat16)]
    dot_general x1 -> x2, matrix products: 2.5 us -> 4.96 us  [space_back(): jnp.einsum('gst,sgh->tgh', probability, grad_heads, preferred_element_typ...]
    dot_general x1 -> x2, matrix products: 0.73 us -> 3.18 us  [space_attend(): jnp.einsum('gst,tgh->sgh', probability, value_heads, preferred_element_ty...]
    unnamed x31 -> x26, local copies, waits for them, and re-layouts: 6 us -> 5.53 us
where the time goes in v5:
time: 208 us; the launch traced here: 207 us
  waiting for transfers between devices  91.5 us (44%)
  matrix products  31.8 us (15%)
  starting transfers between devices  28.5 us (14%)
  local copies, waits for them, and re-layouts  16.2 us (8%)
  blocking collectives  16.2 us (8%)
  between operations  14.5 us (7%)
  other arithmetic  8.54 us (4%)
    all_gather x1, waiting for transfers between devices, local(): lax.all_gather(mine, ('dp', 'space'), axis=0, tiled=True)  67.2 us
    all_to_all x1, blocking collectives, to_space(): lax.all_to_all(frame_rows, 'frame', split_axis=0, concat_axis=1, tiled=True)  16.2 us
    all_to_all x2, waiting for transfers between devices, to_frames(): lax.all_to_all(local_rows[None], 'frame', split_axis=1, concat_axis=0, ti...  15.6 us
    all_to_all x2, starting transfers between devices, to_frames(): lax.all_to_all(local_rows[None], 'frame', split_axis=1, concat_axis=0, ti...  13.8 us
    ppermute x2, starting transfers between devices, padded(): lax.ppermute(tail, axis, [(i, (i + 1) % count) for i in range(ends)])  9.98 us
    ppermute x2, waiting for transfers between devices, padded(): lax.ppermute(head, axis, [((i + 1) % count, i) for i in range(ends)])  6.23 us
    unnamed x26, local copies, waits for them, and re-layouts  5.53 us
    dot_general x2, matrix products, space_back(): jnp.einsum('gst,sgh->tgh', probability, grad_heads, preferred_element_typ...  4.96 us
  transfers between devices with their start and end apart: 7, of which 5 were waited for; matrix products, arithmetic and copies ran while one was open for 5% of the time, Pallas kernels for 0%

profile of v5, /device:TPU:6, one launch (start us, length us, event | category | flops | bytes accessed | tf_op | source)
XLA Modules:
  0.0 207.3 jit_solution(16243167040474465318)
XLA Ops:
  7.2 1.0 maximum_bitcast_fusion
  8.3 0.7 fusion.56
  9.1 2.7 %collective-permute-start.1 = (bf16[128,768]{1,0:T(8,128)(2,1)}, bf16[128,768]{1,0:T(8,128)(2,1)S(1)}, u32[]{:S(2)}, u32[]{:S(2)}) collective-permute-start(bf16[128,768]{1,0:T(8,128)(2,1)} %bitcast.139), channel_id=1, source_target_pairs={{2,0},{4,2},{6,4},{8,6},{10,8},{12,10},{14,12},{16,14},{18,16},{20... | collective-permute-start | bytes 589832 | tf_op jit(solution)/shard_map/ppermute | solution.py:24
  11.8 5.2 %collective-permute-start = (bf16[128,768]{1,0:T(8,128)(2,1)}, bf16[128,768]{1,0:T(8,128)(2,1)S(1)}, u32[]{:S(2)}, u32[]{:S(2)}) collective-permute-start(bf16[128,768]{1,0:T(8,128)(2,1)} %bitcast.140), channel_id=1, source_target_pairs={{0,2},{2,4},{4,6},{6,8},{8,10},{10,12},{12,14},{14,16},{16,18},{18... | collective-permute-start | bytes 589832 | tf_op jit(solution)/shard_map/ppermute | solution.py:22
  17.0 1.2 copy.139
  18.3 0.6 broadcast.348
  18.8 1.9 reduce.9
  20.7 0.7 reshape.385
  21.5 7.1 %all-to-all-start.1 = ((bf16[8,2,6144]{2,1,0:T(2,128)(2,1)}), bf16[8,2,6144]{2,1,0:T(2,128)(2,1)S(1)}, u32[]{:S(2)}, u32[]{:S(2)}) async-start(bf16[8,2,6144]{2,1,0:T(2,128)(2,1)} %reshape.385), calls=%async_computation.1 | async-start | bytes 393216 | tf_op jit(solution)/shard_map/all_to_all | solution.py:113
  28.6 0.2 dynamic-slice_reduce_fusion
  28.9 0.7 compare_and_fusion
  29.7 0.2 fusion.9
  30.1 8.4 %all-to-all-done.1 = bf16[8,2,6144]{2,1,0:T(2,128)(2,1)S(1)} async-done(((bf16[8,2,6144]{2,1,0:T(2,128)(2,1)}), bf16[8,2,6144]{2,1,0:T(2,128)(2,1)S(1)}, u32[]{:S(2)}, u32[]{:S(2)}) %all-to-all-start.1) | async-done | bytes 196640 | tf_op jit(solution)/shard_map/all_to_all | solution.py:113
  38.7 67.2 %all-gather.3.cloned.1.call-done = bf16[1,1536,3072]{2,1,0:T(8,128)(2,1)} async-done(((bf16[1,24,3072]{2,1,0:T(8,128)(2,1)}), bf16[1,1536,3072]{2,1,0:T(8,128)(2,1)}) %all-gather.3.cloned.1.call-update) | async-done | bytes 9437200 | tf_op jit(solution)/shard_map/all_gather | solution.py:129
  105.9 2.2 %slice_bitcast_fusion.1 = bf16[768,2304]{1,0:T(8,128)(2,1)S(1)} fusion(bf16[2,768,3072]{2,1,0:T(8,128)(2,1)} %bitcast.128), kind=kLoop, calls=%fused_computation.2 | loop fusion | bytes 7077888 | tf_op jit(solution)/shard_map/squeeze | solution.py:133
  108.2 0.3 fusion.14
  108.5 1.1 convolution_convert_fusion.1
  109.8 0.3 copy.92
  110.1 0.3 copy.90
  110.5 0.7 fusion.4
  111.2 0.7 convolution_convert_fusion.6
  111.9 0.6 copy-done.5
  112.6 1.6 fusion.25
  114.2 0.3 copy.140
  114.5 1.9 reduce.8
  116.4 0.7 reshape.383
  117.1 6.7 %all-to-all-start = ((bf16[8,2,6144]{2,1,0:T(2,128)(2,1)}), bf16[8,2,6144]{2,1,0:T(2,128)(2,1)S(1)}, u32[]{:S(2)}, u32[]{:S(2)}) async-start(bf16[8,2,6144]{2,1,0:T(2,128)(2,1)} %reshape.383), calls=%async_computation | async-start | bytes 393216 | tf_op jit(solution)/shard_map/all_to_all | solution.py:113
  123.9 1.8 fusion.24
  125.7 0.3 reshape_reshape.7
  126.0 0.4 copy.101
  126.5 1.2 copy.118
  127.6 7.1 %all-to-all-done = bf16[8,2,6144]{2,1,0:T(2,128)(2,1)S(1)} async-done(((bf16[8,2,6144]{2,1,0:T(2,128)(2,1)}), bf16[8,2,6144]{2,1,0:T(2,128)(2,1)S(1)}, u32[]{:S(2)}, u32[]{:S(2)}) %all-to-all-start) | async-done | bytes 196640 | tf_op jit(solution)/shard_map/all_to_all | solution.py:113
  135.3 2.7 %convolution_convert_fusion = bf16[8,16,2304]{2,1,0:T(8,128)(2,1)S(1)} fusion(bf16[8,16,768]{2,1,0:T(8,128)(2,1)S(1)} %bitcast.171, bf16[2,768,3072]{2,1,0:T(8,128)(2,1)} %bitcast.131), kind=kOutput, calls=%fused_computation | convolution fusion | flops 453279744 | bytes 4325376 | tf_op jit(solution)/shard_map/dot_general | solution.py:158
  138.4 1.9 fusion.7
  140.3 0.4 fusion.50
  140.9 2.5 %fusion.23 = bf16[128,12,64]{0,2,1:T(8,128)(2,1)} fusion(bf16[128,12,64]{0,2,1:T(8,128)(2,1)S(1)} %copy.101, f32[12,128,128]{1,2,0:T(8,128)} %fusion.7), kind=kOutput, calls=%fused_computation.47 | convolution fusion | flops 25659008 | bytes 1179648 | tf_op jit(solution)/shard_map/gst,sgh->tgh/dot_general | solution.py:102
  143.4 2.5 %multiply_reduce_fusion = (f32[12,128]{1,0:T(8,128)S(1)}, bf16[12,64,128]{2,1,0:T(8,128)(2,1)}) fusion(f32[12,128,64]{1,2,0:T(8,128)} %copy.118, bf16[128,12,64]{0,2,1:T(8,128)(2,1)S(1)} %bitcast.160, f32[12,128,128]{1,2,0:T(8,128)} %fusion.7), kind=kOutput, calls=%fused_computation.80 | convolution fusion | flops 25952384 | bytes 1579008 | tf_op jit(solution)/shard_map/gst,tgh->sgh/dot_general | solution.py:65
  145.8 0.3 fusion.8
  146.1 0.4 fusion.21
  146.5 0.2 fusion.22
  146.8 1.4 copy.99
  148.1 0.3 reshape_reshape.6
  148.4 1.4 copy.109
  149.8 0.3 convert_element_type.170
  150.1 0.4 copy.104
  150.6 0.3 concatenate.29
  150.9 0.4 copy.106
  151.3 0.3 convert_element_type.167
  151.6 1.6 fusion.18
  153.2 3.4 %multiply_reduce_fusion.1 = (f32[8,16]{1,0:T(8,128)S(1)}, f32[8,16,768]{2,1,0:T(8,128)S(1)}) fusion(f32[8,16,768]{2,1,0:T(8,128)S(1)} %bitcast.137, bf16[2,768,3072]{2,1,0:T(8,128)(2,1)} %bitcast.133, bf16[8,16,768]{2,1,0:T(8,128)(2,1)S(1)} %convert_element_type.170, bf16[8,16,768]{2,1,0:T(8,128)(2,1)S(1)} %convert_element_type.167, ...), kind=kOutput, calls=%fused_computation.82 | convolution fusion | flops 454950784 | bytes 4915712 | tf_op jit(solution)/shard_map/dot_general | solution.py:191
  156.9 16.2 %all_to_all.30 = bf16[8,16,1536]{2,1,0:T(8,128)(2,1)S(1)} all-to-all(bf16[8,16,1536]{2,1,0:T(8,128)(2,1)S(1)} %pad_maximum_fusion.2), channel_id=1, replica_groups=mesh['frame'=8,'space'=32,'dp'=2] {'frame'}, dimensions={0} | all-to-all | bytes 786432 | tf_op jit(solution)/shard_map/all_to_all | solution.py:117
  173.1 1.8 convolution_convert_fusion.2
  175.2 2.5 %fusion.39 = f32[12,64,384]{2,1,0:T(8,128)S(1)} fusion(bf16[128,12,64]{0,2,1:T(8,128)(2,1)S(1)} %bitcast.165, f32[12,128,384]{2,1,0:T(8,128)} %copy-done.5, f32[12,128]{1,0:T(8,128)S(1)} %copy-done.8, pred[384]{0:T(512)(128)(4,1)S(1)} %broadcast_bitcast_fusion), kind=kOutput, calls=%fused_computation.67 | convolution fusion | flops 77856768 | bytes 3742080 | tf_op jit(solution)/shard_map/gst,sgh->tgh/dot_general | solution.py:102
  177.7 1.0 multiply_convert_fusion
  178.7 0.4 convolution_multiply_fusion
  179.2 4.8 %collective-permute-start.2 = (bf16[128,1536]{0,1:T(8,128)(2,1)S(1)}, bf16[128,1536]{0,1:T(8,128)(2,1)S(1)}, u32[]{:S(2)}, u32[]{:S(2)}) collective-permute-start(bf16[128,1536]{0,1:T(8,128)(2,1)S(1)} %get-tuple-element.4), channel_id=1, source_target_pairs={{0,2},{2,4},{4,6},{6,8},{8,10},{10,12},{12,14},{14,16},{16,18},{18... | collective-permute-start | bytes 1179656 | tf_op jit(solution)/shard_map/ppermute | solution.py:22
  184.0 1.9 collective-permute-start.3
  185.9 0.7 slice_bitcast_fusion.10
  186.6 0.6 fusion.13
  187.3 2.5 %collective-permute-done.2 = bf16[128,1536]{0,1:T(8,128)(2,1)S(1)} collective-permute-done((bf16[128,1536]{0,1:T(8,128)(2,1)S(1)}, bf16[128,1536]{0,1:T(8,128)(2,1)S(1)}, u32[]{:S(2)}, u32[]{:S(2)}) %collective-permute-start.2) | collective-permute-done | bytes 393248 | tf_op jit(solution)/shard_map/ppermute | solution.py:22
  189.7 6.2 %collective-permute-done.3 = bf16[128,1536]{0,1:T(8,128)(2,1)S(1)} collective-permute-done((bf16[128,1536]{0,1:T(8,128)(2,1)S(1)}, bf16[128,1536]{0,1:T(8,128)(2,1)S(1)}, u32[]{:S(2)}, u32[]{:S(2)}) %collective-permute-start.3) | collective-permute-done | bytes 393248 | tf_op jit(solution)/shard_map/ppermute | solution.py:24
  196.0 0.2 fusion.29
  196.1 3.4 %fusion.42 = (f32[128]{0:T(128)S(1)}, f32[128]{0:T(128)S(1)}, f32[128,768]{1,0:T(8,128)S(1)}) fusion(bf16[1,128,768]{2,1,0:T(8,128)(2,1)S(1)} %copy-done.1, bf16[2,768,3072]{2,1,0:T(8,128)(2,1)} %bitcast.135, bf16[128,1536]{0,1:T(8,128)(2,1)S(1)} %fusion.29, bf16[128,768]{0,1:T(8,128)(2,1)S(1)} %bitcast.172), kind=kOutput, calls=%fused_computation.71 | convolution fusion | flops 454655744 | bytes 4719616 | tf_op jit(solution)/shard_map/dot_general | solution.py:215
  199.6 0.9 fusion.51
  (52 shorter events, 2.7 us)
Async XLA Ops:
  7.2 21.4 %copy-start = (s32[32,4]{0,1:T(4,128)S(1)}, s32[32,4]{0,1:T(4,128)}, u32[]{:S(2)}) copy-start(s32[32,4]{0,1:T(4,128)} %param.13) | copy-start | bytes 1540
  7.2 22.5 %copy-start.1 = (bf16[1,128,768]{2,1,0:T(8,128)(2,1)S(1)}, bf16[1,128,768]{2,1,0:T(8,128)(2,1)}, u32[]{:S(2)}) copy-start(bf16[1,128,768]{2,1,0:T(8,128)(2,1)} %param.7) | copy-start | bytes 589828
  7.2 98.7 %all-gather.3.cloned.1.call-start = ((), (), s32[]{:S(2)}) async-start(), calls=%async_computation.3 | async-start | bytes 9584640 | tf_op jit(solution)/shard_map/all_gather | solution.py:129
  9.1 20.6 %collective-permute-start.1 = (bf16[128,768]{1,0:T(8,128)(2,1)}, bf16[128,768]{1,0:T(8,128)(2,1)S(1)}, u32[]{:S(2)}, u32[]{:S(2)}) collective-permute-start(bf16[128,768]{1,0:T(8,128)(2,1)} %bitcast.139), channel_id=1, source_target_pairs={{2,0},{4,2},{6,4},{8,6},{10,8},{12,10},{14,12},{16,14},{18,16},{20... | collective-permute-start | bytes 589832 | tf_op jit(solution)/shard_map/ppermute | solution.py:24
  11.8 17.9 %collective-permute-start = (bf16[128,768]{1,0:T(8,128)(2,1)}, bf16[128,768]{1,0:T(8,128)(2,1)S(1)}, u32[]{:S(2)}, u32[]{:S(2)}) collective-permute-start(bf16[128,768]{1,0:T(8,128)(2,1)} %bitcast.140), channel_id=1, source_target_pairs={{0,2},{2,4},{4,6},{6,8},{8,10},{10,12},{12,14},{14,16},{16,18},{18... | collective-permute-start | bytes 589832 | tf_op jit(solution)/shard_map/ppermute | solution.py:22
  21.5 17.0 %all-to-all-start.1 = ((bf16[8,2,6144]{2,1,0:T(2,128)(2,1)}), bf16[8,2,6144]{2,1,0:T(2,128)(2,1)S(1)}, u32[]{:S(2)}, u32[]{:S(2)}) async-start(bf16[8,2,6144]{2,1,0:T(2,128)(2,1)} %reshape.385), calls=%async_computation.1 | async-start | bytes 393216 | tf_op jit(solution)/shard_map/all_to_all | solution.py:113
  110.5 1.5 copy-start.2
  111.2 1.4 copy-start.5
  111.2 1.4 copy-start.7
  117.1 17.6 %all-to-all-start = ((bf16[8,2,6144]{2,1,0:T(2,128)(2,1)}), bf16[8,2,6144]{2,1,0:T(2,128)(2,1)S(1)}, u32[]{:S(2)}, u32[]{:S(2)}) async-start(bf16[8,2,6144]{2,1,0:T(2,128)(2,1)} %reshape.383), calls=%async_computation | async-start | bytes 393216 | tf_op jit(solution)/shard_map/all_to_all | solution.py:113
  138.0 2.3 %copy-start.4 = (pred[128,128]{0,1:T(8,128)(4,1)S(1)}, pred[128,128]{0,1:T(8,128)(4,1)}, u32[]{:S(2)}) copy-start(pred[128,128]{0,1:T(8,128)(4,1)} %compare_and_fusion) | copy-start | bytes 49156
  156.8 18.3 %copy-start.8 = (f32[12,128]{1,0:T(8,128)S(1)}, f32[12,128]{1,0:T(8,128)}, u32[]{:S(2)}) copy-start(f32[12,128]{1,0:T(8,128)} %copy-done.7) | copy-start | bytes 18436
  175.1 2.5 %copy-start.3 = (bf16[384,768]{0,1:T(8,128)(2,1)S(1)}, bf16[384,768]{0,1:T(8,128)(2,1)}, u32[]{:S(2)}) copy-start(bf16[384,768]{0,1:T(8,128)(2,1)} %copy-done.2) | copy-start | bytes 1769476
  175.1 2.6 %copy-start.6 = (f32[12,128,384]{2,1,0:T(8,128)S(1)}, f32[12,128,384]{2,1,0:T(8,128)}, u32[]{:S(2)}) copy-start(f32[12,128,384]{2,1,0:T(8,128)} %copy-done.5) | copy-start | bytes 7077892
  179.2 10.5 %collective-permute-start.2 = (bf16[128,1536]{0,1:T(8,128)(2,1)S(1)}, bf16[128,1536]{0,1:T(8,128)(2,1)S(1)}, u32[]{:S(2)}, u32[]{:S(2)}) collective-permute-start(bf16[128,1536]{0,1:T(8,128)(2,1)S(1)} %get-tuple-element.4), channel_id=1, source_target_pairs={{0,2},{2,4},{4,6},{6,8},{8,10},{10,12},{12,14},{14,16},{16,18},{18... | collective-permute-start | bytes 1179656 | tf_op jit(solution)/shard_map/ppermute | solution.py:22
  184.0 12.0 %collective-permute-start.3 = (bf16[128,1536]{0,1:T(8,128)(2,1)S(1)}, bf16[128,1536]{0,1:T(8,128)(2,1)S(1)}, u32[]{:S(2)}, u32[]{:S(2)}) collective-permute-start(bf16[128,1536]{0,1:T(8,128)(2,1)S(1)} %get-tuple-element.5), channel_id=1, source_target_pairs={{2,0},{4,2},{6,4},{8,6},{10,8},{12,10},{14,12},{16,14},{18,16},{20... | collective-permute-start | bytes 1179656 | tf_op jit(solution)/shard_map/ppermute | solution.py:24
Sparse Core Ops, SparseCore 0:
  11.9 93.9 all-gather.2

commit v6 on v5

--- a/solution.py
+++ b/solution.py
@@ -172,6 +172,7 @@
     attended_time = attended_flat.reshape(frame_count, position_count, feature_count)
     update_time = jnp.dot(attended_time, full_out_time, preferred_element_type=jnp.float32)
     frames_out_rows = (stream_rows.astype(jnp.float32) + update_time).astype(jnp.bfloat16)
+    frames_out = to_space(frames_out_rows)
     grad_att_time = jnp.dot(cot_rows, full_out_time.T, preferred_element_type=jnp.float32).astype(
         jnp.bfloat16
     )
@@ -192,9 +193,7 @@
     grad_stream_rows = (
         cot_rows.astype(jnp.float32) + rms_back(stream_rows, grad_normed_time)
     ).astype(jnp.bfloat16)
-    back_rows = to_space(jnp.concatenate([frames_out_rows, grad_stream_rows], axis=-1))
-    frames_out = back_rows[:, :feature_count]
-    grad_stream = back_rows[:, feature_count:]
+    grad_stream = to_space(grad_stream_rows)
     grad_attended = jnp.dot(
         grad_stream, full_out_space.T, preferred_element_type=jnp.float32
     ).astype(jnp.bfloat16)

time: 208 us -> 206 us (level)
  blocking collectives: 16.2 us -> 0 us
  starting transfers between devices: 28.5 us -> 35.9 us
  waiting for transfers between devices: 91.5 us -> 97.8 us
  matrix products: 31.8 us -> 29.5 us
    all_to_all x1 -> x0, blocking collectives: 16.2 us -> none  [to_space(): lax.all_to_all(frame_rows, 'frame', split_axis=0, concat_axis=1, tiled=True)]
    all_to_all x0 -> x2, starting transfers between devices: none -> 7.41 us  [to_space(): lax.all_to_all(frame_rows, 'frame', split_axis=0, concat_axis=1, tiled=True)]
    all_to_all x0 -> x2, waiting for transfers between devices: none -> 6.66 us  [to_space(): lax.all_to_all(frame_rows, 'frame', split_axis=0, concat_axis=1, tiled=True)]
    unnamed x26 -> x39, local copies, waits for them, and re-layouts: 5.53 us -> 7.46 us
  transfers between devices with their start and end apart: 7 -> 9, of which waited for: 5 -> 6; matrix products, arithmetic and copies ran while one was open for 5% -> 11% of each run, Pallas kernels for 0% -> 0%
where the time goes in v6:
time: 206 us; the launch traced here: 205 us
  waiting for transfers between devices  97.8 us (47%)
  starting transfers between devices  35.9 us (17%)
  matrix products  29.5 us (14%)
  local copies, waits for them, and re-layouts  17.1 us (8%)
  between operations  14.6 us (7%)
  other arithmetic  10.2 us (5%)
    all_gather x1, waiting for transfers between devices, local(): lax.all_gather(mine, ('dp', 'space'), axis=0, tiled=True)  67.2 us
    all_to_all x2, waiting for transfers between devices, to_frames(): lax.all_to_all(local_rows[None], 'frame', split_axis=1, concat_axis=0, ti...  14.9 us
    all_to_all x2, starting transfers between devices, to_frames(): lax.all_to_all(local_rows[None], 'frame', split_axis=1, concat_axis=0, ti...  13.8 us
    ppermute x2, starting transfers between devices, padded(): lax.ppermute(tail, axis, [(i, (i + 1) % count) for i in range(ends)])  9.98 us
    unnamed x39, local copies, waits for them, and re-layouts  7.46 us
    all_to_all x2, starting transfers between devices, to_space(): lax.all_to_all(frame_rows, 'frame', split_axis=0, concat_axis=1, tiled=True)  7.41 us
    all_to_all x2, waiting for transfers between devices, to_space(): lax.all_to_all(frame_rows, 'frame', split_axis=0, concat_axis=1, tiled=True)  6.66 us
    ppermute x2, waiting for transfers between devices, padded(): lax.ppermute(head, axis, [((i + 1) % count, i) for i in range(ends)])  6.23 us
  transfers between devices with their start and end apart: 9, of which 6 were waited for; matrix products, arithmetic and copies ran while one was open for 11% of the time, Pallas kernels for 0%

profile of v6, /device:TPU:6, one launch (start us, length us, event | category | flops | bytes accessed | tf_op | source)
XLA Modules:
  0.0 205.2 jit_solution(17224859431540948908)
XLA Ops:
  7.2 1.0 maximum_bitcast_fusion
  8.3 0.7 fusion.55
  9.1 2.7 %collective-permute-start.1 = (bf16[128,768]{1,0:T(8,128)(2,1)}, bf16[128,768]{1,0:T(8,128)(2,1)S(1)}, u32[]{:S(2)}, u32[]{:S(2)}) collective-permute-start(bf16[128,768]{1,0:T(8,128)(2,1)} %bitcast.140), channel_id=1, source_target_pairs={{2,0},{4,2},{6,4},{8,6},{10,8},{12,10},{14,12},{16,14},{18,16},{20... | collective-permute-start | bytes 589832 | tf_op jit(solution)/shard_map/ppermute | solution.py:24
  11.8 5.2 %collective-permute-start = (bf16[128,768]{1,0:T(8,128)(2,1)}, bf16[128,768]{1,0:T(8,128)(2,1)S(1)}, u32[]{:S(2)}, u32[]{:S(2)}) collective-permute-start(bf16[128,768]{1,0:T(8,128)(2,1)} %bitcast.141), channel_id=1, source_target_pairs={{0,2},{2,4},{4,6},{6,8},{8,10},{10,12},{12,14},{14,16},{16,18},{18... | collective-permute-start | bytes 589832 | tf_op jit(solution)/shard_map/ppermute | solution.py:22
  17.0 1.2 copy.139
  18.3 0.6 broadcast.348
  18.8 1.9 reduce.9
  20.7 0.7 reshape.388
  21.4 7.1 %all-to-all-start.2 = ((bf16[8,2,6144]{2,1,0:T(2,128)(2,1)}), bf16[8,2,6144]{2,1,0:T(2,128)(2,1)S(1)}, u32[]{:S(2)}, u32[]{:S(2)}) async-start(bf16[8,2,6144]{2,1,0:T(2,128)(2,1)} %reshape.388), calls=%async_computation.2 | async-start | bytes 393216 | tf_op jit(solution)/shard_map/all_to_all | solution.py:113
  28.8 0.7 compare_and_fusion
  30.0 8.4 %all-to-all-done.2 = bf16[8,2,6144]{2,1,0:T(2,128)(2,1)S(1)} async-done(((bf16[8,2,6144]{2,1,0:T(2,128)(2,1)}), bf16[8,2,6144]{2,1,0:T(2,128)(2,1)S(1)}, u32[]{:S(2)}, u32[]{:S(2)}) %all-to-all-start.2) | async-done | bytes 196640 | tf_op jit(solution)/shard_map/all_to_all | solution.py:113
  38.7 67.2 %all-gather.3.cloned.1.call-done = bf16[1,1536,3072]{2,1,0:T(8,128)(2,1)} async-done(((bf16[1,24,3072]{2,1,0:T(8,128)(2,1)}), bf16[1,1536,3072]{2,1,0:T(8,128)(2,1)}) %all-gather.3.cloned.1.call-update) | async-done | bytes 9437200 | tf_op jit(solution)/shard_map/all_gather | solution.py:129
  105.9 2.2 %slice_bitcast_fusion.1 = bf16[768,2304]{1,0:T(8,128)(2,1)S(1)} fusion(bf16[2,768,3072]{2,1,0:T(8,128)(2,1)} %bitcast.129), kind=kLoop, calls=%fused_computation.2 | loop fusion | bytes 7077888 | tf_op jit(solution)/shard_map/squeeze | solution.py:133
  108.1 0.3 fusion.14
  108.5 1.1 convolution_convert_fusion.1
  109.8 0.3 copy.92
  110.1 0.3 copy.90
  110.5 0.7 fusion.4
  111.2 0.7 convolution_convert_fusion.6
  111.9 0.6 copy-done.13
  112.6 1.6 fusion.25
  114.2 0.3 copy.140
  114.5 1.9 reduce.8
  116.4 0.7 reshape.386
  117.1 6.7 %all-to-all-start = ((bf16[8,2,6144]{2,1,0:T(2,128)(2,1)}), bf16[8,2,6144]{2,1,0:T(2,128)(2,1)S(1)}, u32[]{:S(2)}, u32[]{:S(2)}) async-start(bf16[8,2,6144]{2,1,0:T(2,128)(2,1)} %reshape.386), calls=%async_computation | async-start | bytes 393216 | tf_op jit(solution)/shard_map/all_to_all | solution.py:113
  123.9 1.8 fusion.24
  125.7 0.3 reshape_reshape.7
  126.0 1.1 copy.101
  127.1 1.1 copy.118
  128.3 6.5 %all-to-all-done = bf16[8,2,6144]{2,1,0:T(2,128)(2,1)S(1)} async-done(((bf16[8,2,6144]{2,1,0:T(2,128)(2,1)}), bf16[8,2,6144]{2,1,0:T(2,128)(2,1)S(1)}, u32[]{:S(2)}, u32[]{:S(2)}) %all-to-all-start) | async-done | bytes 196640 | tf_op jit(solution)/shard_map/all_to_all | solution.py:113
  135.3 2.7 %convolution_convert_fusion = bf16[8,16,2304]{2,1,0:T(8,128)(2,1)S(1)} fusion(bf16[8,16,768]{2,1,0:T(8,128)(2,1)S(1)} %bitcast.170, bf16[2,768,3072]{2,1,0:T(8,128)(2,1)} %bitcast.132), kind=kOutput, calls=%fused_computation | convolution fusion | flops 453279744 | bytes 4325376 | tf_op jit(solution)/shard_map/dot_general | solution.py:158
  138.4 0.3 fusion.7
  138.7 0.4 fusion.50
  139.3 0.3 copy-done.6
  139.6 1.1 fusion.23
  140.7 1.3 multiply_reduce_fusion
  142.0 0.3 fusion.8
  142.3 0.4 fusion.21
  143.0 0.4 copy.109
  143.4 0.3 convert_element_type.170
  143.7 0.4 copy.104
  144.4 0.4 copy.106
  144.9 0.3 convert_element_type.167
  145.2 3.4 %multiply_reduce_fusion.1 = (f32[8,16]{1,0:T(8,128)S(1)}, f32[8,16,768]{2,1,0:T(8,128)S(1)}) fusion(f32[8,16,768]{2,1,0:T(8,128)S(1)} %bitcast.137, bf16[2,768,3072]{2,1,0:T(8,128)(2,1)} %bitcast.133, bf16[8,16,768]{2,1,0:T(8,128)(2,1)S(1)} %convert_element_type.170, bf16[8,16,768]{2,1,0:T(8,128)(2,1)S(1)} %convert_element_type.167, ...), kind=kOutput, calls=%fused_computation.81 | convolution fusion | flops 454950784 | bytes 4915712 | tf_op jit(solution)/shard_map/dot_general | solution.py:192
  148.6 0.9 add_convert_fusion
  149.4 3.4 %all-to-all-start.3 = ((bf16[8,16,768]{2,1,0:T(8,128)(2,1)}), bf16[8,16,768]{2,1,0:T(8,128)(2,1)S(1)}, u32[]{:S(2)}, u32[]{:S(2)}) async-start(bf16[8,16,768]{2,1,0:T(8,128)(2,1)} %add_convert_fusion), calls=%async_computation.3 | async-start | bytes 393216 | tf_op jit(solution)/shard_map/all_to_all | solution.py:117
  152.8 0.4 copy.99
  153.5 2.3 %fusion.18 = bf16[8,16,768]{2,1,0:T(8,128)(2,1)} fusion(f32[8,16,768]{2,1,0:T(8,128)S(1)} %bitcast.139, bf16[8,16,768]{2,1,0:T(8,128)(2,1)S(1)} %reshape_reshape.6, bf16[2,768,3072]{2,1,0:T(8,128)(2,1)} %bitcast.134), kind=kOutput, calls=%fused_computation.37 | convolution fusion | flops 151191552 | bytes 1966080 | tf_op jit(solution)/shard_map/dot_general | solution.py:173
  155.8 6.7 %all-to-all-done.3 = bf16[8,16,768]{2,1,0:T(8,128)(2,1)S(1)} async-done(((bf16[8,16,768]{2,1,0:T(8,128)(2,1)}), bf16[8,16,768]{2,1,0:T(8,128)(2,1)S(1)}, u32[]{:S(2)}, u32[]{:S(2)}) %all-to-all-start.3) | async-done | bytes 196640 | tf_op jit(solution)/shard_map/all_to_all | solution.py:117
  162.5 4.0 %all-to-all-start.1 = ((bf16[8,16,768]{2,1,0:T(8,128)(2,1)}), bf16[8,16,768]{2,1,0:T(8,128)(2,1)}, u32[]{:S(2)}, u32[]{:S(2)}) async-start(bf16[8,16,768]{2,1,0:T(8,128)(2,1)} %fusion.18), calls=%async_computation.1 | async-start | bytes 393216 | tf_op jit(solution)/shard_map/all_to_all | solution.py:117
  166.5 1.8 convolution_convert_fusion.2
  168.6 2.5 %fusion.39 = f32[12,64,384]{2,1,0:T(8,128)S(1)} fusion(bf16[128,12,64]{0,2,1:T(8,128)(2,1)S(1)} %bitcast.163, f32[12,128,384]{2,1,0:T(8,128)} %copy-done.13, f32[12,128]{1,0:T(8,128)S(1)} %get-tuple-element.13, pred[384]{0:T(512)(128)(4,1)S(1)} %broadcast_bitcast_fusion), kind=kOutput, calls=%fused_computation.67 | convolution fusion | flops 77856768 | bytes 3742080 | tf_op jit(solution)/shard_map/gst,sgh->tgh/dot_general | solution.py:102
  171.2 1.0 multiply_convert_fusion
  172.2 0.4 convolution_multiply_fusion
  172.7 0.9 fusion.64
  173.6 4.8 %collective-permute-start.2 = (bf16[128,1536]{0,1:T(8,128)(2,1)}, bf16[128,1536]{0,1:T(8,128)(2,1)}, u32[]{:S(2)}, u32[]{:S(2)}) collective-permute-start(bf16[128,1536]{0,1:T(8,128)(2,1)} %get-tuple-element.4), channel_id=1, source_target_pairs={{0,2},{2,4},{4,6},{6,8},{8,10},{10,12},{12,14},{14,16},{16,18},{18... | collective-permute-start | bytes 1179656 | tf_op jit(solution)/shard_map/ppermute | solution.py:22
  178.4 1.9 collective-permute-start.3
  180.3 1.8 fusion.13
  182.1 2.8 %collective-permute-done.2 = bf16[128,1536]{0,1:T(8,128)(2,1)} collective-permute-done((bf16[128,1536]{0,1:T(8,128)(2,1)}, bf16[128,1536]{0,1:T(8,128)(2,1)}, u32[]{:S(2)}, u32[]{:S(2)}) %collective-permute-start.2) | collective-permute-done | bytes 393248 | tf_op jit(solution)/shard_map/ppermute | solution.py:22
  184.8 6.2 %collective-permute-done.3 = bf16[128,1536]{0,1:T(8,128)(2,1)} collective-permute-done((bf16[128,1536]{0,1:T(8,128)(2,1)}, bf16[128,1536]{0,1:T(8,128)(2,1)}, u32[]{:S(2)}, u32[]{:S(2)}) %collective-permute-start.3) | collective-permute-done | bytes 393248 | tf_op jit(solution)/shard_map/ppermute | solution.py:24
  191.1 1.3 fusion.29
  192.4 3.4 %fusion.42 = (f32[128]{0:T(128)S(1)}, f32[128]{0:T(128)S(1)}, f32[128,768]{1,0:T(8,128)S(1)}) fusion(bf16[1,128,768]{2,1,0:T(8,128)(2,1)S(1)} %copy-done.2, bf16[2,768,3072]{2,1,0:T(8,128)(2,1)} %bitcast.136, bf16[128,1536]{0,1:T(8,128)(2,1)S(1)} %fusion.29, bf16[128,768]{0,1:T(8,128)(2,1)S(1)} %bitcast.171), kind=kOutput, calls=%fused_computation.71 | convolution fusion | flops 454655744 | bytes 4719616 | tf_op jit(solution)/shard_map/dot_general | solution.py:214
  195.9 0.9 fusion.51
  196.7 1.6 copy.142
  (66 shorter events, 3.7 us)
Async XLA Ops:
  7.2 21.4 %copy-start = (s32[32,4]{0,1:T(4,128)S(1)}, s32[32,4]{0,1:T(4,128)}, u32[]{:S(2)}) copy-start(s32[32,4]{0,1:T(4,128)} %param.13) | copy-start | bytes 1540
  7.2 22.4 %copy-start.1 = (bf16[1,128,768]{2,1,0:T(8,128)(2,1)S(1)}, bf16[1,128,768]{2,1,0:T(8,128)(2,1)}, u32[]{:S(2)}) copy-start(bf16[1,128,768]{2,1,0:T(8,128)(2,1)} %param.7) | copy-start | bytes 589828
  7.2 98.7 %all-gather.3.cloned.1.call-start = ((), (), s32[]{:S(2)}) async-start(), calls=%async_computation.4 | async-start | bytes 9584640 | tf_op jit(solution)/shard_map/all_gather | solution.py:129
  9.1 20.6 %collective-permute-start.1 = (bf16[128,768]{1,0:T(8,128)(2,1)}, bf16[128,768]{1,0:T(8,128)(2,1)S(1)}, u32[]{:S(2)}, u32[]{:S(2)}) collective-permute-start(bf16[128,768]{1,0:T(8,128)(2,1)} %bitcast.140), channel_id=1, source_target_pairs={{2,0},{4,2},{6,4},{8,6},{10,8},{12,10},{14,12},{16,14},{18,16},{20... | collective-permute-start | bytes 589832 | tf_op jit(solution)/shard_map/ppermute | solution.py:24
  11.8 17.8 %collective-permute-start = (bf16[128,768]{1,0:T(8,128)(2,1)}, bf16[128,768]{1,0:T(8,128)(2,1)S(1)}, u32[]{:S(2)}, u32[]{:S(2)}) collective-permute-start(bf16[128,768]{1,0:T(8,128)(2,1)} %bitcast.141), channel_id=1, source_target_pairs={{0,2},{2,4},{4,6},{6,8},{8,10},{10,12},{12,14},{14,16},{16,18},{18... | collective-permute-start | bytes 589832 | tf_op jit(solution)/shard_map/ppermute | solution.py:22
  21.4 17.0 %all-to-all-start.2 = ((bf16[8,2,6144]{2,1,0:T(2,128)(2,1)}), bf16[8,2,6144]{2,1,0:T(2,128)(2,1)S(1)}, u32[]{:S(2)}, u32[]{:S(2)}) async-start(bf16[8,2,6144]{2,1,0:T(2,128)(2,1)} %reshape.388), calls=%async_computation.2 | async-start | bytes 393216 | tf_op jit(solution)/shard_map/all_to_all | solution.py:113
  109.7 0.7 copy-start.4
  110.1 1.8 copy-start.3
  110.4 1.5 copy-start.9
  111.2 1.4 copy-start.13
  117.1 17.6 %all-to-all-start = ((bf16[8,2,6144]{2,1,0:T(2,128)(2,1)}), bf16[8,2,6144]{2,1,0:T(2,128)(2,1)S(1)}, u32[]{:S(2)}, u32[]{:S(2)}) async-start(bf16[8,2,6144]{2,1,0:T(2,128)(2,1)} %reshape.386), calls=%async_computation | async-start | bytes 393216 | tf_op jit(solution)/shard_map/all_to_all | solution.py:113
  135.3 3.1 %copy-start.12 = (pred[128,128]{0,1:T(8,128)(4,1)S(1)}, pred[128,128]{0,1:T(8,128)(4,1)}, u32[]{:S(2)}) copy-start(pred[128,128]{0,1:T(8,128)(4,1)} %compare_and_fusion) | copy-start | bytes 49156
  138.7 0.9 copy-start.6
  142.0 1.0 copy-start.11
  149.4 13.1 %all-to-all-start.3 = ((bf16[8,16,768]{2,1,0:T(8,128)(2,1)}), bf16[8,16,768]{2,1,0:T(8,128)(2,1)S(1)}, u32[]{:S(2)}, u32[]{:S(2)}) async-start(bf16[8,16,768]{2,1,0:T(8,128)(2,1)} %add_convert_fusion), calls=%async_computation.3 | async-start | bytes 393216 | tf_op jit(solution)/shard_map/all_to_all | solution.py:117
  162.5 6.1 %copy-start.7 = (bf16[8,16,768]{2,1,0:T(8,128)(2,1)}, bf16[8,16,768]{2,1,0:T(8,128)(2,1)S(1)}, u32[]{:S(2)}) copy-start(bf16[8,16,768]{2,1,0:T(8,128)(2,1)S(1)} %all-to-all-done.3) | copy-start | bytes 589828
  162.5 17.8 %all-to-all-start.1 = ((bf16[8,16,768]{2,1,0:T(8,128)(2,1)}), bf16[8,16,768]{2,1,0:T(8,128)(2,1)}, u32[]{:S(2)}, u32[]{:S(2)}) async-start(bf16[8,16,768]{2,1,0:T(8,128)(2,1)} %fusion.18), calls=%async_computation.1 | async-start | bytes 393216 | tf_op jit(solution)/shard_map/all_to_all | solution.py:117
  168.6 2.5 %copy-start.10 = (bf16[384,768]{0,1:T(8,128)(2,1)S(1)}, bf16[384,768]{0,1:T(8,128)(2,1)}, u32[]{:S(2)}) copy-start(bf16[384,768]{0,1:T(8,128)(2,1)} %copy-done.9) | copy-start | bytes 1769476
  168.6 2.6 %copy-start.14 = (f32[12,128,384]{2,1,0:T(8,128)S(1)}, f32[12,128,384]{2,1,0:T(8,128)}, u32[]{:S(2)}) copy-start(f32[12,128,384]{2,1,0:T(8,128)} %copy-done.13) | copy-start | bytes 7077892
  171.2 1.0 copy-start.5
  173.6 11.2 %collective-permute-start.2 = (bf16[128,1536]{0,1:T(8,128)(2,1)}, bf16[128,1536]{0,1:T(8,128)(2,1)}, u32[]{:S(2)}, u32[]{:S(2)}) collective-permute-start(bf16[128,1536]{0,1:T(8,128)(2,1)} %get-tuple-element.4), channel_id=1, source_target_pairs={{0,2},{2,4},{4,6},{6,8},{8,10},{10,12},{12,14},{14,16},{16,18},{18... | collective-permute-start | bytes 1179656 | tf_op jit(solution)/shard_map/ppermute | solution.py:22
  178.4 12.7 %collective-permute-start.3 = (bf16[128,1536]{0,1:T(8,128)(2,1)}, bf16[128,1536]{0,1:T(8,128)(2,1)}, u32[]{:S(2)}, u32[]{:S(2)}) collective-permute-start(bf16[128,1536]{0,1:T(8,128)(2,1)} %get-tuple-element.5), channel_id=1, source_target_pairs={{2,0},{4,2},{6,4},{8,6},{10,8},{12,10},{14,12},{16,14},{18,16},{20... | collective-permute-start | bytes 1179656 | tf_op jit(solution)/shard_map/ppermute | solution.py:24
  180.3 12.0 %copy-start.2 = (bf16[1,128,768]{2,1,0:T(8,128)(2,1)S(1)}, bf16[1,128,768]{2,1,0:T(8,128)(2,1)}, u32[]{:S(2)}) copy-start(bf16[1,128,768]{2,1,0:T(8,128)(2,1)} %param.7) | copy-start | bytes 589828
  192.4 3.5 %copy-start.8 = (bf16[8,16,768]{2,1,0:T(8,128)(2,1)S(1)}, bf16[8,16,768]{2,1,0:T(8,128)(2,1)}, u32[]{:S(2)}) copy-start(bf16[8,16,768]{2,1,0:T(8,128)(2,1)} %copy-done.7) | copy-start | bytes 589828
Sparse Core Ops, SparseCore 0:
  11.9 93.9 all-gather.2

commit v7 on v6

--- a/solution.py
+++ b/solution.py
@@ -185,11 +185,20 @@
         attended_flat,
         grad_att_time.reshape(row_count, feature_count),
     )
-    gradients = jnp.concatenate(
-        [grad_query_time, grad_key_time.astype(jnp.bfloat16), grad_value_time.astype(jnp.bfloat16)],
-        axis=1,
-    ).reshape(frame_count, position_count, 3 * feature_count)
-    grad_normed_time = jnp.dot(gradients, full_qkv_time.T, preferred_element_type=jnp.float32)
+    grad_normed_flat = (
+        jnp.dot(grad_query_time, full_qkv_time[:, :feature_count].T, preferred_element_type=jnp.float32)
+        + jnp.dot(
+            grad_key_time.astype(jnp.bfloat16),
+            full_qkv_time[:, feature_count : 2 * feature_count].T,
+            preferred_element_type=jnp.float32,
+        )
+        + jnp.dot(
+            grad_value_time.astype(jnp.bfloat16),
+            full_qkv_time[:, 2 * feature_count :].T,
+            preferred_element_type=jnp.float32,
+        )
+    )
+    grad_normed_time = grad_normed_flat.reshape(frame_count, position_count, feature_count)
     grad_stream_rows = (
         cot_rows.astype(jnp.float32) + rms_back(stream_rows, grad_normed_time)
     ).astype(jnp.bfloat16)
@@ -210,8 +219,9 @@
         + kv_got[:shard].astype(jnp.float32)
         + kv_got[3 * shard :].astype(jnp.float32)
     ).astype(jnp.bfloat16)
-    grad_project = jnp.concatenate([grad_query, grad_kv], axis=1)
-    grad_normed = jnp.dot(grad_project, full_qkv_space.T, preferred_element_type=jnp.float32)
+    grad_normed = jnp.dot(
+        grad_query, full_qkv_space[:, :feature_count].T, preferred_element_type=jnp.float32
+    ) + jnp.dot(grad_kv, full_qkv_space[:, feature_count:].T, preferred_element_type=jnp.float32)
     grad_in = (grad_stream.astype(jnp.float32) + rms_back(local_in, grad_normed)).astype(
         jnp.bfloat16
     )

time: 206 us -> 251 us (1.22)
  local copies, waits for them, and re-layouts: 17.1 us -> 45.2 us
  matrix products: 29.5 us -> 43.3 us
  waiting for transfers between devices: 97.8 us -> 86.5 us
  other arithmetic: 10.2 us -> 19.5 us
  starting transfers between devices: 35.9 us -> 39.8 us
    all_to_all x2, waiting for transfers between devices: 14.9 us -> 7.59 us  [to_frames(): lax.all_to_all(local_rows[None], 'frame', split_axis=1, concat_axis=0, ti...]
    unnamed x39 -> x57, local copies, waits for them, and re-layouts: 7.46 us -> 12.4 us
    slice x2, local copies, waits for them, and re-layouts: 0.38 us -> 4.46 us  [local(): key_window = kv_window[:, :feature_count]]
    all_to_all x2, starting transfers between devices: 7.41 us -> 11.2 us  [to_space(): lax.all_to_all(frame_rows, 'frame', split_axis=0, concat_axis=1, tiled=True)]
    unnamed x3, other arithmetic: 3.81 us -> 7.33 us
    squeeze x1, local copies, waits for them, and re-layouts: 2.23 us -> 5.38 us  [local(): full_qkv_time = all_weights[1, :, :qkv_width]]
    dot_general x2, matrix products: 1.04 us -> 4.17 us  [space_attend(): jnp.einsum('sgh,tgh->gst', query_heads, key_heads, preferred_element_type...]
    all_to_all x2, waiting for transfers between devices: 6.66 us -> 3.73 us  [to_space(): lax.all_to_all(frame_rows, 'frame', split_axis=0, concat_axis=1, tiled=True)]
  transfers between devices with their start and end apart: 9 -> 9, of which waited for: 6 -> 5; matrix products, arithmetic and copies ran while one was open for 11% -> 15% of each run, Pallas kernels for 0% -> 0%
where the time goes in v7:
time: 251 us; the launch traced here: 249 us
  waiting for transfers between devices  86.5 us (34%)
  local copies, waits for them, and re-layouts  45.2 us (18%)
  matrix products  43.3 us (17%)
  starting transfers between devices  39.8 us (16%)
  other arithmetic  19.5 us (8%)
  between operations  14.5 us (6%)
    all_gather x1, waiting for transfers between devices, local(): lax.all_gather(mine, ('dp', 'space'), axis=0, tiled=True)  66.6 us
    all_to_all x2, starting transfers between devices, to_frames(): lax.all_to_all(local_rows[None], 'frame', split_axis=1, concat_axis=0, ti...  13.8 us
    unnamed x57, local copies, waits for them, and re-layouts  12.4 us
    all_to_all x2, starting transfers between devices, to_space(): lax.all_to_all(frame_rows, 'frame', split_axis=0, concat_axis=1, tiled=True)  11.2 us
    ppermute x2, starting transfers between devices, padded(): lax.ppermute(tail, axis, [(i, (i + 1) % count) for i in range(ends)])  9.99 us
    all_to_all x2, waiting for transfers between devices, to_frames(): lax.all_to_all(local_rows[None], 'frame', split_axis=1, concat_axis=0, ti...  7.59 us
    unnamed x3, other arithmetic  7.33 us
    ppermute x2, waiting for transfers between devices, padded(): lax.ppermute(head, axis, [((i + 1) % count, i) for i in range(ends)])  6.23 us
  transfers between devices with their start and end apart: 9, of which 5 were waited for; matrix products, arithmetic and copies ran while one was open for 15% of the time, Pallas kernels for 0%

profile of v7, /device:TPU:6, one launch (start us, length us, event | category | flops | bytes accessed | tf_op | source)
XLA Modules:
  0.0 248.8 jit_solution(11569210367757991013)
XLA Ops:
  7.2 1.0 maximum_bitcast_fusion
  9.1 2.7 %collective-permute-start.1 = (bf16[128,768]{1,0:T(8,128)(2,1)}, bf16[128,768]{1,0:T(8,128)(2,1)S(1)}, u32[]{:S(2)}, u32[]{:S(2)}) collective-permute-start(bf16[128,768]{1,0:T(8,128)(2,1)} %bitcast.138), channel_id=1, source_target_pairs={{2,0},{4,2},{6,4},{8,6},{10,8},{12,10},{14,12},{16,14},{18,16},{20... | collective-permute-start | bytes 589832 | tf_op jit(solution)/shard_map/ppermute | solution.py:24
  11.8 5.2 %collective-permute-start = (bf16[128,768]{1,0:T(8,128)(2,1)}, bf16[128,768]{1,0:T(8,128)(2,1)S(1)}, u32[]{:S(2)}, u32[]{:S(2)}) collective-permute-start(bf16[128,768]{1,0:T(8,128)(2,1)} %bitcast.139), channel_id=1, source_target_pairs={{0,2},{2,4},{4,6},{6,8},{8,10},{10,12},{12,14},{14,16},{16,18},{18... | collective-permute-start | bytes 589832 | tf_op jit(solution)/shard_map/ppermute | solution.py:22
  17.0 1.2 copy.121
  18.8 1.8 reduce.10
  21.4 7.1 %all-to-all-start.2 = ((bf16[8,2,6144]{2,1,0:T(2,128)(2,1)}), bf16[8,2,6144]{2,1,0:T(2,128)(2,1)S(1)}, u32[]{:S(2)}, u32[]{:S(2)}) async-start(bf16[8,2,6144]{2,1,0:T(2,128)(2,1)} %reshape.399), calls=%async_computation.2 | async-start | bytes 393216 | tf_op jit(solution)/shard_map/all_to_all | solution.py:113
  29.8 1.0 fusion.16
  30.8 7.6 %all-to-all-done.2 = bf16[8,2,6144]{2,1,0:T(2,128)(2,1)S(1)} async-done(((bf16[8,2,6144]{2,1,0:T(2,128)(2,1)}), bf16[8,2,6144]{2,1,0:T(2,128)(2,1)S(1)}, u32[]{:S(2)}, u32[]{:S(2)}) %all-to-all-start.2) | async-done | bytes 196640 | tf_op jit(solution)/shard_map/all_to_all | solution.py:113
  39.3 66.6 %all-gather.3.cloned.1.call-done = bf16[1,1536,3072]{2,1,0:T(8,128)(2,1)} async-done(((bf16[1,24,3072]{2,1,0:T(8,128)(2,1)}), bf16[1,1536,3072]{2,1,0:T(8,128)(2,1)}) %all-gather.3.cloned.1.call-update) | async-done | bytes 9437200 | tf_op jit(solution)/shard_map/all_gather | solution.py:129
  105.9 5.4 %slice_bitcast_fusion.1 = (bf16[768,2304]{1,0:T(8,128)(2,1)}, bf16[768,2304]{1,0:T(8,128)(2,1)S(1)}) fusion(bf16[2,768,3072]{2,1,0:T(8,128)(2,1)} %bitcast.132), kind=kLoop, calls=%fused_computation.4 | loop fusion | bytes 14155776 | tf_op jit(solution)/shard_map/squeeze | solution.py:135
  111.3 1.0 convolution_convert_fusion.7
  112.3 2.1 convolution_convert_fusion.1
  114.4 1.7 copy.80
  116.1 2.3 fusion.62
  118.5 2.1 copy.81
  120.6 2.1 copy.79
  122.7 1.9 fusion.7
  126.0 1.7 fusion.27
  127.8 1.1 copy.122
  128.8 3.4 %reduce.9 = bf16[128,768]{1,0:T(8,128)(2,1)} reduce(bf16[128,1,768]{2,1,0:T(2,128)(2,1)} %bitcast.157, bf16[]{:T(256)} %broadcast.346), dimensions={1}, to_apply=%bitcast.129.reduce_sub_computation | reduce | bytes 393218
  132.2 1.6 reshape.397
  133.8 6.7 %all-to-all-start = ((bf16[8,2,6144]{2,1,0:T(2,128)(2,1)}), bf16[8,2,6144]{2,1,0:T(2,128)(2,1)}, u32[]{:S(2)}, u32[]{:S(2)}) async-start(bf16[8,2,6144]{2,1,0:T(2,128)(2,1)} %reshape.397), calls=%async_computation | async-start | bytes 393216 | tf_op jit(solution)/shard_map/all_to_all | solution.py:113
  140.6 2.5 %fusion.26 = bf16[8,16,768]{2,1,0:T(8,128)(2,1)} fusion(bf16[8,16,768]{2,1,0:T(8,128)(2,1)} %bitcast.168, bf16[2,768,3072]{2,1,0:T(8,128)(2,1)} %bitcast.134), kind=kOutput, calls=%fused_computation.53 | convolution fusion | flops 151093248 | bytes 1572864 | tf_op jit(solution)/shard_map/dot_general | solution.py:176
  143.1 2.1 reshape_reshape.7
  145.2 2.1 copy.90
  147.2 2.1 bitcast_convert_fusion
  149.3 2.3 copy.104
  151.6 2.2 reshape.398
  153.9 1.7 multiply_reduce_fusion.1
  155.7 1.0 multiply_convert_fusion.1
  156.7 2.6 %convolution_convert_fusion = bf16[8,16,2304]{2,1,0:T(8,128)(2,1)S(1)} fusion(bf16[8,16,768]{2,1,0:T(8,128)(2,1)S(1)} %bitcast.175, bf16[2,768,3072]{2,1,0:T(8,128)(2,1)} %bitcast.135), kind=kOutput, calls=%fused_computation | convolution fusion | flops 453279744 | bytes 4325376 | tf_op jit(solution)/shard_map/dot_general | solution.py:158
  160.2 1.7 copy.86
  161.9 1.7 copy.85
  163.7 2.3 fusion.10
  165.9 2.3 fusion.48
  168.3 1.7 copy.84
  170.0 2.5 %convolution_convert_fusion.3 = bf16[12,64,128]{2,1,0:T(8,128)(2,1)} fusion(bf16[128,12,64]{0,2,1:T(8,128)(2,1)} %copy.90, f32[12,128,128]{1,2,0:T(8,128)} %fusion.10), kind=kOutput, calls=%fused_computation.46 | convolution fusion | flops 25659008 | bytes 1179648 | tf_op jit(solution)/shard_map/gst,sgh->tgh/dot_general | solution.py:102
  172.5 2.5 multiply_reduce_fusion
  175.0 1.8 fusion.11
  176.8 1.3 fusion.25
  178.4 1.8 fusion.19
  180.8 1.3 fusion.46
  183.4 2.0 add_convert_fusion
  185.4 7.2 %all-to-all-start.3 = ((bf16[8,16,768]{2,1,0:T(8,128)(2,1)}), bf16[8,16,768]{2,1,0:T(8,128)(2,1)}, u32[]{:S(2)}, u32[]{:S(2)}) async-start(bf16[8,16,768]{2,1,0:T(8,128)(2,1)} %get-tuple-element.4), calls=%async_computation.3 | async-start | bytes 393216 | tf_op jit(solution)/shard_map/all_to_all | solution.py:117
  192.6 2.1 copy.88
  194.8 2.1 reshape_reshape.6
  196.8 2.5 %fusion.23 = bf16[8,16,768]{2,1,0:T(8,128)(2,1)} fusion(f32[8,16,768]{2,1,0:T(8,128)} %get-tuple-element.5, bf16[8,16,768]{2,1,0:T(8,128)(2,1)} %reshape_reshape.6, bf16[2,768,3072]{2,1,0:T(8,128)(2,1)} %bitcast.136), kind=kOutput, calls=%fused_computation.44 | convolution fusion | flops 151191552 | bytes 1966080 | tf_op jit(solution)/shard_map/dot_general | solution.py:173
  199.3 3.7 %all-to-all-done.3 = bf16[8,16,768]{2,1,0:T(8,128)(2,1)} async-done(((bf16[8,16,768]{2,1,0:T(8,128)(2,1)}), bf16[8,16,768]{2,1,0:T(8,128)(2,1)}, u32[]{:S(2)}, u32[]{:S(2)}) %all-to-all-start.3) | async-done | bytes 196640 | tf_op jit(solution)/shard_map/all_to_all | solution.py:117
  203.1 4.0 %all-to-all-start.1 = ((bf16[8,16,768]{2,1,0:T(8,128)(2,1)}), bf16[8,16,768]{2,1,0:T(8,128)(2,1)}, u32[]{:S(2)}, u32[]{:S(2)}) async-start(bf16[8,16,768]{2,1,0:T(8,128)(2,1)} %fusion.23), calls=%async_computation.1 | async-start | bytes 393216 | tf_op jit(solution)/shard_map/all_to_all | solution.py:117
  207.1 2.6 %convolution_convert_fusion.2 = bf16[128,768]{1,0:T(8,128)(2,1)} fusion(bf16[128,768]{1,0:T(8,128)(2,1)} %bitcast.39, bf16[2,768,3072]{2,1,0:T(8,128)(2,1)} %bitcast.137), kind=kOutput, calls=%fused_computation.45 | convolution fusion | flops 151093248 | bytes 1572864 | tf_op jit(solution)/shard_map/dot_general | solution.py:206
  209.7 1.7 copy.96
  211.4 1.1 fusion.45
  212.6 2.6 %fusion.35 = f32[12,64,384]{2,1,0:T(8,128)S(1)} fusion(bf16[128,12,64]{0,2,1:T(8,128)(2,1)} %bitcast.165, f32[12,128,384]{2,1,0:T(8,128)} %copy-done.20, f32[12,128]{1,0:T(8,128)S(1)} %copy-done.23, pred[384]{0:T(512)(128)(4,1)S(1)} %copy-done.19), kind=kOutput, calls=%fused_computation.66 | convolution fusion | flops 77856768 | bytes 3742080 | tf_op jit(solution)/shard_map/gst,sgh->tgh/dot_general | solution.py:102
  215.3 1.0 multiply_convert_fusion
  217.0 0.9 fusion.61
  218.1 4.8 %collective-permute-start.2 = (bf16[128,1536]{0,1:T(8,128)(2,1)}, bf16[128,1536]{0,1:T(8,128)(2,1)}, u32[]{:S(2)}, u32[]{:S(2)}) collective-permute-start(bf16[128,1536]{0,1:T(8,128)(2,1)} %get-tuple-element.10), channel_id=1, source_target_pairs={{0,2},{2,4},{4,6},{6,8},{8,10},{10,12},{12,14},{14,16},{16,18},{18... | collective-permute-start | bytes 1179656 | tf_op jit(solution)/shard_map/ppermute | solution.py:22
  222.8 1.9 collective-permute-start.3
  224.8 1.3 fusion.21
  226.1 1.6 fusion.28
  227.7 2.3 collective-permute-done.2
  230.0 6.2 %collective-permute-done.3 = bf16[128,1536]{0,1:T(8,128)(2,1)} collective-permute-done((bf16[128,1536]{0,1:T(8,128)(2,1)}, bf16[128,1536]{0,1:T(8,128)(2,1)}, u32[]{:S(2)}, u32[]{:S(2)}) %collective-permute-start.3) | collective-permute-done | bytes 393248 | tf_op jit(solution)/shard_map/ppermute | solution.py:24
  236.2 2.2 fusion.38
  238.5 1.8 fusion.49
  240.3 1.6 copy.124
  (80 shorter events, 9.6 us)
Async XLA Ops:
  7.2 21.3 %copy-start = (s32[32,4]{0,1:T(4,128)S(1)}, s32[32,4]{0,1:T(4,128)}, u32[]{:S(2)}) copy-start(s32[32,4]{0,1:T(4,128)} %param.13) | copy-start | bytes 1540
  7.2 22.4 %copy-start.4 = (bf16[1,128,768]{2,1,0:T(8,128)(2,1)S(1)}, bf16[1,128,768]{2,1,0:T(8,128)(2,1)}, u32[]{:S(2)}) copy-start(bf16[1,128,768]{2,1,0:T(8,128)(2,1)} %param.7) | copy-start | bytes 589828
  7.2 98.7 %all-gather.3.cloned.1.call-start = ((), (), s32[]{:S(2)}) async-start(), calls=%async_computation.4 | async-start | bytes 9584640 | tf_op jit(solution)/shard_map/all_gather | solution.py:129
  9.1 20.5 %collective-permute-start.1 = (bf16[128,768]{1,0:T(8,128)(2,1)}, bf16[128,768]{1,0:T(8,128)(2,1)S(1)}, u32[]{:S(2)}, u32[]{:S(2)}) collective-permute-start(bf16[128,768]{1,0:T(8,128)(2,1)} %bitcast.138), channel_id=1, source_target_pairs={{2,0},{4,2},{6,4},{8,6},{10,8},{12,10},{14,12},{16,14},{18,16},{20... | collective-permute-start | bytes 589832 | tf_op jit(solution)/shard_map/ppermute | solution.py:24
  11.8 17.7 %collective-permute-start = (bf16[128,768]{1,0:T(8,128)(2,1)}, bf16[128,768]{1,0:T(8,128)(2,1)S(1)}, u32[]{:S(2)}, u32[]{:S(2)}) collective-permute-start(bf16[128,768]{1,0:T(8,128)(2,1)} %bitcast.139), channel_id=1, source_target_pairs={{0,2},{2,4},{4,6},{6,8},{8,10},{10,12},{12,14},{14,16},{16,18},{18... | collective-permute-start | bytes 589832 | tf_op jit(solution)/shard_map/ppermute | solution.py:22
  21.4 17.0 %all-to-all-start.2 = ((bf16[8,2,6144]{2,1,0:T(2,128)(2,1)}), bf16[8,2,6144]{2,1,0:T(2,128)(2,1)S(1)}, u32[]{:S(2)}, u32[]{:S(2)}) async-start(bf16[8,2,6144]{2,1,0:T(2,128)(2,1)} %reshape.399), calls=%async_computation.2 | async-start | bytes 393216 | tf_op jit(solution)/shard_map/all_to_all | solution.py:113
  29.5 95.1 %copy-start.18 = (pred[384]{0:T(512)(128)(4,1)}, pred[384]{0:T(512)(128)(4,1)S(1)}, u32[]{:S(2)}) copy-start(pred[384]{0:T(512)(128)(4,1)S(1)} %broadcast_bitcast_fusion) | copy-start | bytes 1156
  105.9 5.4 %copy-start.16 = (bf16[384,768]{1,0:T(8,128)(2,1)S(1)}, bf16[384,768]{1,0:T(8,128)(2,1)}, u32[]{:S(2)}) copy-start(bf16[384,768]{1,0:T(8,128)(2,1)} %fusion.16) | copy-start | bytes 1769476
  122.7 2.0 copy-start.14
  124.6 1.4 copy-start.20
  124.7 1.4 copy-start.22
  124.7 1.4 copy-start.5
  126.0 1.7 copy-start.12
  133.8 17.8 %all-to-all-start = ((bf16[8,2,6144]{2,1,0:T(2,128)(2,1)}), bf16[8,2,6144]{2,1,0:T(2,128)(2,1)}, u32[]{:S(2)}, u32[]{:S(2)}) async-start(bf16[8,2,6144]{2,1,0:T(2,128)(2,1)} %reshape.397), calls=%async_computation | async-start | bytes 393216 | tf_op jit(solution)/shard_map/all_to_all | solution.py:113
  175.0 3.1 %copy-start.10 = (bf16[128,768]{0,1:T(8,128)(2,1)S(1)}, bf16[128,768]{0,1:T(8,128)(2,1)}, u32[]{:S(2)}) copy-start(bf16[128,768]{0,1:T(8,128)(2,1)} %copy.86) | copy-start | bytes 589828
  175.0 5.2 %copy-start.1 = (bf16[768,2304]{1,0:T(8,128)(2,1)S(1)}, bf16[768,2304]{1,0:T(8,128)(2,1)}, u32[]{:S(2)}) copy-start(bf16[768,2304]{1,0:T(8,128)(2,1)} %get-tuple-element.8) | copy-start | bytes 10616836
  178.1 2.6 %copy-start.8 = (bf16[1,128,768]{2,1,0:T(8,128)(2,1)S(1)}, bf16[1,128,768]{2,1,0:T(8,128)(2,1)}, u32[]{:S(2)}) copy-start(bf16[1,128,768]{2,1,0:T(8,128)(2,1)} %get-tuple-element.7) | copy-start | bytes 589828
  178.1 2.6 %copy-start.17 = (bf16[12,64,128]{2,1,0:T(8,128)(2,1)S(1)}, bf16[12,64,128]{2,1,0:T(8,128)(2,1)}, u32[]{:S(2)}) copy-start(bf16[12,64,128]{2,1,0:T(8,128)(2,1)} %convolution_convert_fusion.3) | copy-start | bytes 589828
  185.4 17.7 %all-to-all-start.3 = ((bf16[8,16,768]{2,1,0:T(8,128)(2,1)}), bf16[8,16,768]{2,1,0:T(8,128)(2,1)}, u32[]{:S(2)}, u32[]{:S(2)}) async-start(bf16[8,16,768]{2,1,0:T(8,128)(2,1)} %get-tuple-element.4), calls=%async_computation.3 | async-start | bytes 393216 | tf_op jit(solution)/shard_map/all_to_all | solution.py:117
  196.8 15.7 %copy-start.19 = (pred[384]{0:T(512)(128)(4,1)S(1)}, pred[384]{0:T(512)(128)(4,1)}, u32[]{:S(2)}) copy-start(pred[384]{0:T(512)(128)(4,1)} %copy-done.18) | copy-start | bytes 1156
  196.8 15.7 %copy-start.23 = (f32[12,128]{1,0:T(8,128)S(1)}, f32[12,128]{1,0:T(8,128)}, u32[]{:S(2)}) copy-start(f32[12,128]{1,0:T(8,128)} %copy-done.22) | copy-start | bytes 18436
  203.1 23.1 %all-to-all-start.1 = ((bf16[8,16,768]{2,1,0:T(8,128)(2,1)}), bf16[8,16,768]{2,1,0:T(8,128)(2,1)}, u32[]{:S(2)}, u32[]{:S(2)}) async-start(bf16[8,16,768]{2,1,0:T(8,128)(2,1)} %fusion.23), calls=%async_computation.1 | async-start | bytes 393216 | tf_op jit(solution)/shard_map/all_to_all | solution.py:117
  212.5 2.6 %copy-start.13 = (bf16[128,768]{0,1:T(8,128)(2,1)S(1)}, bf16[128,768]{0,1:T(8,128)(2,1)}, u32[]{:S(2)}) copy-start(bf16[128,768]{0,1:T(8,128)(2,1)} %copy.96) | copy-start | bytes 589828
  212.6 2.6 %copy-start.15 = (bf16[384,768]{0,1:T(8,128)(2,1)S(1)}, bf16[384,768]{0,1:T(8,128)(2,1)}, u32[]{:S(2)}) copy-start(bf16[384,768]{0,1:T(8,128)(2,1)} %copy.79) | copy-start | bytes 1769476
  212.6 2.7 %copy-start.21 = (f32[12,128,384]{2,1,0:T(8,128)S(1)}, f32[12,128,384]{2,1,0:T(8,128)}, u32[]{:S(2)}) copy-start(f32[12,128,384]{2,1,0:T(8,128)} %copy-done.20) | copy-start | bytes 7077892
  215.3 1.5 copy-start.7
  215.3 1.1 copy-start.11
  216.8 1.3 copy-start.2
  216.8 8.0 %copy-start.9 = (bf16[384,768]{0,1:T(8,128)(2,1)S(1)}, bf16[384,768]{0,1:T(8,128)(2,1)}, u32[]{:S(2)}) copy-start(bf16[384,768]{0,1:T(8,128)(2,1)} %copy.81) | copy-start | bytes 1769476
  218.1 11.9 %collective-permute-start.2 = (bf16[128,1536]{0,1:T(8,128)(2,1)}, bf16[128,1536]{0,1:T(8,128)(2,1)}, u32[]{:S(2)}, u32[]{:S(2)}) collective-permute-start(bf16[128,1536]{0,1:T(8,128)(2,1)} %get-tuple-element.10), channel_id=1, source_target_pairs={{0,2},{2,4},{4,6},{6,8},{8,10},{10,12},{12,14},{14,16},{16,18},{18... | collective-permute-start | bytes 1179656 | tf_op jit(solution)/shard_map/ppermute | solution.py:22
  222.8 13.4 %collective-permute-start.3 = (bf16[128,1536]{0,1:T(8,128)(2,1)}, bf16[128,1536]{0,1:T(8,128)(2,1)}, u32[]{:S(2)}, u32[]{:S(2)}) collective-permute-start(bf16[128,1536]{0,1:T(8,128)(2,1)} %get-tuple-element.11), channel_id=1, source_target_pairs={{2,0},{4,2},{6,4},{8,6},{10,8},{12,10},{14,12},{16,14},{18,16},{20... | collective-permute-start | bytes 1179656 | tf_op jit(solution)/shard_map/ppermute | solution.py:24
  226.1 10.1 %copy-start.3 = (f32[12,64,384]{2,1,0:T(8,128)S(1)}, f32[12,64,384]{2,1,0:T(8,128)}, u32[]{:S(2)}) copy-start(f32[12,64,384]{2,1,0:T(8,128)} %copy-done.2) | copy-start | bytes 3538948
  227.7 10.8 %copy-start.6 = (bf16[1,128,768]{2,1,0:T(8,128)(2,1)S(1)}, bf16[1,128,768]{2,1,0:T(8,128)(2,1)}, u32[]{:S(2)}) copy-start(bf16[1,128,768]{2,1,0:T(8,128)(2,1)} %param.7) | copy-start | bytes 589828
Sparse Core Ops, SparseCore 0:
  11.9 93.9 all-gather.2

commit v8 on v6

--- a/solution.py
+++ b/solution.py
@@ -141,15 +141,12 @@
     input_window = padded(local_in, (("space", 0),), shard)
     cot_rows = to_frames(grad_out)
     normed_window = rms_norm(input_window)
-    normed_space = normed_window[shard : 2 * shard]
-    queries = jnp.dot(
-        normed_space, full_qkv_space[:, :feature_count], preferred_element_type=jnp.float32
-    ).astype(jnp.bfloat16)
-    kv_window = jnp.dot(
-        normed_window, full_qkv_space[:, feature_count:], preferred_element_type=jnp.float32
-    ).astype(jnp.bfloat16)
-    key_window = kv_window[:, :feature_count]
-    value_window = kv_window[:, feature_count:]
+    projected_window = jnp.dot(
+        normed_window, full_qkv_space, preferred_element_type=jnp.float32
+    ).astype(jnp.bfloat16)
+    queries = projected_window[shard : 2 * shard, :feature_count]
+    key_window = projected_window[:, feature_count : 2 * feature_count]
+    value_window = projected_window[:, 2 * feature_count :]
     attended, totals = space_attend(queries, key_window, value_window, allowed)
     update = jnp.dot(attended, full_out_space, preferred_element_type=jnp.float32)
     stream = (local_in.astype(jnp.float32) + update).astype(jnp.bfloat16)

time: 206 us -> 206 us (level)
  local copies, waits for them, and re-layouts: 17.1 us -> 14.4 us
  matrix products: 29.5 us -> 31.6 us
    squeeze x1 -> x0, local copies, waits for them, and re-layouts: 2.23 us -> none  [local(): full_qkv_space = all_weights[0, :, :qkv_width]]
    dot_general x2 -> x1, matrix products: 1.42 us -> 3.59 us  [local(): jnp.dot(normed_window, full_qkv_space, preferred_element_type=jnp.float32)]
    unnamed x39 -> x41, local copies, waits for them, and re-layouts: 7.46 us -> 6.87 us
  transfers between devices with their start and end apart: 9 -> 9, of which waited for: 6 -> 6; matrix products, arithmetic and copies ran while one was open for 11% -> 10% of each run, Pallas kernels for 0% -> 0%
where the time goes in v8:
time: 206 us; the launch traced here: 205 us
  waiting for transfers between devices  98.6 us (48%)
  starting transfers between devices  35.9 us (17%)
  matrix products  31.6 us (15%)
  between operations  14.7 us (7%)
  local copies, waits for them, and re-layouts  14.4 us (7%)
  other arithmetic  9.47 us (5%)
    all_gather x1, waiting for transfers between devices, local(): lax.all_gather(mine, ('dp', 'space'), axis=0, tiled=True)  67.2 us
    all_to_all x2, waiting for transfers between devices, to_frames(): lax.all_to_all(local_rows[None], 'frame', split_axis=1, concat_axis=0, ti...  15.7 us
    all_to_all x2, starting transfers between devices, to_frames(): lax.all_to_all(local_rows[None], 'frame', split_axis=1, concat_axis=0, ti...  13.8 us
    ppermute x2, starting transfers between devices, padded(): lax.ppermute(tail, axis, [(i, (i + 1) % count) for i in range(ends)])  9.98 us
    all_to_all x2, starting transfers between devices, to_space(): lax.all_to_all(frame_rows, 'frame', split_axis=0, concat_axis=1, tiled=True)  7.41 us
    unnamed x41, local copies, waits for them, and re-layouts  6.87 us
    all_to_all x2, waiting for transfers between devices, to_space(): lax.all_to_all(frame_rows, 'frame', split_axis=0, concat_axis=1, tiled=True)  6.63 us
    ppermute x2, waiting for transfers between devices, padded(): lax.ppermute(head, axis, [((i + 1) % count, i) for i in range(ends)])  6.23 us
  transfers between devices with their start and end apart: 9, of which 6 were waited for; matrix products, arithmetic and copies ran while one was open for 10% of the time, Pallas kernels for 0%

profile of v8, /device:TPU:6, one launch (start us, length us, event | category | flops | bytes accessed | tf_op | source)
XLA Modules:
  0.0 204.6 jit_solution(12629448771202549506)
XLA Ops:
  7.2 1.0 maximum_bitcast_fusion
  8.3 0.7 fusion.50
  9.1 2.7 %collective-permute-start.1 = (bf16[128,768]{1,0:T(8,128)(2,1)}, bf16[128,768]{1,0:T(8,128)(2,1)S(1)}, u32[]{:S(2)}, u32[]{:S(2)}) collective-permute-start(bf16[128,768]{1,0:T(8,128)(2,1)} %bitcast.140), channel_id=1, source_target_pairs={{2,0},{4,2},{6,4},{8,6},{10,8},{12,10},{14,12},{16,14},{18,16},{20... | collective-permute-start | bytes 589832 | tf_op jit(solution)/shard_map/ppermute | solution.py:24
  11.8 5.2 %collective-permute-start = (bf16[128,768]{1,0:T(8,128)(2,1)}, bf16[128,768]{1,0:T(8,128)(2,1)S(1)}, u32[]{:S(2)}, u32[]{:S(2)}) collective-permute-start(bf16[128,768]{1,0:T(8,128)(2,1)} %bitcast.141), channel_id=1, source_target_pairs={{0,2},{2,4},{4,6},{6,8},{8,10},{10,12},{12,14},{14,16},{16,18},{18... | collective-permute-start | bytes 589832 | tf_op jit(solution)/shard_map/ppermute | solution.py:22
  17.0 1.2 copy.139
  18.3 0.6 broadcast.348
  18.8 1.9 reduce.9
  20.7 0.7 reshape.388
  21.4 7.1 %all-to-all-start.2 = ((bf16[8,2,6144]{2,1,0:T(2,128)(2,1)}), bf16[8,2,6144]{2,1,0:T(2,128)(2,1)S(1)}, u32[]{:S(2)}, u32[]{:S(2)}) async-start(bf16[8,2,6144]{2,1,0:T(2,128)(2,1)} %reshape.388), calls=%async_computation.2 | async-start | bytes 393216 | tf_op jit(solution)/shard_map/all_to_all | solution.py:113
  29.0 0.2 fusion.9
  29.2 9.2 %all-to-all-done.2 = bf16[8,2,6144]{2,1,0:T(2,128)(2,1)S(1)} async-done(((bf16[8,2,6144]{2,1,0:T(2,128)(2,1)}), bf16[8,2,6144]{2,1,0:T(2,128)(2,1)S(1)}, u32[]{:S(2)}, u32[]{:S(2)}) %all-to-all-start.2) | async-done | bytes 196640 | tf_op jit(solution)/shard_map/all_to_all | solution.py:113
  38.7 67.2 %all-gather.3.cloned.1.call-done = bf16[1,1536,3072]{2,1,0:T(8,128)(2,1)} async-done(((bf16[1,24,3072]{2,1,0:T(8,128)(2,1)}), bf16[1,1536,3072]{2,1,0:T(8,128)(2,1)}) %all-gather.3.cloned.1.call-update) | async-done | bytes 9437200 | tf_op jit(solution)/shard_map/all_gather | solution.py:129
  105.9 3.6 %convolution_convert_fusion = bf16[384,2304]{1,0:T(8,128)(2,1)S(1)} fusion(bf16[2,768,3072]{2,1,0:T(8,128)(2,1)} %bitcast.158, f32[384]{0:T(512)S(1)} %add_rsqrt_fusion, bf16[128,768]{1,0:T(8,128)(2,1)S(1)} %collective-permute-done.1, bf16[128,768]{1,0:T(8,128)(2,1)S(1)} %bitcast.143, bf16[128,768]{1,0:T(8,128)(2,1)S(1)} %collective-permute-done), kind=kOutput, calls=%fused_computation | convolution fusion | flops 1362198528 | bytes 5899776 | tf_op jit(solution)/shard_map/dot_general | solution.py:144
  109.6 0.3 copy.92
  110.1 0.3 copy.90
  110.4 0.7 fusion.4
  111.2 0.7 convolution_convert_fusion.6
  111.9 1.7 fusion.20
  113.6 0.3 copy.140
  113.9 1.9 reduce.8
  115.8 0.7 reshape.386
  116.5 6.7 %all-to-all-start = ((bf16[8,2,6144]{2,1,0:T(2,128)(2,1)}), bf16[8,2,6144]{2,1,0:T(2,128)(2,1)S(1)}, u32[]{:S(2)}, u32[]{:S(2)}) async-start(bf16[8,2,6144]{2,1,0:T(2,128)(2,1)} %reshape.386), calls=%async_computation | async-start | bytes 393216 | tf_op jit(solution)/shard_map/all_to_all | solution.py:113
  123.2 1.8 fusion.19
  125.0 0.3 reshape_reshape.7
  125.4 1.1 copy.101
  126.5 1.2 copy.118
  127.7 6.5 %all-to-all-done = bf16[8,2,6144]{2,1,0:T(2,128)(2,1)S(1)} async-done(((bf16[8,2,6144]{2,1,0:T(2,128)(2,1)}), bf16[8,2,6144]{2,1,0:T(2,128)(2,1)S(1)}, u32[]{:S(2)}, u32[]{:S(2)}) %all-to-all-start) | async-done | bytes 196640 | tf_op jit(solution)/shard_map/all_to_all | solution.py:113
  134.7 2.6 %convolution_convert_fusion.1 = bf16[8,16,2304]{2,1,0:T(8,128)(2,1)S(1)} fusion(bf16[8,16,768]{2,1,0:T(8,128)(2,1)S(1)} %bitcast.170, bf16[2,768,3072]{2,1,0:T(8,128)(2,1)} %bitcast.161), kind=kOutput, calls=%fused_computation.1 | convolution fusion | flops 453279744 | bytes 4325376 | tf_op jit(solution)/shard_map/dot_general | solution.py:155
  137.7 0.3 fusion.7
  138.1 0.4 fusion.46
  138.7 0.3 copy-done.6
  139.0 1.1 fusion.18
  140.1 1.3 multiply_reduce_fusion
  141.4 0.3 fusion.8
  141.7 0.4 fusion.16
  142.1 0.2 fusion.17
  142.3 0.4 copy.109
  142.8 0.3 convert_element_type.166
  143.1 0.4 copy.104
  143.5 0.3 concatenate.26
  143.8 0.4 copy.106
  144.3 0.3 convert_element_type.163
  144.6 3.4 %multiply_reduce_fusion.1 = (f32[8,16]{1,0:T(8,128)S(1)}, f32[8,16,768]{2,1,0:T(8,128)S(1)}) fusion(f32[8,16,768]{2,1,0:T(8,128)S(1)} %bitcast.129, bf16[2,768,3072]{2,1,0:T(8,128)(2,1)} %bitcast.162, bf16[8,16,768]{2,1,0:T(8,128)(2,1)S(1)} %convert_element_type.166, bf16[8,16,768]{2,1,0:T(8,128)(2,1)S(1)} %convert_element_type.163, ...), kind=kOutput, calls=%fused_computation.78 | convolution fusion | flops 454950784 | bytes 4915712 | tf_op jit(solution)/shard_map/dot_general | solution.py:189
  148.0 0.9 add_convert_fusion
  148.8 3.4 %all-to-all-start.3 = ((bf16[8,16,768]{2,1,0:T(8,128)(2,1)}), bf16[8,16,768]{2,1,0:T(8,128)(2,1)S(1)}, u32[]{:S(2)}, u32[]{:S(2)}) async-start(bf16[8,16,768]{2,1,0:T(8,128)(2,1)} %add_convert_fusion), calls=%async_computation.3 | async-start | bytes 393216 | tf_op jit(solution)/shard_map/all_to_all | solution.py:117
  152.2 0.4 copy.99
  152.7 0.3 reshape_reshape.6
  153.0 2.3 %fusion.13 = bf16[8,16,768]{2,1,0:T(8,128)(2,1)} fusion(f32[8,16,768]{2,1,0:T(8,128)S(1)} %bitcast.131, bf16[8,16,768]{2,1,0:T(8,128)(2,1)S(1)} %reshape_reshape.6, bf16[2,768,3072]{2,1,0:T(8,128)(2,1)} %bitcast.163), kind=kOutput, calls=%fused_computation.34 | convolution fusion | flops 151191552 | bytes 1966080 | tf_op jit(solution)/shard_map/dot_general | solution.py:170
  155.3 6.6 %all-to-all-done.3 = bf16[8,16,768]{2,1,0:T(8,128)(2,1)S(1)} async-done(((bf16[8,16,768]{2,1,0:T(8,128)(2,1)}), bf16[8,16,768]{2,1,0:T(8,128)(2,1)S(1)}, u32[]{:S(2)}, u32[]{:S(2)}) %all-to-all-start.3) | async-done | bytes 196640 | tf_op jit(solution)/shard_map/all_to_all | solution.py:117
  161.9 4.0 %all-to-all-start.1 = ((bf16[8,16,768]{2,1,0:T(8,128)(2,1)}), bf16[8,16,768]{2,1,0:T(8,128)(2,1)}, u32[]{:S(2)}, u32[]{:S(2)}) async-start(bf16[8,16,768]{2,1,0:T(8,128)(2,1)} %fusion.13), calls=%async_computation.1 | async-start | bytes 393216 | tf_op jit(solution)/shard_map/all_to_all | solution.py:117
  165.9 1.8 convolution_convert_fusion.2
  168.0 2.5 %fusion.34 = f32[12,64,384]{2,1,0:T(8,128)S(1)} fusion(bf16[128,12,64]{0,2,1:T(8,128)(2,1)S(1)} %bitcast.155, f32[12,128,384]{2,1,0:T(8,128)} %copy-done.12, f32[12,128]{1,0:T(8,128)S(1)} %copy-done.15, pred[384]{0:T(512)(128)(4,1)S(1)} %broadcast_bitcast_fusion), kind=kOutput, calls=%fused_computation.63 | convolution fusion | flops 77856768 | bytes 3742080 | tf_op jit(solution)/shard_map/gst,sgh->tgh/dot_general | solution.py:102
  170.6 0.9 multiply_convert_fusion
  171.5 0.4 convolution_multiply_fusion
  172.0 0.9 fusion.61
  173.0 4.8 %collective-permute-start.2 = (bf16[128,1536]{0,1:T(8,128)(2,1)}, bf16[128,1536]{0,1:T(8,128)(2,1)}, u32[]{:S(2)}, u32[]{:S(2)}) collective-permute-start(bf16[128,1536]{0,1:T(8,128)(2,1)} %get-tuple-element.6), channel_id=1, source_target_pairs={{0,2},{2,4},{4,6},{6,8},{8,10},{10,12},{12,14},{14,16},{16,18},{18... | collective-permute-start | bytes 1179656 | tf_op jit(solution)/shard_map/ppermute | solution.py:22
  177.8 1.9 collective-permute-start.3
  179.7 1.8 fusion.11
  181.5 2.8 %collective-permute-done.2 = bf16[128,1536]{0,1:T(8,128)(2,1)} collective-permute-done((bf16[128,1536]{0,1:T(8,128)(2,1)}, bf16[128,1536]{0,1:T(8,128)(2,1)}, u32[]{:S(2)}, u32[]{:S(2)}) %collective-permute-start.2) | collective-permute-done | bytes 393248 | tf_op jit(solution)/shard_map/ppermute | solution.py:22
  184.2 6.2 %collective-permute-done.3 = bf16[128,1536]{0,1:T(8,128)(2,1)} collective-permute-done((bf16[128,1536]{0,1:T(8,128)(2,1)}, bf16[128,1536]{0,1:T(8,128)(2,1)}, u32[]{:S(2)}, u32[]{:S(2)}) %collective-permute-start.3) | collective-permute-done | bytes 393248 | tf_op jit(solution)/shard_map/ppermute | solution.py:24
  190.4 1.3 fusion.24
  191.8 3.5 %fusion.38 = (f32[128]{0:T(128)S(1)}, f32[128]{0:T(128)S(1)}, f32[128,768]{1,0:T(8,128)S(1)}) fusion(bf16[1,128,768]{2,1,0:T(8,128)(2,1)S(1)} %copy-done.3, bf16[2,768,3072]{2,1,0:T(8,128)(2,1)} %bitcast.165, bf16[128,1536]{0,1:T(8,128)(2,1)S(1)} %fusion.24, bf16[128,768]{0,1:T(8,128)(2,1)S(1)} %bitcast.171), kind=kOutput, calls=%fused_computation.68 | convolution fusion | flops 454655744 | bytes 4719616 | tf_op jit(solution)/shard_map/dot_general | solution.py:211
  195.2 0.9 fusion.47
  196.1 1.6 copy.142
  (66 shorter events, 2.6 us)
Async XLA Ops:
  7.2 21.4 %copy-start = (s32[32,4]{0,1:T(4,128)S(1)}, s32[32,4]{0,1:T(4,128)}, u32[]{:S(2)}) copy-start(s32[32,4]{0,1:T(4,128)} %param.13) | copy-start | bytes 1540
  7.2 21.8 %copy-start.2 = (bf16[1,128,768]{2,1,0:T(8,128)(2,1)S(1)}, bf16[1,128,768]{2,1,0:T(8,128)(2,1)}, u32[]{:S(2)}) copy-start(bf16[1,128,768]{2,1,0:T(8,128)(2,1)} %param.7) | copy-start | bytes 589828
  7.2 98.7 %all-gather.3.cloned.1.call-start = ((), (), s32[]{:S(2)}) async-start(), calls=%async_computation.4 | async-start | bytes 9584640 | tf_op jit(solution)/shard_map/all_gather | solution.py:129
  9.1 20.0 %collective-permute-start.1 = (bf16[128,768]{1,0:T(8,128)(2,1)}, bf16[128,768]{1,0:T(8,128)(2,1)S(1)}, u32[]{:S(2)}, u32[]{:S(2)}) collective-permute-start(bf16[128,768]{1,0:T(8,128)(2,1)} %bitcast.140), channel_id=1, source_target_pairs={{2,0},{4,2},{6,4},{8,6},{10,8},{12,10},{14,12},{16,14},{18,16},{20... | collective-permute-start | bytes 589832 | tf_op jit(solution)/shard_map/ppermute | solution.py:24
  11.8 17.2 %collective-permute-start = (bf16[128,768]{1,0:T(8,128)(2,1)}, bf16[128,768]{1,0:T(8,128)(2,1)S(1)}, u32[]{:S(2)}, u32[]{:S(2)}) collective-permute-start(bf16[128,768]{1,0:T(8,128)(2,1)} %bitcast.141), channel_id=1, source_target_pairs={{0,2},{2,4},{4,6},{6,8},{8,10},{10,12},{12,14},{14,16},{16,18},{18... | collective-permute-start | bytes 589832 | tf_op jit(solution)/shard_map/ppermute | solution.py:22
  21.4 17.0 %all-to-all-start.2 = ((bf16[8,2,6144]{2,1,0:T(2,128)(2,1)}), bf16[8,2,6144]{2,1,0:T(2,128)(2,1)S(1)}, u32[]{:S(2)}, u32[]{:S(2)}) async-start(bf16[8,2,6144]{2,1,0:T(2,128)(2,1)} %reshape.388), calls=%async_computation.2 | async-start | bytes 393216 | tf_op jit(solution)/shard_map/all_to_all | solution.py:113
  109.9 1.2 copy-start.1
  110.1 1.8 copy-start.4
  110.4 1.5 copy-start.9
  111.1 0.8 copy-start.14
  111.1 2.7 %copy-start.12 = (f32[12,128,384]{2,1,0:T(8,128)}, f32[12,128,384]{2,1,0:T(8,128)S(1)}, u32[]{:S(2)}) copy-start(f32[12,128,384]{2,1,0:T(8,128)S(1)} %get-tuple-element.14) | copy-start | bytes 7077892
  116.5 17.6 %all-to-all-start = ((bf16[8,2,6144]{2,1,0:T(2,128)(2,1)}), bf16[8,2,6144]{2,1,0:T(2,128)(2,1)S(1)}, u32[]{:S(2)}, u32[]{:S(2)}) async-start(bf16[8,2,6144]{2,1,0:T(2,128)(2,1)} %reshape.386), calls=%async_computation | async-start | bytes 393216 | tf_op jit(solution)/shard_map/all_to_all | solution.py:113
  138.1 0.9 copy-start.6
  141.3 1.0 copy-start.11
  148.8 13.1 %all-to-all-start.3 = ((bf16[8,16,768]{2,1,0:T(8,128)(2,1)}), bf16[8,16,768]{2,1,0:T(8,128)(2,1)S(1)}, u32[]{:S(2)}, u32[]{:S(2)}) async-start(bf16[8,16,768]{2,1,0:T(8,128)(2,1)} %add_convert_fusion), calls=%async_computation.3 | async-start | bytes 393216 | tf_op jit(solution)/shard_map/all_to_all | solution.py:117
  153.0 15.0 %copy-start.15 = (f32[12,128]{1,0:T(8,128)S(1)}, f32[12,128]{1,0:T(8,128)}, u32[]{:S(2)}) copy-start(f32[12,128]{1,0:T(8,128)} %copy-done.14) | copy-start | bytes 18436
  161.9 6.1 %copy-start.7 = (bf16[8,16,768]{2,1,0:T(8,128)(2,1)}, bf16[8,16,768]{2,1,0:T(8,128)(2,1)S(1)}, u32[]{:S(2)}) copy-start(bf16[8,16,768]{2,1,0:T(8,128)(2,1)S(1)} %all-to-all-done.3) | copy-start | bytes 589828
  161.9 17.8 %all-to-all-start.1 = ((bf16[8,16,768]{2,1,0:T(8,128)(2,1)}), bf16[8,16,768]{2,1,0:T(8,128)(2,1)}, u32[]{:S(2)}, u32[]{:S(2)}) async-start(bf16[8,16,768]{2,1,0:T(8,128)(2,1)} %fusion.13), calls=%async_computation.1 | async-start | bytes 393216 | tf_op jit(solution)/shard_map/all_to_all | solution.py:117
  168.0 2.5 %copy-start.10 = (bf16[384,768]{0,1:T(8,128)(2,1)S(1)}, bf16[384,768]{0,1:T(8,128)(2,1)}, u32[]{:S(2)}) copy-start(bf16[384,768]{0,1:T(8,128)(2,1)} %copy-done.9) | copy-start | bytes 1769476
  168.0 2.6 %copy-start.13 = (f32[12,128,384]{2,1,0:T(8,128)S(1)}, f32[12,128,384]{2,1,0:T(8,128)}, u32[]{:S(2)}) copy-start(f32[12,128,384]{2,1,0:T(8,128)} %copy-done.12) | copy-start | bytes 7077892
  170.6 1.0 copy-start.5
  173.0 11.2 %collective-permute-start.2 = (bf16[128,1536]{0,1:T(8,128)(2,1)}, bf16[128,1536]{0,1:T(8,128)(2,1)}, u32[]{:S(2)}, u32[]{:S(2)}) collective-permute-start(bf16[128,1536]{0,1:T(8,128)(2,1)} %get-tuple-element.6), channel_id=1, source_target_pairs={{0,2},{2,4},{4,6},{6,8},{8,10},{10,12},{12,14},{14,16},{16,18},{18... | collective-permute-start | bytes 1179656 | tf_op jit(solution)/shard_map/ppermute | solution.py:22
  177.8 12.7 %collective-permute-start.3 = (bf16[128,1536]{0,1:T(8,128)(2,1)}, bf16[128,1536]{0,1:T(8,128)(2,1)}, u32[]{:S(2)}, u32[]{:S(2)}) collective-permute-start(bf16[128,1536]{0,1:T(8,128)(2,1)} %get-tuple-element.7), channel_id=1, source_target_pairs={{2,0},{4,2},{6,4},{8,6},{10,8},{12,10},{14,12},{16,14},{18,16},{20... | collective-permute-start | bytes 1179656 | tf_op jit(solution)/shard_map/ppermute | solution.py:24
  179.7 12.0 %copy-start.3 = (bf16[1,128,768]{2,1,0:T(8,128)(2,1)S(1)}, bf16[1,128,768]{2,1,0:T(8,128)(2,1)}, u32[]{:S(2)}) copy-start(bf16[1,128,768]{2,1,0:T(8,128)(2,1)} %param.7) | copy-start | bytes 589828
  191.7 3.5 %copy-start.8 = (bf16[8,16,768]{2,1,0:T(8,128)(2,1)S(1)}, bf16[8,16,768]{2,1,0:T(8,128)(2,1)}, u32[]{:S(2)}) copy-start(bf16[8,16,768]{2,1,0:T(8,128)(2,1)} %copy-done.7) | copy-start | bytes 589828
Sparse Core Ops, SparseCore 0:
  11.9 93.9 all-gather.2

commit v9 on v8

--- a/solution.py
+++ b/solution.py
@@ -167,9 +167,9 @@
     allowed_time = same_position & causal
     attended_flat, totals_time = space_attend(query_time, key_time, value_time, allowed_time)
     attended_time = attended_flat.reshape(frame_count, position_count, feature_count)
-    update_time = jnp.dot(attended_time, full_out_time, preferred_element_type=jnp.float32)
-    frames_out_rows = (stream_rows.astype(jnp.float32) + update_time).astype(jnp.bfloat16)
-    frames_out = to_space(frames_out_rows)
+    attended_back = to_space(attended_time)
+    update_time = jnp.dot(attended_back, full_out_time, preferred_element_type=jnp.float32)
+    frames_out = (stream.astype(jnp.float32) + update_time).astype(jnp.bfloat16)
     grad_att_time = jnp.dot(cot_rows, full_out_time.T, preferred_element_type=jnp.float32).astype(
         jnp.bfloat16
     )

time: 206 us -> 205 us (level)
    ppermute x2, waiting for transfers between devices: 2.76 us -> 0.43 us  [padded(): lax.ppermute(tail, axis, [(i, (i + 1) % count) for i in range(ends)])]
    unnamed x41 -> x36, local copies, waits for them, and re-layouts: 6.87 us -> 6.2 us
  transfers between devices with their start and end apart: 9 -> 9, of which waited for: 6 -> 6; matrix products, arithmetic and copies ran while one was open for 10% -> 11% of each run, Pallas kernels for 0% -> 0%
where the time goes in v9:
time: 205 us; the launch traced here: 204 us
  waiting for transfers between devices  98.5 us (48%)
  starting transfers between devices  35.9 us (18%)
  matrix products  31.7 us (15%)
  between operations  14.6 us (7%)
  local copies, waits for them, and re-layouts  13.7 us (7%)
  other arithmetic  9.47 us (5%)
    all_gather x1, waiting for transfers between devices, local(): lax.all_gather(mine, ('dp', 'space'), axis=0, tiled=True)  67.2 us
    all_to_all x2, waiting for transfers between devices, to_frames(): lax.all_to_all(local_rows[None], 'frame', split_axis=1, concat_axis=0, ti...  16.4 us
    all_to_all x2, starting transfers between devices, to_frames(): lax.all_to_all(local_rows[None], 'frame', split_axis=1, concat_axis=0, ti...  13.8 us
    ppermute x2, starting transfers between devices, padded(): lax.ppermute(tail, axis, [(i, (i + 1) % count) for i in range(ends)])  9.97 us
    all_to_all x2, waiting for transfers between devices, to_space(): lax.all_to_all(frame_rows, 'frame', split_axis=0, concat_axis=1, tiled=True)  8.26 us
    all_to_all x2, starting transfers between devices, to_space(): lax.all_to_all(frame_rows, 'frame', split_axis=0, concat_axis=1, tiled=True)  7.41 us
    ppermute x2, waiting for transfers between devices, padded(): lax.ppermute(head, axis, [((i + 1) % count, i) for i in range(ends)])  6.23 us
    unnamed x36, local copies, waits for them, and re-layouts  6.2 us
  transfers between devices with their start and end apart: 9, of which 6 were waited for; matrix products, arithmetic and copies ran while one was open for 11% of the time, Pallas kernels for 0%

profile of v9, /device:TPU:6, one launch (start us, length us, event | category | flops | bytes accessed | tf_op | source)
XLA Modules:
  0.0 203.9 jit_solution(2426698669210370801)
XLA Ops:
  7.2 1.0 maximum_bitcast_fusion
  8.3 0.7 fusion.64
  9.1 2.7 %collective-permute-start.1 = (bf16[128,768]{1,0:T(8,128)(2,1)}, bf16[128,768]{1,0:T(8,128)(2,1)S(1)}, u32[]{:S(2)}, u32[]{:S(2)}) collective-permute-start(bf16[128,768]{1,0:T(8,128)(2,1)} %bitcast.147), channel_id=1, source_target_pairs={{2,0},{4,2},{6,4},{8,6},{10,8},{12,10},{14,12},{16,14},{18,16},{20... | collective-permute-start | bytes 589832 | tf_op jit(solution)/shard_map/ppermute | solution.py:24
  11.8 5.2 %collective-permute-start = (bf16[128,768]{1,0:T(8,128)(2,1)}, bf16[128,768]{1,0:T(8,128)(2,1)S(1)}, u32[]{:S(2)}, u32[]{:S(2)}) collective-permute-start(bf16[128,768]{1,0:T(8,128)(2,1)} %bitcast.148), channel_id=1, source_target_pairs={{0,2},{2,4},{4,6},{6,8},{8,10},{10,12},{12,14},{14,16},{16,18},{18... | collective-permute-start | bytes 589832 | tf_op jit(solution)/shard_map/ppermute | solution.py:22
  17.0 1.2 copy.138
  18.3 0.6 broadcast.348
  18.8 1.9 reduce.8
  20.7 0.7 reshape.389
  21.4 7.1 %all-to-all-start.2 = ((bf16[8,2,6144]{2,1,0:T(2,128)(2,1)}), bf16[8,2,6144]{2,1,0:T(2,128)(2,1)S(1)}, u32[]{:S(2)}, u32[]{:S(2)}) async-start(bf16[8,2,6144]{2,1,0:T(2,128)(2,1)} %reshape.389), calls=%async_computation.2 | async-start | bytes 393216 | tf_op jit(solution)/shard_map/all_to_all | solution.py:113
  29.0 0.2 fusion.9
  29.2 9.2 %all-to-all-done.2 = bf16[8,2,6144]{2,1,0:T(2,128)(2,1)S(1)} async-done(((bf16[8,2,6144]{2,1,0:T(2,128)(2,1)}), bf16[8,2,6144]{2,1,0:T(2,128)(2,1)S(1)}, u32[]{:S(2)}, u32[]{:S(2)}) %all-to-all-start.2) | async-done | bytes 196640 | tf_op jit(solution)/shard_map/all_to_all | solution.py:113
  38.7 67.2 %all-gather.3.cloned.1.call-done = bf16[1,1536,3072]{2,1,0:T(8,128)(2,1)} async-done(((bf16[1,24,3072]{2,1,0:T(8,128)(2,1)}), bf16[1,1536,3072]{2,1,0:T(8,128)(2,1)}) %all-gather.3.cloned.1.call-update) | async-done | bytes 9437200 | tf_op jit(solution)/shard_map/all_gather | solution.py:129
  105.9 3.6 %convolution_convert_fusion = bf16[384,2304]{1,0:T(8,128)(2,1)S(1)} fusion(bf16[2,768,3072]{2,1,0:T(8,128)(2,1)} %bitcast.174, f32[384]{0:T(512)S(1)} %add_rsqrt_fusion, bf16[128,768]{1,0:T(8,128)(2,1)S(1)} %collective-permute-done.1, bf16[128,768]{1,0:T(8,128)(2,1)S(1)} %bitcast.150, bf16[128,768]{1,0:T(8,128)(2,1)S(1)} %collective-permute-done), kind=kOutput, calls=%fused_computation | convolution fusion | flops 1362198528 | bytes 5899776 | tf_op jit(solution)/shard_map/dot_general | solution.py:144
  109.6 0.3 copy.91
  110.1 0.3 copy.89
  110.4 0.7 fusion.4
  111.1 0.7 convolution_convert_fusion.5
  111.9 0.6 copy-done.12
  112.5 1.6 fusion.18
  114.2 0.7 copy-done.6
  114.8 0.3 copy.139
  115.1 1.9 reduce.9
  117.0 0.7 reshape.387
  117.7 6.7 %all-to-all-start = ((bf16[8,2,6144]{2,1,0:T(2,128)(2,1)}), bf16[8,2,6144]{2,1,0:T(2,128)(2,1)S(1)}, u32[]{:S(2)}, u32[]{:S(2)}) async-start(bf16[8,2,6144]{2,1,0:T(2,128)(2,1)} %reshape.387), calls=%async_computation | async-start | bytes 393216 | tf_op jit(solution)/shard_map/all_to_all | solution.py:113
  124.5 1.8 fusion.30
  126.3 0.3 reshape_reshape.7
  126.6 0.4 copy.100
  127.1 1.2 copy.117
  128.3 7.1 %all-to-all-done = bf16[8,2,6144]{2,1,0:T(2,128)(2,1)S(1)} async-done(((bf16[8,2,6144]{2,1,0:T(2,128)(2,1)}), bf16[8,2,6144]{2,1,0:T(2,128)(2,1)S(1)}, u32[]{:S(2)}, u32[]{:S(2)}) %all-to-all-start) | async-done | bytes 196640 | tf_op jit(solution)/shard_map/all_to_all | solution.py:113
  135.9 2.6 %convolution_convert_fusion.1 = bf16[8,16,2304]{2,1,0:T(8,128)(2,1)S(1)} fusion(bf16[8,16,768]{2,1,0:T(8,128)(2,1)S(1)} %bitcast.172, bf16[2,768,3072]{2,1,0:T(8,128)(2,1)} %bitcast.177), kind=kOutput, calls=%fused_computation.1 | convolution fusion | flops 453279744 | bytes 4325376 | tf_op jit(solution)/shard_map/dot_general | solution.py:155
  139.0 0.3 fusion.7
  139.3 0.4 fusion.60
  139.9 1.1 fusion.26
  141.0 1.3 multiply_reduce_fusion
  142.3 0.3 fusion.8
  142.6 0.4 fusion.24
  143.0 0.2 fusion.25
  143.2 0.4 copy.108
  143.7 0.3 convert_element_type.167
  144.0 0.4 copy.103
  144.4 0.3 concatenate.26
  144.8 0.4 copy.105
  145.2 0.3 convert_element_type.164
  145.5 3.4 %multiply_reduce_fusion.1 = (f32[8,16]{1,0:T(8,128)S(1)}, f32[8,16,768]{2,1,0:T(8,128)S(1)}) fusion(f32[8,16,768]{2,1,0:T(8,128)S(1)} %bitcast.152, bf16[2,768,3072]{2,1,0:T(8,128)(2,1)} %bitcast.178, bf16[8,16,768]{2,1,0:T(8,128)(2,1)S(1)} %convert_element_type.167, bf16[8,16,768]{2,1,0:T(8,128)(2,1)S(1)} %convert_element_type.164, ...), kind=kOutput, calls=%fused_computation.82 | convolution fusion | flops 454950784 | bytes 4915712 | tf_op jit(solution)/shard_map/dot_general | solution.py:189
  148.9 0.9 add_convert_fusion
  149.7 3.4 %all-to-all-start.3 = ((bf16[8,16,768]{2,1,0:T(8,128)(2,1)}), bf16[8,16,768]{2,1,0:T(8,128)(2,1)S(1)}, u32[]{:S(2)}, u32[]{:S(2)}) async-start(bf16[8,16,768]{2,1,0:T(8,128)(2,1)} %add_convert_fusion), calls=%async_computation.3 | async-start | bytes 393216 | tf_op jit(solution)/shard_map/all_to_all | solution.py:117
  153.1 0.4 copy.98
  153.6 1.0 reshape_reshape.6
  154.6 8.3 %all-to-all-done.3 = bf16[8,16,768]{2,1,0:T(8,128)(2,1)S(1)} async-done(((bf16[8,16,768]{2,1,0:T(8,128)(2,1)}), bf16[8,16,768]{2,1,0:T(8,128)(2,1)S(1)}, u32[]{:S(2)}, u32[]{:S(2)}) %all-to-all-start.3) | async-done | bytes 196640 | tf_op jit(solution)/shard_map/all_to_all | solution.py:117
  162.8 4.0 %all-to-all-start.1 = ((bf16[8,16,768]{2,1,0:T(8,128)(2,1)}), bf16[8,16,768]{2,1,0:T(8,128)(2,1)}, u32[]{:S(2)}, u32[]{:S(2)}) async-start(bf16[8,16,768]{2,1,0:T(8,128)(2,1)} %reshape_reshape.6), calls=%async_computation.1 | async-start | bytes 393216 | tf_op jit(solution)/shard_map/all_to_all | solution.py:117
  166.8 1.8 convolution_convert_fusion.2
  168.9 2.5 %fusion.48 = f32[12,64,384]{2,1,0:T(8,128)S(1)} fusion(bf16[128,12,64]{0,2,1:T(8,128)(2,1)S(1)} %bitcast.165, f32[12,128,384]{2,1,0:T(8,128)} %copy-done.12, f32[12,128]{1,0:T(8,128)S(1)} %get-tuple-element.13, pred[384]{0:T(512)(128)(4,1)S(1)} %broadcast_bitcast_fusion), kind=kOutput, calls=%fused_computation.67 | convolution fusion | flops 77856768 | bytes 3742080 | tf_op jit(solution)/shard_map/gst,sgh->tgh/dot_general | solution.py:102
  171.5 0.9 multiply_convert_fusion
  172.4 0.4 convolution_multiply_fusion
  172.9 0.9 fusion.75
  173.9 4.8 %collective-permute-start.2 = (bf16[128,1536]{0,1:T(8,128)(2,1)}, bf16[128,1536]{0,1:T(8,128)(2,1)}, u32[]{:S(2)}, u32[]{:S(2)}) collective-permute-start(bf16[128,1536]{0,1:T(8,128)(2,1)} %get-tuple-element.6), channel_id=1, source_target_pairs={{0,2},{2,4},{4,6},{6,8},{8,10},{10,12},{12,14},{14,16},{16,18},{18... | collective-permute-start | bytes 1179656 | tf_op jit(solution)/shard_map/ppermute | solution.py:22
  178.6 1.9 collective-permute-start.3
  180.6 2.4 %fusion.27 = bf16[1,128,768]{2,1,0:T(8,128)(2,1)} fusion(bf16[128,768]{1,0:T(8,128)(2,1)} %bitcast.25, bf16[2,768,3072]{2,1,0:T(8,128)(2,1)} %bitcast.180, bf16[128,768]{1,0:T(8,128)(2,1)} %copy-done.6), kind=kOutput, calls=%fused_computation.47 | convolution fusion | flops 151289856 | bytes 1769472 | tf_op jit(solution)/shard_map/dot_general | solution.py:171
  183.0 1.7 fusion.14
  184.7 0.4 collective-permute-done.2
  185.1 6.2 %collective-permute-done.3 = bf16[128,1536]{0,1:T(8,128)(2,1)} collective-permute-done((bf16[128,1536]{0,1:T(8,128)(2,1)}, bf16[128,1536]{0,1:T(8,128)(2,1)}, u32[]{:S(2)}, u32[]{:S(2)}) %collective-permute-start.3) | collective-permute-done | bytes 393248 | tf_op jit(solution)/shard_map/ppermute | solution.py:24
  191.4 1.3 fusion.38
  192.7 3.5 %fusion.52 = (f32[128]{0:T(128)S(1)}, f32[128]{0:T(128)S(1)}, f32[128,768]{1,0:T(8,128)S(1)}) fusion(bf16[1,128,768]{2,1,0:T(8,128)(2,1)S(1)} %copy-done.3, bf16[2,768,3072]{2,1,0:T(8,128)(2,1)} %bitcast.181, bf16[128,1536]{0,1:T(8,128)(2,1)S(1)} %fusion.38, bf16[128,768]{0,1:T(8,128)(2,1)S(1)} %bitcast.173), kind=kOutput, calls=%fused_computation.72 | convolution fusion | flops 454655744 | bytes 4719616 | tf_op jit(solution)/shard_map/dot_general | solution.py:211
  196.2 0.9 fusion.61
  (61 shorter events, 2.6 us)
Async XLA Ops:
  7.2 21.4 %copy-start = (s32[32,4]{0,1:T(4,128)S(1)}, s32[32,4]{0,1:T(4,128)}, u32[]{:S(2)}) copy-start(s32[32,4]{0,1:T(4,128)} %param.13) | copy-start | bytes 1540
  7.2 21.8 %copy-start.2 = (bf16[1,128,768]{2,1,0:T(8,128)(2,1)S(1)}, bf16[1,128,768]{2,1,0:T(8,128)(2,1)}, u32[]{:S(2)}) copy-start(bf16[1,128,768]{2,1,0:T(8,128)(2,1)} %param.7) | copy-start | bytes 589828
  7.2 98.7 %all-gather.3.cloned.1.call-start = ((), (), s32[]{:S(2)}) async-start(), calls=%async_computation.4 | async-start | bytes 9584640 | tf_op jit(solution)/shard_map/all_gather | solution.py:129
  9.1 20.0 %collective-permute-start.1 = (bf16[128,768]{1,0:T(8,128)(2,1)}, bf16[128,768]{1,0:T(8,128)(2,1)S(1)}, u32[]{:S(2)}, u32[]{:S(2)}) collective-permute-start(bf16[128,768]{1,0:T(8,128)(2,1)} %bitcast.147), channel_id=1, source_target_pairs={{2,0},{4,2},{6,4},{8,6},{10,8},{12,10},{14,12},{16,14},{18,16},{20... | collective-permute-start | bytes 589832 | tf_op jit(solution)/shard_map/ppermute | solution.py:24
  11.8 17.2 %collective-permute-start = (bf16[128,768]{1,0:T(8,128)(2,1)}, bf16[128,768]{1,0:T(8,128)(2,1)S(1)}, u32[]{:S(2)}, u32[]{:S(2)}) collective-permute-start(bf16[128,768]{1,0:T(8,128)(2,1)} %bitcast.148), channel_id=1, source_target_pairs={{0,2},{2,4},{4,6},{6,8},{8,10},{10,12},{12,14},{14,16},{16,18},{18... | collective-permute-start | bytes 589832 | tf_op jit(solution)/shard_map/ppermute | solution.py:22
  21.4 17.0 %all-to-all-start.2 = ((bf16[8,2,6144]{2,1,0:T(2,128)(2,1)}), bf16[8,2,6144]{2,1,0:T(2,128)(2,1)S(1)}, u32[]{:S(2)}, u32[]{:S(2)}) async-start(bf16[8,2,6144]{2,1,0:T(2,128)(2,1)} %reshape.389), calls=%async_computation.2 | async-start | bytes 393216 | tf_op jit(solution)/shard_map/all_to_all | solution.py:113
  109.9 1.2 copy-start.1
  110.1 1.8 copy-start.4
  110.4 1.5 copy-start.9
  111.1 1.4 copy-start.12
  114.2 0.7 copy-start.6
  117.7 17.6 %all-to-all-start = ((bf16[8,2,6144]{2,1,0:T(2,128)(2,1)}), bf16[8,2,6144]{2,1,0:T(2,128)(2,1)S(1)}, u32[]{:S(2)}, u32[]{:S(2)}) async-start(bf16[8,2,6144]{2,1,0:T(2,128)(2,1)} %reshape.387), calls=%async_computation | async-start | bytes 393216 | tf_op jit(solution)/shard_map/all_to_all | solution.py:113
  142.3 1.0 copy-start.11
  149.7 13.1 %all-to-all-start.3 = ((bf16[8,16,768]{2,1,0:T(8,128)(2,1)}), bf16[8,16,768]{2,1,0:T(8,128)(2,1)S(1)}, u32[]{:S(2)}, u32[]{:S(2)}) async-start(bf16[8,16,768]{2,1,0:T(8,128)(2,1)} %add_convert_fusion), calls=%async_computation.3 | async-start | bytes 393216 | tf_op jit(solution)/shard_map/all_to_all | solution.py:117
  162.8 6.1 %copy-start.7 = (bf16[8,16,768]{2,1,0:T(8,128)(2,1)}, bf16[8,16,768]{2,1,0:T(8,128)(2,1)S(1)}, u32[]{:S(2)}) copy-start(bf16[8,16,768]{2,1,0:T(8,128)(2,1)S(1)} %all-to-all-done.3) | copy-start | bytes 589828
  162.8 17.8 %all-to-all-start.1 = ((bf16[8,16,768]{2,1,0:T(8,128)(2,1)}), bf16[8,16,768]{2,1,0:T(8,128)(2,1)}, u32[]{:S(2)}, u32[]{:S(2)}) async-start(bf16[8,16,768]{2,1,0:T(8,128)(2,1)} %reshape_reshape.6), calls=%async_computation.1 | async-start | bytes 393216 | tf_op jit(solution)/shard_map/all_to_all | solution.py:117
  168.9 2.5 %copy-start.10 = (bf16[384,768]{0,1:T(8,128)(2,1)S(1)}, bf16[384,768]{0,1:T(8,128)(2,1)}, u32[]{:S(2)}) copy-start(bf16[384,768]{0,1:T(8,128)(2,1)} %copy-done.9) | copy-start | bytes 1769476
  168.9 2.6 %copy-start.13 = (f32[12,128,384]{2,1,0:T(8,128)S(1)}, f32[12,128,384]{2,1,0:T(8,128)}, u32[]{:S(2)}) copy-start(f32[12,128,384]{2,1,0:T(8,128)} %copy-done.12) | copy-start | bytes 7077892
  171.5 1.0 copy-start.5
  173.9 11.2 %collective-permute-start.2 = (bf16[128,1536]{0,1:T(8,128)(2,1)}, bf16[128,1536]{0,1:T(8,128)(2,1)}, u32[]{:S(2)}, u32[]{:S(2)}) collective-permute-start(bf16[128,1536]{0,1:T(8,128)(2,1)} %get-tuple-element.6), channel_id=1, source_target_pairs={{0,2},{2,4},{4,6},{6,8},{8,10},{10,12},{12,14},{14,16},{16,18},{18... | collective-permute-start | bytes 1179656 | tf_op jit(solution)/shard_map/ppermute | solution.py:22
  178.6 12.7 %collective-permute-start.3 = (bf16[128,1536]{0,1:T(8,128)(2,1)}, bf16[128,1536]{0,1:T(8,128)(2,1)}, u32[]{:S(2)}, u32[]{:S(2)}) collective-permute-start(bf16[128,1536]{0,1:T(8,128)(2,1)} %get-tuple-element.7), channel_id=1, source_target_pairs={{2,0},{4,2},{6,4},{8,6},{10,8},{12,10},{14,12},{16,14},{18,16},{20... | collective-permute-start | bytes 1179656 | tf_op jit(solution)/shard_map/ppermute | solution.py:24
  182.9 9.7 %copy-start.3 = (bf16[1,128,768]{2,1,0:T(8,128)(2,1)S(1)}, bf16[1,128,768]{2,1,0:T(8,128)(2,1)}, u32[]{:S(2)}) copy-start(bf16[1,128,768]{2,1,0:T(8,128)(2,1)} %param.7) | copy-start | bytes 589828
  192.7 3.5 %copy-start.8 = (bf16[8,16,768]{2,1,0:T(8,128)(2,1)S(1)}, bf16[8,16,768]{2,1,0:T(8,128)(2,1)}, u32[]{:S(2)}) copy-start(bf16[8,16,768]{2,1,0:T(8,128)(2,1)} %copy-done.7) | copy-start | bytes 589828
Sparse Core Ops, SparseCore 0:
  11.9 93.9 all-gather.2
